TPU v7x, 128 devices: a whole 4x4x4 slice. The times are simulated.
128 devices in a mesh: req: 64 (over z, y, x), col: 2 (over core).
Axes of the slice: x: 4, y: 4, z: 4, core: 2. Of those that a mesh axis runs over, the one named last changes fastest.
Arguments:
- tokens: bfloat16 [32768, 1024], P(('req', 'col')), may hold values from -6 to 6
- norm_gain_pair: float32 [2, 1024], replicated, may hold values from 0.5 to 1.5
- query_key_value_weight: bfloat16 [3, 1024, 1024], P(None, None, 'col'), may hold values from -1 to 1
- head_gate_weight: bfloat16 [2, 1024, 8], P(None, None, 'col'), may hold values from -0.1875 to 0.1875
- decay_logit_bias: float32 [8], P('col'), may hold values from -1 to 1024, as said below
- adapter_down_factor: bfloat16 [64, 1024, 16], P('col'), may hold values from -0.1875 to 0.1875
- adapter_up_factor: bfloat16 [64, 16, 1024], P(None, None, 'col'), may hold values from -1.5 to 1.5
- lengths: int32 [64, 2, 3], P('req'), may hold values from 1 to 128, 256 in all within a row
- request_adapter_index: int32 [64, 6], P('req'), may hold values from 0 to 63
- request_cache_index: int32 [64, 6], P('req'), may hold values from 0 to 511
- caches: bfloat16 [256, 8, 128, 128], P('req', 'col'), may hold values from -6 to 6
- head_output_weight: bfloat16 [1024, 1024], P('col'), may hold values from -0.1875 to 0.1875
- feedforward_weight: bfloat16 [3, 1024, 2816], P(None, None, 'col'), may hold values from -0.1875 to 0.1875
Outputs:
- layer_out: bfloat16 [32768, 1024], P(('req', 'col'))
Inputs may be any that keep to these rules, and one draw needn't show every extreme that they name: The 3 lengths of one device sum to 256, and the longest of them is exactly 128. `request_cache_index`: a value of 256 or more means that the request has no cached memory state. `decay_logit_bias`: at most the logarithm of 512.
All inputs are finite; a program needn't handle non-finite values.
Results may differ from a plain program's by a relative error of at most 0.015.
Values may be sent and summed in bfloat16 or wider, within the bound.
No kernel may reach another device: no remote copies, remote signals or barrier semaphores. Data moves between devices by JAX's collectives and lax.ppermute only.
A program may use at most 192 MiB of HBM per device.

v0:
```python
import math

import jax
import jax.numpy as jnp
import numpy as np
from jax import lax
from jax.experimental import pallas as pl
from jax.experimental.pallas import tpu as pltpu
from jax.sharding import Mesh
from jax.sharding import PartitionSpec as P

epsilon = 1e-05
ROWS = ("z", "y", "x", "col")


def rms_scale(values, gain):
    widened = values.astype(jnp.float32)
    factor = lax.rsqrt(jnp.mean(widened * widened, axis=-1, keepdims=True) + epsilon)
    return (widened * factor * gain).astype(jnp.bfloat16)


def swap(value):
    return lax.ppermute(value, "col", perm=[(0, 1), (1, 0)])


def pair_rows(mine, other, col):
    first = jnp.where(col == 0, mine, other)
    second = jnp.where(col == 0, other, mine)
    return jnp.concatenate([first, second], axis=0)


def pick_states(index, valid, plane, lines):
    slots = index.shape[0]
    per_line = slots // lines
    block = plane.shape[1:]

    def body(index_ref, valid_ref, plane_ref, out_ref, zero_ref, sems):
        zero_ref[...] = jnp.zeros(block, plane.dtype)
        for s in range(slots):
            dst = out_ref.at[s // per_line, s % per_line]

            @pl.when(valid_ref[s] != 0)
            def _():
                pltpu.make_async_copy(plane_ref.at[index_ref[s]], dst, sems.at[s]).start()

            @pl.when(valid_ref[s] == 0)
            def _():
                pltpu.make_async_copy(zero_ref, dst, sems.at[s]).start()

        for s in range(slots):
            dst = out_ref.at[s // per_line, s % per_line]
            pltpu.make_async_copy(zero_ref, dst, sems.at[s]).wait()

    return pl.pallas_call(
        body,
        out_shape=jax.ShapeDtypeStruct((lines, per_line) + block, plane.dtype),
        grid_spec=pltpu.PrefetchScalarGridSpec(
            num_scalar_prefetch=2,
            grid=(),
            in_specs=[pl.BlockSpec(memory_space=pl.ANY)],
            out_specs=pl.BlockSpec(memory_space=pl.ANY),
            scratch_shapes=[pltpu.VMEM(block, plane.dtype), pltpu.SemaphoreType.DMA((slots,))],
        ),
    )(index, valid, plane)


def on_device(
    tokens,
    norm_gain_pair,
    query_key_value_weight,
    head_gate_weight,
    decay_logit_bias,
    adapter_down_factor,
    adapter_up_factor,
    lengths,
    request_adapter_index,
    request_cache_index,
    caches,
    head_output_weight,
    feedforward_weight,
):
    tok_rows, width = tokens.shape
    col = lax.axis_index("col")
    col_count = 2
    group = tok_rows * col_count
    head_cols = query_key_value_weight.shape[2]
    local_heads = head_gate_weight.shape[2]
    head_size = head_cols // local_heads
    group_lengths = lengths[0].reshape(-1)
    scale = 1.0 / math.sqrt(head_size)

    ff_other = swap(feedforward_weight)
    down_other = swap(adapter_down_factor)

    plane = lax.all_gather(caches, ("y", "x"), axis=0, tiled=True)
    per_plane = plane.shape[0]

    normalized_rows = rms_scale(tokens, norm_gain_pair[0])
    gathered = pair_rows(normalized_rows, swap(normalized_rows), col)
    positions = jnp.arange(group, dtype=jnp.int32)
    ends = jnp.cumsum(group_lengths)
    starts = ends - group_lengths
    member = (
        (positions[:, None] >= starts[None, :]) & (positions[:, None] < ends[None, :])
    ).astype(jnp.float32)
    segment = jnp.sum((positions[:, None] >= ends[None, :]).astype(jnp.int32), axis=1)
    projected = jnp.einsum(
        "td,kdc->ktc", gathered, query_key_value_weight, preferred_element_type=jnp.float32
    )
    half_adapters = adapter_down_factor.shape[0]
    mine_numbers = col * half_adapters + jnp.arange(half_adapters, dtype=jnp.int32)
    other_numbers = (1 - col) * half_adapters + jnp.arange(half_adapters, dtype=jnp.int32)
    wanted = request_adapter_index[0][:, None]
    select_mine = (wanted == mine_numbers[None, :]).astype(jnp.bfloat16)
    select_other = (wanted == other_numbers[None, :]).astype(jnp.bfloat16)
    chosen = (
        jnp.einsum("sa,adr->sdr", select_mine, adapter_down_factor, preferred_element_type=jnp.float32)
        + jnp.einsum("sa,adr->sdr", select_other, down_other, preferred_element_type=jnp.float32)
    ).astype(jnp.bfloat16)
    per_request = jnp.einsum("td,sdr->tsr", gathered, chosen, preferred_element_type=jnp.float32)
    low_rank_delta = jnp.sum(member[:, :, None] * per_request, axis=1)
    low_rank_delta = low_rank_delta.astype(jnp.bfloat16)
    adapter_onehot = (
        request_adapter_index[0][:, None]
        == jnp.arange(adapter_up_factor.shape[0], dtype=jnp.int32)[None, :]
    ).astype(jnp.bfloat16)
    up_chosen = jnp.einsum(
        "gq,qjl->gjl", adapter_onehot, adapter_up_factor, preferred_element_type=jnp.float32
    ).astype(jnp.bfloat16)
    masked_low = low_rank_delta[:, None, :] * member.astype(jnp.bfloat16)[:, :, None]
    delta = jnp.einsum("tsr,src->tc", masked_low, up_chosen, preferred_element_type=jnp.float32)
    queries = (projected[0] + delta).astype(jnp.bfloat16).reshape(group, local_heads, head_size)
    plane, queries = lax.optimization_barrier((plane, queries))
    z_count = lax.axis_size("z")
    z_here = lax.axis_index("z")
    own_index = request_cache_index[0]
    shifts = range(1, z_count)

    def along_z(value, d):
        return lax.ppermute(value, "z", perm=[(i, (i + d) % z_count) for i in range(z_count)])

    behind = jnp.stack([own_index] + [along_z(own_index, d) for d in shifts])
    line_rows = jnp.take(behind, (z_here - jnp.arange(z_count, dtype=jnp.int32)) % z_count, axis=0)
    local = line_rows - z_here * per_plane
    valid = ((local >= 0) & (local < per_plane)).astype(jnp.int32)
    slots = pick_states(jnp.clip(local, 0, per_plane - 1).reshape(-1), valid.reshape(-1), plane, z_count)
    states = lax.psum_scatter(slots, "z", scatter_dimension=0, tiled=True)[0]
    keys = projected[1].astype(jnp.bfloat16).reshape(group, local_heads, head_size)
    values = projected[2].astype(jnp.bfloat16).reshape(group, local_heads, head_size)
    gate_terms = jnp.einsum(
        "td,kdh->kth", gathered, head_gate_weight, preferred_element_type=jnp.float32
    )
    log_keep = jax.nn.log_sigmoid(gate_terms[0] + decay_logit_bias[None, :])
    mix_gate = jax.nn.sigmoid(gate_terms[1])
    running = jnp.cumsum(log_keep, axis=0)
    before = running - log_keep
    start_hot = (positions[None, :] == starts[:, None]).astype(jnp.float32)
    start_level = jnp.sum(start_hot[:, :, None] * before[None, :, :], axis=1)
    level = running - jnp.sum(member[:, :, None] * start_level[None, :, :], axis=1)
    masked_queries = queries[:, None, :, :] * member.astype(jnp.bfloat16)[:, :, None, None]
    from_state = jnp.einsum(
        "tshi,shij->thj", masked_queries, states, preferred_element_type=jnp.float32
    )
    carried = from_state * jnp.exp(level)[:, :, None]

    scores = jnp.einsum("qhd,khd->hqk", queries, keys, preferred_element_type=jnp.float32) * scale
    allowed = (segment[:, None] == segment[None, :]) & (positions[None, :] <= positions[:, None])
    masked = jnp.where(allowed[None], scores, -jnp.inf)
    peak = jnp.max(masked, axis=2, keepdims=True)
    weights = jnp.exp(masked - peak)
    probs = (weights / jnp.sum(weights, axis=2, keepdims=True)).astype(jnp.bfloat16)
    attended = jnp.einsum("hqk,khd->qhd", probs, values, preferred_element_type=jnp.float32)
    gap = jnp.where(allowed[None], running.T[:, :, None] - running.T[:, None, :], -jnp.inf)
    memory_w = (scores * jnp.exp(gap)).astype(jnp.bfloat16)
    recalled = jnp.einsum("hqk,khd->qhd", memory_w, values, preferred_element_type=jnp.float32)
    recalled = recalled + carried
    factor = lax.rsqrt(jnp.mean(recalled * recalled, axis=2, keepdims=True) + epsilon)
    combined = attended + mix_gate[:, :, None] * recalled * factor
    head_out = combined.astype(jnp.bfloat16).reshape(group, head_cols)

    partial = jnp.dot(head_out, head_output_weight, preferred_element_type=jnp.float32)
    own = lax.dynamic_slice_in_dim(partial, col * tok_rows, tok_rows, axis=0)
    sent = lax.dynamic_slice_in_dim(partial, (1 - col) * tok_rows, tok_rows, axis=0)
    attn_proj = own + swap(sent)
    mixed = (tokens.astype(jnp.float32) + attn_proj).astype(jnp.bfloat16)
    normed_two = rms_scale(mixed, norm_gain_pair[1])

    def feed_half(weight):
        gate_up = jnp.einsum(
            "td,kdf->ktf", normed_two, weight[:2], preferred_element_type=jnp.float32
        )
        hidden = (jax.nn.silu(gate_up[0]) * gate_up[1]).astype(jnp.bfloat16)
        return jnp.einsum("tf,df->td", hidden, weight[2], preferred_element_type=jnp.float32)

    feed = feed_half(feedforward_weight) + feed_half(ff_other)
    return (mixed.astype(jnp.float32) + feed).astype(jnp.bfloat16)


def solution(mesh):
    n_req = mesh.shape["req"]
    side = round(n_req ** (1.0 / 3.0))
    devices = np.asarray(mesh.devices).reshape(side, side, n_req // (side * side), mesh.shape["col"])
    grid = Mesh(devices, ROWS)
    placed = (
        P(ROWS, None),
        P(),
        P(None, None, "col"),
        P(None, None, "col"),
        P("col"),
        P("col", None, None),
        P(None, None, "col"),
        P(ROWS[:3], None, None),
        P(ROWS[:3], None),
        P(ROWS[:3], None),
        P(ROWS[:3], "col", None, None),
        P("col", None),
        P(None, None, "col"),
    )
    return jax.shard_map(
        on_device, mesh=grid, in_specs=placed, out_specs=P(ROWS, None), check_vma=False
    )
```

profile of v0, /device:TPU:1, one launch (start us, length us, event | category | flops | bytes accessed | tf_op | source)
XLA Modules:
  0.0 189.8 jit_solution(13971139892839321821)
XLA Ops:
  6.5 0.7 all-gather.2.cloned.1.call-update
  7.3 0.0 reduce-scatter.2.cloned.1.call-start
  7.3 4.7 %collective-permute-start.4 = (s32[6]{0:T(128)}, s32[6]{0:T(128)S(1)}, u32[]{:S(2)}, u32[]{:S(2)}) collective-permute-start(s32[6]{0:T(128)} %bitcast.160), channel_id=1, source_target_pairs={{0,96},{32,0},{64,32},{96,64},{1,97},{33,1},{65,33},{97,65},{2,98}... | collective-permute-start | bytes 80 | tf_op jit(solution)/shard_map/ppermute | solution.py:140
  12.0 0.7 collective-permute-start.2
  12.7 1.2 fusion.44
  13.9 0.8 fusion.111
  14.7 2.0 %fusion.46 = bf16[256,1024]{1,0:T(8,128)(2,1)} fusion(bf16[256,1024]{1,0:T(8,128)(2,1)} %param.13, f32[1024]{0:T(1024)S(1)} %bitcast.149, f32[256]{0:T(256)S(1)} %add_rsqrt_fusion.2), kind=kLoop, calls=%fused_computation.57 | loop fusion | flops 1048576 | bytes 1053696 | tf_op jit(solution)/shard_map/convert_element_type | solution.py:19
  16.7 1.5 collective-permute-start
  18.2 2.8 %copy.49 = bf16[32,1024,16]{1,0,2:T(8,128)(2,1)} copy(bf16[32,1024,16]{1,2,0:T(8,128)(2,1)} %param.18) | data formatting | bytes 2097152 | tf_op args[5]
  21.0 0.1 reshape_squeeze.3
  21.1 0.1 reshape.386
  21.2 0.2 reduce-window.14
  21.4 0.1 fusion.71
  21.5 2.5 %convolution_convert_fusion = bf16[6,16,512]{2,0,1:T(8,128)(2,1)S(1)} fusion(bf16[64,16,512]{2,1,0:T(8,128)(2,1)} %param.19, s32[6]{0:T(128)S(1)} %bitcast.153), kind=kOutput, calls=%fused_computation.53 | convolution fusion | flops 6340992 | bytes 1146904 | tf_op jit(solution)/shard_map/gq,qjl->gjl/dot_general | solution.py:127
  24.0 3.3 %fusion.85 = f32[6,1024,16]{1,0,2:T(8,128)} fusion(s32[32]{0:T(128)S(1)} %iota_add_fusion.1, s32[6]{0:T(128)S(1)} %bitcast.154, bf16[32,1024,16]{1,2,0:T(8,128)(2,1)} %param.18), kind=kOutput, calls=%fused_computation.115 | convolution fusion | flops 6291648 | bytes 1441944 | tf_op jit(solution)/shard_map/sa,adr->sdr/dot_general | solution.py:117
  27.3 0.6 gather_fusion
  27.9 0.1 and_convert_fusion
  28.0 0.6 reshape.392.valid_ref
  28.6 0.1 fusion.94
  28.6 0.6 min.12.index_ref
  29.2 1.5 broadcast_select_fusion.1
  30.8 0.0 copy-start.8
  30.8 3.0 %fusion.112 = (bf16[3,512,512]{1,2,0:T(8,128)(2,1)}, f32[3,512,512]{1,2,0:T(8,128)S(1)}) fusion(bf16[3,1024,512]{2,1,0:T(8,128)(2,1)S(1)} %copy-done, bf16[256,1024]{1,0:T(8,128)(2,1)S(1)} %get-tuple-element.14, bf16[256,1024]{1,0:T(8,128)(2,1)S(1)} %get-tuple-element.13), kind=kOutput, calls=%fused_computation.159 | convolution fusion | flops 1613496320 | bytes 8912896 | tf_op jit(solution)/shard_map/td,kdc->ktc/dot_general | solution.py:107
  33.9 1.6 fusion.43
  35.4 0.1 copy.51
  35.6 0.5 fusion.63
  36.0 0.3 fusion.41
  36.4 47.0 %all-gather.2.cloned.1.call-done.plane_ref = bf16[64,4,128,128]{3,2,1,0:T(8,128)(2,1)} async-done(((bf16[4,4,128,128]{3,2,1,0:T(8,128)(2,1)}), bf16[64,4,128,128]{3,2,1,0:T(8,128)(2,1)}) %all-gather.2.cloned.1.call-update) | async-done | bytes 8388624 | tf_op jit(solution)/shard_map/all_gather | solution.py:95
  83.4 17.9 %shard_map.127 = bf16[4,6,4,128,128]{4,3,2,1,0:T(8,128)(2,1)} custom-call(s32[24]{0:T(128)} %min.12.index_ref, s32[24]{0:T(128)} %reshape.392.valid_ref, bf16[64,4,128,128]{3,2,1,0:T(8,128)(2,1)} %all-gather.2.cloned.1.call-done.plane_ref), custom_call_target="tpu_custom_call" | custom-call | tf_op jit(solution)/shard_map/pallas_call | solution.py:54
  101.3 0.0 copy-start.9
  101.3 0.0 copy-start.13
  101.3 0.0 copy-start.11
  101.3 0.0 reduce-scatter.2.cloned.1.call-update
  101.4 0.9 collective-permute-start.6
  102.3 0.1 convert_reduce_fusion
  102.4 0.1 fusion.72
  102.5 0.2 fusion.54
  102.7 0.4 convolution_bitcast_fusion.2
  103.1 0.1 fusion.107
  103.2 1.2 reduce-window.18
  104.4 0.2 slice_reduce_fusion
  104.6 0.2 reduce-window.19
  104.8 0.1 add_bitcast_fusion
  104.8 0.1 bitcast_subtract_fusion.1
  104.9 0.1 multiply_reduce_fusion.3
  105.0 0.1 multiply_reduce_fusion.2
  105.2 0.1 fusion.110
  105.3 0.3 copy.58
  105.5 3.6 %fusion.113 = (f32[4,512]{1,0:T(4,128)S(1)}, f32[4,512,512]{1,2,0:T(8,128)}) fusion(pred[512,512]{0,1:T(8,128)(4,1)S(1)} %fusion.54, bf16[512,4,128]{0,2,1:T(8,128)(2,1)S(1)} %bitcast.140, bf16[512,4,128]{0,2,1:T(8,128)(2,1)S(1)} %bitcast.145), kind=kOutput, calls=%fused_computation.160 | convolution fusion | flops 272630272 | bytes 5513216 | tf_op jit(solution)/shard_map/sub | solution.py:170
  109.1 43.0 %reduce-scatter.2.cloned.1.call-done = bf16[1,6,4,128,128]{4,3,2,1,0:T(8,128)(2,1)} async-done(((bf16[4,6,4,128,128]{4,3,2,1,0:T(8,128)(2,1)}), bf16[1,6,4,128,128]{4,3,2,1,0:T(8,128)(2,1)}) %reduce-scatter.2.cloned.1.call-update) | async-done | bytes 786448 | tf_op jit(solution)/shard_map/reduce_scatter | solution.py:147
  152.1 2.6 %fusion.37 = f32[512,4,128]{0,2,1:T(8,128)S(1)} fusion(bf16[512,6]{0,1:T(8,128)(2,1)S(1)} %get-tuple-element.18, bf16[512,4,128]{2,0,1:T(8,128)(2,1)S(1)} %copy.58, bf16[1,6,4,128,128]{4,3,2,1,0:T(8,128)(2,1)} %reduce-scatter.2.cloned.1.call-done, f32[512,4]{0,1:T(4,128)S(1)} %fusion.80), kind=kOutput, calls=%fused_computation.47 | convolution fusion | flops 404488192 | bytes 2373632 | tf_op jit(solution)/shard_map/tshi,shij->thj/dot_general | solution.py:161
  154.8 2.9 %multiply_reduce_fusion = (f32[512,4]{0,1:T(4,128)S(1)}, f32[512,4,128]{0,2,1:T(8,128)}) fusion(f32[512,4,128]{0,2,1:T(8,128)S(1)} %fusion.37, bf16[512,4,128]{0,2,1:T(8,128)(2,1)S(1)} %bitcast.143, f32[4,512]{1,0:T(4,128)S(1)} %bitcast.152, pred[512,512]{0,1:T(8,128)(4,1)S(1)} %fusion.54, bf16[512,4,128]{0,2,1:T(8,128)(2,1)S(1)} %bitcast.141, ...), kind=kOutput, calls=%fused_computation.67 | convolution fusion | flops 542898176 | bytes 3948544 | tf_op jit(solution)/shard_map/hqk,khd->qhd/dot_general | solution.py:175
  157.7 3.1 %fusion.40 = bf16[512,4,128]{0,2,1:T(8,128)(2,1)S(1)} fusion(bf16[512,4,128]{0,2,1:T(8,128)(2,1)S(1)} %bitcast.144, f32[4,512,512]{1,2,0:T(8,128)} %get-tuple-element.22, f32[4,512]{1,0:T(4,128)S(1)} %get-tuple-element.21, f32[512,4,128]{0,2,1:T(8,128)} %get-tuple-element.24, f32[512,4]{0,1:T(4,128)S(1)} %add_rsqrt_fusion, f32[512,4]{0,1:T(4,128)S(1)} %fusion.79), kind=kOutput, calls=%fused_computation.48 | convolution fusion | flops 271581184 | bytes 6316032 | tf_op jit(solution)/shard_map/hqk,khd->qhd/dot_general | solution.py:172
  160.8 0.0 copy-start.2
  160.8 0.7 fusion.116
  161.6 1.2 constant_dynamic-slice_fusion
  162.7 0.6 collective-permute-start.5
  163.4 2.6 %collective-permute-done.5 = f32[256,1024]{1,0:T(8,128)} collective-permute-done((f32[256,1024]{1,0:T(8,128)}, f32[256,1024]{1,0:T(8,128)}, u32[]{:S(2)}, u32[]{:S(2)}) %collective-permute-start.5) | collective-permute-done | bytes 1048608 | tf_op jit(solution)/shard_map/ppermute | solution.py:23
  166.0 1.5 fusion.48
  167.5 4.4 %fusion.5 = f32[2,256,1408]{2,1,0:T(8,128)S(1)} fusion(bf16[3,1024,1408]{2,1,0:T(8,128)(2,1)} %param.25, bf16[256,1024]{1,0:T(8,128)(2,1)S(1)} %get-tuple-element.10, f32[1024]{0:T(1024)S(1)} %bitcast.156, f32[256]{0:T(256)S(1)} %add_rsqrt_fusion.1), kind=kOutput, calls=%fused_computation.10 | convolution fusion | flops 1477443584 | bytes 9180160 | tf_op jit(solution)/shard_map/td,kdf->ktf/dot_general | solution.py:189
  171.9 2.9 %fusion.15 = f32[256,1024]{1,0:T(8,128)S(1)} fusion(bf16[3,1024,1408]{2,1,0:T(8,128)(2,1)} %param.25, f32[2,256,1408]{2,1,0:T(8,128)S(1)} %fusion.5), kind=kOutput, calls=%fused_computation.17 | convolution fusion | flops 740360192 | bytes 6815744 | tf_op jit(solution)/shard_map/tf,df->td/dot_general | solution.py:193
  174.8 4.4 %fusion.8 = f32[2,256,1408]{2,1,0:T(8,128)S(1)} fusion(bf16[3,1024,1408]{2,1,0:T(8,128)(2,1)} %collective-permute-done.6, bf16[256,1024]{1,0:T(8,128)(2,1)S(1)} %get-tuple-element.10, f32[1024]{0:T(1024)S(1)} %bitcast.157, f32[256]{0:T(256)S(1)} %add_rsqrt_fusion.1), kind=kOutput, calls=%fused_computation.11 | convolution fusion | flops 1477443584 | bytes 9180160 | tf_op jit(solution)/shard_map/td,kdf->ktf/dot_general | solution.py:189
  179.1 0.0 copy-start.1
  179.1 3.8 %fusion.42 = bf16[256,1024]{1,0:T(8,128)(2,1)} fusion(f32[256,1024]{1,0:T(8,128)S(1)} %fusion.15, bf16[3,1024,1408]{2,1,0:T(8,128)(2,1)} %collective-permute-done.6, bf16[256,1024]{1,0:T(8,128)(2,1)S(1)} %get-tuple-element.10, f32[2,256,1408]{2,1,0:T(8,128)S(1)} %fusion.8), kind=kOutput, calls=%fused_computation.50 | convolution fusion | flops 741408768 | bytes 7864320 | tf_op jit(solution)/shard_map/tf,df->td/dot_general | solution.py:193
  (48 shorter events, 0.2 us)
Async XLA Ops:
  6.5 24.2 %copy-start = (bf16[3,1024,512]{2,1,0:T(8,128)(2,1)S(1)}, bf16[3,1024,512]{2,1,0:T(8,128)(2,1)}, u32[]{:S(2)}) copy-start(bf16[3,1024,512]{2,1,0:T(8,128)(2,1)} %param.15) | copy-start | bytes 9437188
  6.5 14.5 %copy-start.14 = (s32[1,2,3]{2,1,0:T(2,128)S(1)}, s32[1,2,3]{2,1,0:T(2,128)}, u32[]{:S(2)}) copy-start(s32[1,2,3]{2,1,0:T(2,128)} %param.20) | copy-start | bytes 76
  6.5 15.0 %copy-start.10 = (s32[1,6]{1,0:T(1,128)S(1)}, s32[1,6]{1,0:T(1,128)}, u32[]{:S(2)}) copy-start(s32[1,6]{1,0:T(1,128)} %param.21) | copy-start | bytes 76
  6.5 76.8 %all-gather.2.cloned.1.call-start = ((), (), s32[]{:S(2)}) async-start(), calls=%async_computation.1 | async-start | bytes 8912896 | tf_op jit(solution)/shard_map/all_gather | solution.py:95
  7.3 144.9 %reduce-scatter.2.cloned.1.call-start = ((), (), s32[]{:S(2)}) async-start(), calls=%async_computation.2 | async-start | bytes 3932160 | tf_op jit(solution)/shard_map/reduce_scatter | solution.py:147
  7.3 20.0 %copy-start.12 = (s32[1,6]{1,0:T(1,128)S(1)}, s32[1,6]{1,0:T(1,128)}, u32[]{:S(2)}) copy-start(s32[1,6]{1,0:T(1,128)} %param.22) | copy-start | bytes 76
  7.3 20.0 %collective-permute-start.4 = (s32[6]{0:T(128)}, s32[6]{0:T(128)S(1)}, u32[]{:S(2)}, u32[]{:S(2)}) collective-permute-start(s32[6]{0:T(128)} %bitcast.160), channel_id=1, source_target_pairs={{0,96},{32,0},{64,32},{96,64},{1,97},{33,1},{65,33},{97,65},{2,98}... | collective-permute-start | bytes 80 | tf_op jit(solution)/shard_map/ppermute | solution.py:140
  12.0 15.3 %collective-permute-start.3 = (s32[6]{0:T(128)}, s32[6]{0:T(128)S(1)}, u32[]{:S(2)}, u32[]{:S(2)}) collective-permute-start(s32[6]{0:T(128)} %bitcast.161), channel_id=1, source_target_pairs={{0,64},{32,96},{64,0},{96,32},{1,65},{33,97},{65,1},{97,33},{2,66}... | collective-permute-start | bytes 80 | tf_op jit(solution)/shard_map/ppermute | solution.py:140
  12.0 15.3 %collective-permute-start.2 = (s32[6]{0:T(128)}, s32[6]{0:T(128)S(1)}, u32[]{:S(2)}, u32[]{:S(2)}) collective-permute-start(s32[6]{0:T(128)} %bitcast.162), channel_id=1, source_target_pairs={{0,32},{32,64},{64,96},{96,0},{1,33},{33,65},{65,97},{97,1},{2,34}... | collective-permute-start | bytes 80 | tf_op jit(solution)/shard_map/ppermute | solution.py:140
  16.7 12.5 %collective-permute-start = (bf16[256,1024]{1,0:T(8,128)(2,1)}, bf16[256,1024]{1,0:T(8,128)(2,1)}, u32[]{:S(2)}, u32[]{:S(2)}) collective-permute-start(bf16[256,1024]{1,0:T(8,128)(2,1)} %fusion.46), channel_id=1, source_target_pairs={{0,1},{1,0},{2,3},{3,2},{4,5},{5,4},{6,7},{7,6},{8,9},{9,8},{10,11... | collective-permute-start | bytes 1572872 | tf_op jit(solution)/shard_map/ppermute | solution.py:23
  21.0 12.8 %collective-permute-start.1 = (bf16[32,1024,16]{1,0,2:T(8,128)(2,1)}, bf16[32,1024,16]{1,0,2:T(8,128)(2,1)}, u32[]{:S(2)}, u32[]{:S(2)}) collective-permute-start(bf16[32,1024,16]{1,0,2:T(8,128)(2,1)} %copy.49), channel_id=1, source_target_pairs={{0,1},{1,0},{2,3},{3,2},{4,5},{5,4},{6,7},{7,6},{8,9},{9,8},{10,11... | collective-permute-start | bytes 3145736 | tf_op jit(solution)/shard_map/ppermute | solution.py:23
  30.8 4.8 %copy-start.6 = (bf16[256,1024]{1,0:T(8,128)(2,1)}, bf16[256,1024]{1,0:T(8,128)(2,1)S(1)}, u32[]{:S(2)}) copy-start(bf16[256,1024]{1,0:T(8,128)(2,1)S(1)} %get-tuple-element.13) | copy-start | bytes 1572868
  30.8 4.8 %copy-start.8 = (bf16[256,1024]{1,0:T(8,128)(2,1)}, bf16[256,1024]{1,0:T(8,128)(2,1)S(1)}, u32[]{:S(2)}) copy-start(bf16[256,1024]{1,0:T(8,128)(2,1)S(1)} %get-tuple-element.14) | copy-start | bytes 1572868
  30.8 3.1 %copy-start.3 = (f32[6,1024,16]{1,0,2:T(8,128)S(1)}, f32[6,1024,16]{1,0,2:T(8,128)}, u32[]{:S(2)}) copy-start(f32[6,1024,16]{1,0,2:T(8,128)} %fusion.85) | copy-start | bytes 1179652
  101.3 1.4 copy-start.7
  101.3 1.4 copy-start.9
  101.3 1.4 copy-start.13
  101.3 1.8 copy-start.11
  101.3 3.8 %copy-start.5 = (bf16[3,512,512]{1,2,0:T(8,128)(2,1)S(1)}, bf16[3,512,512]{1,2,0:T(8,128)(2,1)}, u32[]{:S(2)}) copy-start(bf16[3,512,512]{1,2,0:T(8,128)(2,1)} %get-tuple-element.19) | copy-start | bytes 4718596
  101.4 73.4 %collective-permute-start.6 = (bf16[3,1024,1408]{2,1,0:T(8,128)(2,1)}, bf16[3,1024,1408]{2,1,0:T(8,128)(2,1)}, u32[]{:S(2)}, u32[]{:S(2)}) collective-permute-start(bf16[3,1024,1408]{2,1,0:T(8,128)(2,1)} %param.25), channel_id=1, source_target_pairs={{0,1},{1,0},{2,3},{3,2},{4,5},{5,4},{6,7},{7,6},{8,9},{9,8},{10,11... | collective-permute-start | bytes 25952264 | tf_op jit(solution)/shard_map/ppermute | solution.py:23
  157.7 3.1 %copy-start.4 = (bf16[512,1024]{1,0:T(8,128)(2,1)S(1)}, bf16[512,1024]{1,0:T(8,128)(2,1)}, u32[]{:S(2)}) copy-start(bf16[512,1024]{1,0:T(8,128)(2,1)} %param.24) | copy-start | bytes 3145732
  160.8 5.2 %copy-start.2 = (bf16[256,1024]{1,0:T(8,128)(2,1)S(1)}, bf16[256,1024]{1,0:T(8,128)(2,1)}, u32[]{:S(2)}) copy-start(bf16[256,1024]{1,0:T(8,128)(2,1)} %param.13) | copy-start | bytes 1572868
  162.7 3.2 %collective-permute-start.5 = (f32[256,1024]{1,0:T(8,128)}, f32[256,1024]{1,0:T(8,128)}, u32[]{:S(2)}, u32[]{:S(2)}) collective-permute-start(f32[256,1024]{1,0:T(8,128)} %constant_dynamic-slice_fusion), channel_id=1, source_target_pairs={{0,1},{1,0},{2,3},{3,2},{4,5},{5,4},{6,7},{7,6},{8,9},{9,8},{10,11... | collective-permute-start | bytes 3145736 | tf_op jit(solution)/shard_map/ppermute | solution.py:23
  179.1 3.9 %copy-start.1 = (bf16[3,1024,512]{2,1,0:T(8,128)(2,1)S(1)}, bf16[3,1024,512]{2,1,0:T(8,128)(2,1)}, u32[]{:S(2)}) copy-start(bf16[3,1024,512]{2,1,0:T(8,128)(2,1)} %param.15) | copy-start | bytes 9437188
Sparse Core Ops, SparseCore 0:
  9.5 73.8 all-gather.1
  101.5 50.5 reduce-scatter.1
where the time goes:
time: 189 us; the launch traced here: 190 us
  waiting for transfers between devices  93.3 us (49%)
  matrix products  40 us (21%)
  Pallas kernels  17.9 us (9%)
  between operations  13.8 us (7%)
  other arithmetic  9.03 us (5%)
  starting transfers between devices  8.46 us (4%)
  local copies, waits for them, and re-layouts  7.35 us (4%)
    all_gather x1, waiting for transfers between devices, on_device(): plane = lax.all_gather(caches, ('y', 'x'), axis=0, tiled=True)  47 us
    reduce_scatter x1, waiting for transfers between devices, on_device(): states = lax.psum_scatter(slots, 'z', scatter_dimension=0, tiled=True)[0]  43 us
    pallas_call x1, Pallas kernels, pick_states(): pl.pallas_call(body, out_shape=jax.ShapeDtypeStruct((lines, per_line) + b...  17.9 us
    dot_general x2, matrix products, feed_half(): jnp.einsum('td,kdf->ktf', normed_two, weight[:2], preferred_element_type=...  8.74 us
    dot_general x2, matrix products, feed_half(): jnp.einsum('tf,df->td', hidden, weight[2], preferred_element_type=jnp.flo...  6.71 us
    ppermute x3, starting transfers between devices, along_z(): lax.ppermute(value, 'z', perm=[(i, (i + d) % z_count) for i in range(z_co...  5.36 us
  transfers between devices with their start and end apart: 9, of which 3 were waited for; matrix products, arithmetic and copies ran while one was open for 25% of the time, Pallas kernels for 0%

commit v1 on v0

--- a/solution.py
+++ b/solution.py
@@ -89,7 +89,6 @@
     group_lengths = lengths[0].reshape(-1)
     scale = 1.0 / math.sqrt(head_size)
 
-    ff_other = swap(feedforward_weight)
     down_other = swap(adapter_down_factor)
 
     plane = lax.all_gather(caches, ("y", "x"), axis=0, tiled=True)
@@ -185,14 +184,17 @@
     mixed = (tokens.astype(jnp.float32) + attn_proj).astype(jnp.bfloat16)
     normed_two = rms_scale(mixed, norm_gain_pair[1])
 
-    def feed_half(weight):
-        gate_up = jnp.einsum(
-            "td,kdf->ktf", normed_two, weight[:2], preferred_element_type=jnp.float32
-        )
-        hidden = (jax.nn.silu(gate_up[0]) * gate_up[1]).astype(jnp.bfloat16)
-        return jnp.einsum("tf,df->td", hidden, weight[2], preferred_element_type=jnp.float32)
-
-    feed = feed_half(feedforward_weight) + feed_half(ff_other)
+    rows_two = pair_rows(normed_two, swap(normed_two), col)
+    gate_up = jnp.einsum(
+        "td,kdf->ktf", rows_two, feedforward_weight[:2], preferred_element_type=jnp.float32
+    )
+    hidden = (jax.nn.silu(gate_up[0]) * gate_up[1]).astype(jnp.bfloat16)
+    feed_part = jnp.einsum(
+        "tf,df->td", hidden, feedforward_weight[2], preferred_element_type=jnp.float32
+    )
+    feed_own = lax.dynamic_slice_in_dim(feed_part, col * tok_rows, tok_rows, axis=0)
+    feed_sent = lax.dynamic_slice_in_dim(feed_part, (1 - col) * tok_rows, tok_rows, axis=0)
+    feed = feed_own + swap(feed_sent)
     return (mixed.astype(jnp.float32) + feed).astype(jnp.bfloat16)
 
 

time: 189 us -> 192 us (1.016)
  waiting for transfers between devices: 93.3 us -> 83.4 us
  local copies, waits for them, and re-layouts: 7.35 us -> 13 us
  Pallas kernels: 17.9 us -> 21.9 us
  other arithmetic: 9.03 us -> 11.2 us
    reduce_scatter x1, waiting for transfers between devices: 43 us -> 31.4 us  [on_device(): states = lax.psum_scatter(slots, 'z', scatter_dimension=0, tiled=True)[0]]
    dot_general x4 -> x2, matrix products: 15.4 us -> 9.47 us  [the longest x1 5.79 us: on_device(): jnp.einsum('td,kdf->ktf', rows_two, feedforward_weight[:2], preferred_ele...]
    pallas_call x1, Pallas kernels: 17.9 us -> 21.9 us  [pick_states(): pl.pallas_call(body, out_shape=jax.ShapeDtypeStruct((lines, per_line) + b...]
    ppermute x4 -> x5, waiting for transfers between devices: 2.64 us -> 6.46 us  [swap(): return lax.ppermute(value, 'col', perm=[(0, 1), (1, 0)])]
    slice x1, local copies, waits for them, and re-layouts: 0.07 us -> 2.25 us  [on_device(): projected[1].astype(jnp.bfloat16).reshape(group, local_heads, head_size)]
    all_gather x1, waiting for transfers between devices: 47 us -> 44.8 us  [on_device(): plane = lax.all_gather(caches, ('y', 'x'), axis=0, tiled=True)]
    unnamed x32 -> x24, local copies, waits for them, and re-layouts: 2.85 us -> 4.48 us
  transfers between devices with their start and end apart: 9 -> 10, of which waited for: 3 -> 5; matrix products, arithmetic and copies ran while one was open for 25% -> 19% of each run, Pallas kernels for 0% -> 0%
where the time goes in v1:
time: 192 us; the launch traced here: 193 us
  waiting for transfers between devices  83.4 us (43%)
  matrix products  40.1 us (21%)
  Pallas kernels  21.9 us (11%)
  between operations  13.7 us (7%)
  local copies, waits for them, and re-layouts  13 us (7%)
  other arithmetic  11.2 us (6%)
  starting transfers between devices  9.65 us (5%)
    all_gather x1, waiting for transfers between devices, on_device(): plane = lax.all_gather(caches, ('y', 'x'), axis=0, tiled=True)  44.8 us
    reduce_scatter x1, waiting for transfers between devices, on_device(): states = lax.psum_scatter(slots, 'z', scatter_dimension=0, tiled=True)[0]  31.4 us
    pallas_call x1, Pallas kernels, pick_states(): pl.pallas_call(body, out_shape=jax.ShapeDtypeStruct((lines, per_line) + b...  21.9 us
    ppermute x3, starting transfers between devices, along_z(): lax.ppermute(value, 'z', perm=[(i, (i + d) % z_count) for i in range(z_co...  6.57 us
    ppermute x5, waiting for transfers between devices, swap(): return lax.ppermute(value, 'col', perm=[(0, 1), (1, 0)])  6.46 us
    dot_general x1, matrix products, on_device(): jnp.einsum('td,kdf->ktf', rows_two, feedforward_weight[:2], preferred_ele...  5.79 us
    sub x1, matrix products, on_device(): weights = jnp.exp(masked - peak)  4.77 us
    dot_general x1, matrix products, on_device(): jnp.einsum('hqk,khd->qhd', memory_w, values, preferred_element_type=jnp.f...  4.51 us
  transfers between devices with their start and end apart: 10, of which 5 were waited for; matrix products, arithmetic and copies ran while one was open for 19% of the time, Pallas kernels for 0%

profile of v1, /device:TPU:1, one launch (start us, length us, event | category | flops | bytes accessed | tf_op | source)
XLA Modules:
  0.0 192.9 jit_solution(14306725844883789178)
XLA Ops:
  6.5 0.7 all-gather.2.cloned.1.call-update
  7.3 2.5 %collective-permute-start.2 = (s32[6]{0:T(128)}, s32[6]{0:T(128)S(1)}, u32[]{:S(2)}, u32[]{:S(2)}) collective-permute-start(s32[6]{0:T(128)} %bitcast.145), channel_id=1, source_target_pairs={{0,32},{32,64},{64,96},{96,0},{1,33},{33,65},{65,97},{97,1},{2,34}... | collective-permute-start | bytes 80 | tf_op jit(solution)/shard_map/ppermute | solution.py:139
  9.9 3.3 %collective-permute-start.3 = (s32[6]{0:T(128)}, s32[6]{0:T(128)S(1)}, u32[]{:S(2)}, u32[]{:S(2)}) collective-permute-start(s32[6]{0:T(128)} %bitcast.146), channel_id=1, source_target_pairs={{0,64},{32,96},{64,0},{96,32},{1,65},{33,97},{65,1},{97,33},{2,66}... | collective-permute-start | bytes 80 | tf_op jit(solution)/shard_map/ppermute | solution.py:139
  13.2 0.7 collective-permute-start.4
  13.9 1.2 fusion.37
  15.1 0.8 fusion.100
  15.9 2.0 %fusion.39 = bf16[256,1024]{1,0:T(8,128)(2,1)} fusion(bf16[256,1024]{1,0:T(8,128)(2,1)} %param.13, f32[1024]{0:T(1024)S(1)} %bitcast.136, f32[256]{0:T(256)S(1)} %add_rsqrt_fusion.2), kind=kLoop, calls=%fused_computation.49 | loop fusion | flops 1048576 | bytes 1053696 | tf_op jit(solution)/shard_map/convert_element_type | solution.py:19
  17.9 1.5 collective-permute-start
  19.5 2.8 %copy.49 = bf16[32,1024,16]{1,0,2:T(8,128)(2,1)} copy(bf16[32,1024,16]{1,2,0:T(8,128)(2,1)} %param.18) | data formatting | bytes 2097152 | tf_op args[5]
  22.2 0.1 reshape.385
  22.3 0.1 reshape_squeeze.3
  22.4 0.2 reduce-window.14
  22.7 0.1 fusion.60
  22.7 2.5 %convolution_convert_fusion = bf16[6,16,512]{2,0,1:T(8,128)(2,1)S(1)} fusion(bf16[64,16,512]{2,1,0:T(8,128)(2,1)} %param.19, s32[6]{0:T(128)S(1)} %bitcast.140), kind=kOutput, calls=%fused_computation.45 | convolution fusion | flops 6340992 | bytes 1146904 | tf_op jit(solution)/shard_map/gq,qjl->gjl/dot_general | solution.py:126
  25.2 3.3 %fusion.74 = f32[6,1024,16]{1,0,2:T(8,128)} fusion(s32[32]{0:T(128)S(1)} %iota_add_fusion.1, s32[6]{0:T(128)S(1)} %bitcast.141, bf16[32,1024,16]{1,2,0:T(8,128)(2,1)} %param.18), kind=kOutput, calls=%fused_computation.110 | convolution fusion | flops 6291648 | bytes 1441944 | tf_op jit(solution)/shard_map/sa,adr->sdr/dot_general | solution.py:116
  28.5 0.6 gather_fusion
  29.1 0.1 fusion.83
  29.2 0.6 min.12.index_ref
  29.8 0.1 and_convert_fusion
  29.9 0.7 reshape.391.valid_ref
  30.5 1.5 broadcast_select_fusion.3
  32.1 3.0 %fusion.101 = (bf16[3,512,512]{1,2,0:T(8,128)(2,1)}, f32[3,512,512]{1,2,0:T(8,128)S(1)}) fusion(bf16[3,1024,512]{2,1,0:T(8,128)(2,1)S(1)} %copy-done, bf16[256,1024]{1,0:T(8,128)(2,1)S(1)} %get-tuple-element.16, bf16[256,1024]{1,0:T(8,128)(2,1)S(1)} %get-tuple-element.15), kind=kOutput, calls=%fused_computation.155 | convolution fusion | flops 1613496320 | bytes 8912896 | tf_op jit(solution)/shard_map/td,kdc->ktc/dot_general | solution.py:106
  35.2 1.5 fusion.36
  36.7 0.1 copy.51
  36.9 0.5 fusion.54
  37.4 1.2 fusion.35
  38.6 44.8 %all-gather.2.cloned.1.call-done.plane_ref = bf16[64,4,128,128]{3,2,1,0:T(8,128)(2,1)} async-done(((bf16[4,4,128,128]{3,2,1,0:T(8,128)(2,1)}), bf16[64,4,128,128]{3,2,1,0:T(8,128)(2,1)}) %all-gather.2.cloned.1.call-update) | async-done | bytes 8388624 | tf_op jit(solution)/shard_map/all_gather | solution.py:94
  83.4 21.9 %shard_map.127 = bf16[4,6,4,128,128]{4,3,2,1,0:T(8,128)(2,1)} custom-call(s32[24]{0:T(128)} %min.12.index_ref, s32[24]{0:T(128)} %reshape.391.valid_ref, bf16[64,4,128,128]{3,2,1,0:T(8,128)(2,1)} %all-gather.2.cloned.1.call-done.plane_ref), custom_call_target="tpu_custom_call" | custom-call | tf_op jit(solution)/shard_map/pallas_call | solution.py:54
  105.3 0.1 convert_reduce_fusion
  105.4 0.1 fusion.61
  105.5 0.2 fusion.50
  105.7 0.3 copy-done.9
  106.0 1.6 convolution_bitcast_fusion.2
  107.5 0.1 fusion.96
  107.7 1.4 reduce-window.18
  109.1 0.2 slice_reduce_fusion
  109.2 0.2 reduce-window.19
  109.4 0.1 add_bitcast_fusion
  109.5 0.1 bitcast_subtract_fusion.1
  109.6 0.1 multiply_reduce_fusion.3
  109.7 0.1 multiply_reduce_fusion.2
  109.8 2.2 %fusion.99 = (bf16[1,512,512]{1,2,0:T(8,128)(2,1)}, bf16[1,512,512]{1,2,0:T(8,128)(2,1)}) fusion(bf16[3,512,512]{1,2,0:T(8,128)(2,1)} %get-tuple-element.21), kind=kLoop, calls=%fused_computation.153 | loop fusion | bytes 2097152 | tf_op jit(solution)/shard_map/slice | solution.py:147
  112.1 2.0 %copy.58 = bf16[512,4,128]{2,0,1:T(8,128)(2,1)} copy(bf16[512,4,128]{0,2,1:T(8,128)(2,1)} %bitcast.124) | data formatting | bytes 1048576 | tf_op jit(solution)/shard_map/optimization_barrier | solution.py:132
  114.1 4.8 %fusion.102 = (f32[4,512]{1,0:T(4,128)S(1)}, f32[4,512,512]{1,2,0:T(8,128)}) fusion(pred[512,512]{0,1:T(8,128)(4,1)S(1)} %fusion.50, bf16[512,4,128]{0,2,1:T(8,128)(2,1)} %bitcast.125, bf16[512,4,128]{0,2,1:T(8,128)(2,1)} %bitcast.130), kind=kOutput, calls=%fused_computation.156 | convolution fusion | flops 272630272 | bytes 5513216 | tf_op jit(solution)/shard_map/sub | solution.py:169
  118.9 31.4 %reduce-scatter.2.cloned.1.call-done = bf16[1,6,4,128,128]{4,3,2,1,0:T(8,128)(2,1)} async-done(((bf16[4,6,4,128,128]{4,3,2,1,0:T(8,128)(2,1)}), bf16[1,6,4,128,128]{4,3,2,1,0:T(8,128)(2,1)}) %reduce-scatter.2.cloned.1.call-update) | async-done | bytes 786448 | tf_op jit(solution)/shard_map/reduce_scatter | solution.py:146
  150.3 3.8 %fusion.31 = f32[512,4,128]{0,2,1:T(8,128)} fusion(bf16[512,6]{0,1:T(8,128)(2,1)S(1)} %get-tuple-element.20, bf16[512,4,128]{2,0,1:T(8,128)(2,1)} %copy.58, bf16[1,6,4,128,128]{4,3,2,1,0:T(8,128)(2,1)} %reduce-scatter.2.cloned.1.call-done, f32[512,4]{0,1:T(4,128)S(1)} %fusion.69), kind=kOutput, calls=%fused_computation.40 | convolution fusion | flops 404488192 | bytes 2373632 | tf_op jit(solution)/shard_map/tshi,shij->thj/dot_general | solution.py:160
  154.0 4.5 %multiply_reduce_fusion = (f32[512,4]{0,1:T(4,128)S(1)}, f32[512,4,128]{0,2,1:T(8,128)}) fusion(f32[512,4,128]{0,2,1:T(8,128)} %fusion.31, bf16[512,4,128]{0,2,1:T(8,128)(2,1)} %bitcast.128, f32[4,512]{1,0:T(4,128)S(1)} %bitcast.139, pred[512,512]{0,1:T(8,128)(4,1)S(1)} %fusion.50, bf16[512,4,128]{0,2,1:T(8,128)(2,1)} %bitcast.126, ...), kind=kOutput, calls=%fused_computation.63 | convolution fusion | flops 542898176 | bytes 3948544 | tf_op jit(solution)/shard_map/hqk,khd->qhd/dot_general | solution.py:174
  158.6 3.3 %fusion.34 = bf16[512,4,128]{0,2,1:T(8,128)(2,1)S(1)} fusion(bf16[512,4,128]{0,2,1:T(8,128)(2,1)} %bitcast.129, f32[4,512,512]{1,2,0:T(8,128)} %get-tuple-element.24, f32[4,512]{1,0:T(4,128)S(1)} %get-tuple-element.23, f32[512,4,128]{0,2,1:T(8,128)} %get-tuple-element.26, f32[512,4]{0,1:T(4,128)S(1)} %add_rsqrt_fusion, f32[512,4]{0,1:T(4,128)S(1)} %fusion.68), kind=kOutput, calls=%fused_computation.41 | convolution fusion | flops 271581184 | bytes 6316032 | tf_op jit(solution)/shard_map/hqk,khd->qhd/dot_general | solution.py:171
  161.8 0.7 fusion.105
  162.6 1.3 copy-done.1
  163.9 1.1 constant_dynamic-slice_fusion.1
  165.0 0.6 collective-permute-start.5
  165.6 2.6 %collective-permute-done.5 = f32[256,1024]{1,0:T(8,128)} collective-permute-done((f32[256,1024]{1,0:T(8,128)}, f32[256,1024]{1,0:T(8,128)}, u32[]{:S(2)}, u32[]{:S(2)}) %collective-permute-start.5) | collective-permute-done | bytes 1048608 | tf_op jit(solution)/shard_map/ppermute | solution.py:23
  168.3 1.9 %fusion.41 = (f32[256]{0:T(256)S(1)}, bf16[256,1024]{1,0:T(8,128)(2,1)S(1)}) fusion(f32[256,1024]{1,0:T(8,128)} %collective-permute-done.5, f32[512,1024]{1,0:T(8,128)} %copy-done.1, s32[]{:T(128)S(6)} %select_n.92, bf16[256,1024]{1,0:T(8,128)(2,1)} %param.13), kind=kLoop, calls=%fused_computation.51 | loop fusion | flops 1834752 | bytes 3146756 | tf_op jit(solution)/shard_map/reduce_sum | solution.py:18
  170.2 0.2 fusion.43
  170.4 0.5 collective-permute-start.6
  170.9 1.5 collective-permute-done.6
  172.4 0.3 broadcast_select_fusion.1
  172.7 5.8 %fusion.3 = f32[2,512,1408]{2,1,0:T(8,128)S(1)} fusion(bf16[3,1024,1408]{2,1,0:T(8,128)(2,1)} %param.25, bf16[256,1024]{1,0:T(8,128)(2,1)S(1)} %get-tuple-element.14, bf16[256,1024]{1,0:T(8,128)(2,1)S(1)} %get-tuple-element.13), kind=kOutput, calls=%fused_computation.4 | convolution fusion | flops 2954887168 | bytes 12582912 | tf_op jit(solution)/shard_map/td,kdf->ktf/dot_general | solution.py:188
  178.5 3.7 %fusion.10 = f32[512,1024]{1,0:T(8,128)S(1)} fusion(bf16[3,1024,1408]{2,1,0:T(8,128)(2,1)} %param.25, f32[2,512,1408]{2,1,0:T(8,128)S(1)} %fusion.3), kind=kOutput, calls=%fused_computation.14 | convolution fusion | flops 1480720384 | bytes 10747904 | tf_op jit(solution)/shard_map/tf,df->td/dot_general | solution.py:192
  182.2 0.1 constant_dynamic-slice_fusion
  182.3 0.5 collective-permute-start.7
  182.7 2.3 %collective-permute-done.7 = f32[256,1024]{1,0:T(8,128)S(1)} collective-permute-done((f32[256,1024]{1,0:T(8,128)S(1)}, f32[256,1024]{1,0:T(8,128)S(1)}, u32[]{:S(2)}, u32[]{:S(2)}) %collective-permute-start.7) | collective-permute-done | bytes 1048608 | tf_op jit(solution)/shard_map/ppermute | solution.py:23
  185.0 1.1 fusion.44
  (44 shorter events, 0.3 us)
Async XLA Ops:
  6.5 25.6 %copy-start = (bf16[3,1024,512]{2,1,0:T(8,128)(2,1)S(1)}, bf16[3,1024,512]{2,1,0:T(8,128)(2,1)}, u32[]{:S(2)}) copy-start(bf16[3,1024,512]{2,1,0:T(8,128)(2,1)} %param.15) | copy-start | bytes 9437188
  6.5 15.7 %copy-start.10 = (s32[1,2,3]{2,1,0:T(2,128)S(1)}, s32[1,2,3]{2,1,0:T(2,128)}, u32[]{:S(2)}) copy-start(s32[1,2,3]{2,1,0:T(2,128)} %param.20) | copy-start | bytes 76
  6.5 16.2 %copy-start.6 = (s32[1,6]{1,0:T(1,128)S(1)}, s32[1,6]{1,0:T(1,128)}, u32[]{:S(2)}) copy-start(s32[1,6]{1,0:T(1,128)} %param.21) | copy-start | bytes 76
  6.5 76.8 %all-gather.2.cloned.1.call-start = ((), (), s32[]{:S(2)}) async-start(), calls=%async_computation.1 | async-start | bytes 8912896 | tf_op jit(solution)/shard_map/all_gather | solution.py:94
  7.3 143.0 %reduce-scatter.2.cloned.1.call-start = ((), (), s32[]{:S(2)}) async-start(), calls=%async_computation.2 | async-start | bytes 3932160 | tf_op jit(solution)/shard_map/reduce_scatter | solution.py:146
  7.3 21.2 %copy-start.8 = (s32[1,6]{1,0:T(1,128)S(1)}, s32[1,6]{1,0:T(1,128)}, u32[]{:S(2)}) copy-start(s32[1,6]{1,0:T(1,128)} %param.22) | copy-start | bytes 76
  7.3 21.2 %collective-permute-start.2 = (s32[6]{0:T(128)}, s32[6]{0:T(128)S(1)}, u32[]{:S(2)}, u32[]{:S(2)}) collective-permute-start(s32[6]{0:T(128)} %bitcast.145), channel_id=1, source_target_pairs={{0,32},{32,64},{64,96},{96,0},{1,33},{33,65},{65,97},{97,1},{2,34}... | collective-permute-start | bytes 80 | tf_op jit(solution)/shard_map/ppermute | solution.py:139
  9.9 18.7 %collective-permute-start.3 = (s32[6]{0:T(128)}, s32[6]{0:T(128)S(1)}, u32[]{:S(2)}, u32[]{:S(2)}) collective-permute-start(s32[6]{0:T(128)} %bitcast.146), channel_id=1, source_target_pairs={{0,64},{32,96},{64,0},{96,32},{1,65},{33,97},{65,1},{97,33},{2,66}... | collective-permute-start | bytes 80 | tf_op jit(solution)/shard_map/ppermute | solution.py:139
  13.2 15.4 %collective-permute-start.4 = (s32[6]{0:T(128)}, s32[6]{0:T(128)S(1)}, u32[]{:S(2)}, u32[]{:S(2)}) collective-permute-start(s32[6]{0:T(128)} %bitcast.147), channel_id=1, source_target_pairs={{0,96},{32,0},{64,32},{96,64},{1,97},{33,1},{65,33},{97,65},{2,98}... | collective-permute-start | bytes 80 | tf_op jit(solution)/shard_map/ppermute | solution.py:139
  17.9 12.6 %collective-permute-start = (bf16[256,1024]{1,0:T(8,128)(2,1)}, bf16[256,1024]{1,0:T(8,128)(2,1)}, u32[]{:S(2)}, u32[]{:S(2)}) collective-permute-start(bf16[256,1024]{1,0:T(8,128)(2,1)} %fusion.39), channel_id=1, source_target_pairs={{0,1},{1,0},{2,3},{3,2},{4,5},{5,4},{6,7},{7,6},{8,9},{9,8},{10,11... | collective-permute-start | bytes 1572872 | tf_op jit(solution)/shard_map/ppermute | solution.py:23
  22.2 12.9 %collective-permute-start.1 = (bf16[32,1024,16]{1,0,2:T(8,128)(2,1)}, bf16[32,1024,16]{1,0,2:T(8,128)(2,1)}, u32[]{:S(2)}, u32[]{:S(2)}) collective-permute-start(bf16[32,1024,16]{1,0,2:T(8,128)(2,1)} %copy.49), channel_id=1, source_target_pairs={{0,1},{1,0},{2,3},{3,2},{4,5},{5,4},{6,7},{7,6},{8,9},{9,8},{10,11... | collective-permute-start | bytes 3145736 | tf_op jit(solution)/shard_map/ppermute | solution.py:23
  32.1 4.7 %copy-start.4 = (bf16[256,1024]{1,0:T(8,128)(2,1)}, bf16[256,1024]{1,0:T(8,128)(2,1)S(1)}, u32[]{:S(2)}) copy-start(bf16[256,1024]{1,0:T(8,128)(2,1)S(1)} %get-tuple-element.15) | copy-start | bytes 1572868
  32.1 4.7 %copy-start.5 = (bf16[256,1024]{1,0:T(8,128)(2,1)}, bf16[256,1024]{1,0:T(8,128)(2,1)S(1)}, u32[]{:S(2)}) copy-start(bf16[256,1024]{1,0:T(8,128)(2,1)S(1)} %get-tuple-element.16) | copy-start | bytes 1572868
  32.1 3.0 %copy-start.2 = (f32[6,1024,16]{1,0,2:T(8,128)S(1)}, f32[6,1024,16]{1,0,2:T(8,128)}, u32[]{:S(2)}) copy-start(f32[6,1024,16]{1,0,2:T(8,128)} %fusion.74) | copy-start | bytes 1179652
  105.2 0.7 copy-start.9
  105.3 2.3 %copy-start.7 = (f32[4]{0:T(128)S(1)}, f32[4]{0:T(128)}, u32[]{:S(2)}) copy-start(f32[4]{0:T(128)} %param.17) | copy-start | bytes 52
  158.5 3.3 %copy-start.3 = (bf16[512,1024]{1,0:T(8,128)(2,1)S(1)}, bf16[512,1024]{1,0:T(8,128)(2,1)}, u32[]{:S(2)}) copy-start(bf16[512,1024]{1,0:T(8,128)(2,1)} %param.24) | copy-start | bytes 3145732
  162.6 1.4 copy-start.1
  165.0 3.3 %collective-permute-start.5 = (f32[256,1024]{1,0:T(8,128)}, f32[256,1024]{1,0:T(8,128)}, u32[]{:S(2)}, u32[]{:S(2)}) collective-permute-start(f32[256,1024]{1,0:T(8,128)} %constant_dynamic-slice_fusion.1), channel_id=1, source_target_pairs={{0,1},{1,0},{2,3},{3,2},{4,5},{5,4},{6,7},{7,6},{8,9},{9,8},{10,11... | collective-permute-start | bytes 3145736 | tf_op jit(solution)/shard_map/ppermute | solution.py:23
  170.4 2.0 %collective-permute-start.6 = (bf16[256,1024]{1,0:T(8,128)(2,1)S(1)}, bf16[256,1024]{1,0:T(8,128)(2,1)S(1)}, u32[]{:S(2)}, u32[]{:S(2)}) collective-permute-start(bf16[256,1024]{1,0:T(8,128)(2,1)S(1)} %fusion.43), channel_id=1, source_target_pairs={{0,1},{1,0},{2,3},{3,2},{4,5},{5,4},{6,7},{7,6},{8,9},{9,8},{10,11... | collective-permute-start | bytes 1572872 | tf_op jit(solution)/shard_map/ppermute | solution.py:23
  182.3 2.7 %collective-permute-start.7 = (f32[256,1024]{1,0:T(8,128)S(1)}, f32[256,1024]{1,0:T(8,128)S(1)}, u32[]{:S(2)}, u32[]{:S(2)}) collective-permute-start(f32[256,1024]{1,0:T(8,128)S(1)} %constant_dynamic-slice_fusion), channel_id=1, source_target_pairs={{0,1},{1,0},{2,3},{3,2},{4,5},{5,4},{6,7},{7,6},{8,9},{9,8},{10,11... | collective-permute-start | bytes 3145736 | tf_op jit(solution)/shard_map/ppermute | solution.py:23
Sparse Core Ops, SparseCore 0:
  9.5 73.8 all-gather.1
  105.4 44.7 reduce-scatter.1

commit v2 on v1

--- a/solution.py
+++ b/solution.py
@@ -91,7 +91,7 @@
 
     down_other = swap(adapter_down_factor)
 
-    plane = lax.all_gather(caches, ("y", "x"), axis=0, tiled=True)
+    plane = lax.all_gather(jnp.swapaxes(caches, -1, -2), ("y", "x"), axis=0, tiled=True)
     per_plane = plane.shape[0]
 
     normalized_rows = rms_scale(tokens, norm_gain_pair[0])
@@ -142,7 +142,9 @@
     line_rows = jnp.take(behind, (z_here - jnp.arange(z_count, dtype=jnp.int32)) % z_count, axis=0)
     local = line_rows - z_here * per_plane
     valid = ((local >= 0) & (local < per_plane)).astype(jnp.int32)
-    slots = pick_states(jnp.clip(local, 0, per_plane - 1).reshape(-1), valid.reshape(-1), plane, z_count)
+    picked = jnp.take(plane, jnp.clip(local, 0, per_plane - 1).reshape(-1), axis=0)
+    keep = valid.reshape(-1).astype(plane.dtype)[:, None, None, None]
+    slots = (picked * keep).reshape((z_count, -1) + plane.shape[1:])
     states = lax.psum_scatter(slots, "z", scatter_dimension=0, tiled=True)[0]
     keys = projected[1].astype(jnp.bfloat16).reshape(group, local_heads, head_size)
     values = projected[2].astype(jnp.bfloat16).reshape(group, local_heads, head_size)
@@ -158,7 +160,7 @@
     level = running - jnp.sum(member[:, :, None] * start_level[None, :, :], axis=1)
     masked_queries = queries[:, None, :, :] * member.astype(jnp.bfloat16)[:, :, None, None]
     from_state = jnp.einsum(
-        "tshi,shij->thj", masked_queries, states, preferred_element_type=jnp.float32
+        "tshi,shji->thj", masked_queries, states, preferred_element_type=jnp.float32
     )
     carried = from_state * jnp.exp(level)[:, :, None]
 

time: 192 us -> 167 us (0.87)
  Pallas kernels: 21.9 us -> 0 us
  matrix products: 40.1 us -> 34.7 us
    pallas_call x1 -> x0, Pallas kernels: 21.9 us -> none  [pick_states(): pl.pallas_call(body, out_shape=jax.ShapeDtypeStruct((lines, per_line) + b...]
    gather x0 -> x1, local copies, waits for them, and re-layouts: none -> 4.53 us  [on_device(): jnp.take(plane, jnp.clip(local, 0, per_plane - 1).reshape(-1), axis=0)]
    slice x1, local copies, waits for them, and re-layouts: 2.25 us -> 0.07 us  [on_device(): projected[1].astype(jnp.bfloat16).reshape(group, local_heads, head_size)]
    mul x0 -> x1, other arithmetic: none -> 2.04 us  [on_device(): slots = (picked * keep).reshape((z_count, -1) + plane.shape[1:])]
    unnamed x24 -> x35, local copies, waits for them, and re-layouts: 4.48 us -> 5.86 us
  transfers between devices with their start and end apart: 10 -> 10, of which waited for: 5 -> 5; matrix products, arithmetic and copies ran while one was open for 19% -> 17% of each run, Pallas kernels for 0% -> 0%
where the time goes in v2:
time: 167 us; the launch traced here: 166 us
  waiting for transfers between devices  81.8 us (49%)
  matrix products  34.7 us (21%)
  local copies, waits for them, and re-layouts  13.8 us (8%)
  between operations  13.8 us (8%)
  other arithmetic  12.8 us (8%)
  starting transfers between devices  9.64 us (6%)
    all_gather x1, waiting for transfers between devices, on_device(): lax.all_gather(jnp.swapaxes(caches, -1, -2), ('y', 'x'), axis=0, tiled=True)  44.7 us
    reduce_scatter x1, waiting for transfers between devices, on_device(): states = lax.psum_scatter(slots, 'z', scatter_dimension=0, tiled=True)[0]  30.7 us
    ppermute x3, starting transfers between devices, along_z(): lax.ppermute(value, 'z', perm=[(i, (i + d) % z_count) for i in range(z_co...  6.57 us
    ppermute x5, waiting for transfers between devices, swap(): return lax.ppermute(value, 'col', perm=[(0, 1), (1, 0)])  6.46 us
    unnamed x35, local copies, waits for them, and re-layouts  5.86 us
    dot_general x1, matrix products, on_device(): jnp.einsum('td,kdf->ktf', rows_two, feedforward_weight[:2], preferred_ele...  5.79 us
    gather x1, local copies, waits for them, and re-layouts, on_device(): jnp.take(plane, jnp.clip(local, 0, per_plane - 1).reshape(-1), axis=0)  4.53 us
    dot_general x1, matrix products, on_device(): jnp.einsum('tf,df->td', hidden, feedforward_weight[2], preferred_element_...  3.83 us
  transfers between devices with their start and end apart: 10, of which 5 were waited for; matrix products, arithmetic and copies ran while one was open for 17% of the time, Pallas kernels for 0%

profile of v2, /device:TPU:1, one launch (start us, length us, event | category | flops | bytes accessed | tf_op | source)
XLA Modules:
  0.0 166.4 jit_solution(15746825777017364594)
XLA Ops:
  6.5 2.2 %copy.50 = bf16[4,4,128,128]{2,3,1,0:T(8,128)(2,1)} copy(bf16[4,4,128,128]{3,2,1,0:T(8,128)(2,1)} %param.23) | data formatting | bytes 1048576 | tf_op args[10]
  8.8 0.0 reduce-scatter.2.cloned.1.call-start
  8.8 2.5 %collective-permute-start.2 = (s32[6]{0:T(128)}, s32[6]{0:T(128)S(1)}, u32[]{:S(2)}, u32[]{:S(2)}) collective-permute-start(s32[6]{0:T(128)} %bitcast.152), channel_id=1, source_target_pairs={{0,32},{32,64},{64,96},{96,0},{1,33},{33,65},{65,97},{97,1},{2,34}... | collective-permute-start | bytes 80 | tf_op jit(solution)/shard_map/ppermute | solution.py:139
  11.4 3.3 %collective-permute-start.3 = (s32[6]{0:T(128)}, s32[6]{0:T(128)S(1)}, u32[]{:S(2)}, u32[]{:S(2)}) collective-permute-start(s32[6]{0:T(128)} %bitcast.153), channel_id=1, source_target_pairs={{0,64},{32,96},{64,0},{96,32},{1,65},{33,97},{65,1},{97,33},{2,66}... | collective-permute-start | bytes 80 | tf_op jit(solution)/shard_map/ppermute | solution.py:139
  14.7 0.7 collective-permute-start.4
  15.4 1.2 fusion.38
  16.6 0.8 fusion.103
  17.4 2.0 %fusion.40 = bf16[256,1024]{1,0:T(8,128)(2,1)} fusion(bf16[256,1024]{1,0:T(8,128)(2,1)} %param.13, f32[1024]{0:T(1024)S(1)} %bitcast.143, f32[256]{0:T(256)S(1)} %add_rsqrt_fusion.2), kind=kLoop, calls=%fused_computation.52 | loop fusion | flops 1048576 | bytes 1053696 | tf_op jit(solution)/shard_map/convert_element_type | solution.py:19
  19.5 1.5 collective-permute-start
  21.0 2.8 %copy.51 = bf16[32,1024,16]{1,0,2:T(8,128)(2,1)} copy(bf16[32,1024,16]{1,2,0:T(8,128)(2,1)} %param.18) | data formatting | bytes 2097152 | tf_op args[5]
  23.8 0.1 reshape.438
  23.9 0.1 reshape_squeeze.3
  23.9 0.2 reduce-window.14
  24.2 0.1 fusion.61
  24.3 2.4 %convolution_convert_fusion = bf16[6,16,512]{2,0,1:T(8,128)(2,1)S(1)} fusion(bf16[64,16,512]{2,1,0:T(8,128)(2,1)} %param.19, s32[6]{0:T(128)S(1)} %bitcast.147), kind=kOutput, calls=%fused_computation.48 | convolution fusion | flops 6340992 | bytes 1146904 | tf_op jit(solution)/shard_map/gq,qjl->gjl/dot_general | solution.py:126
  26.7 3.2 %fusion.75 = f32[6,1024,16]{1,0,2:T(8,128)} fusion(s32[32]{0:T(128)S(1)} %iota_add_fusion.1, s32[6]{0:T(128)S(1)} %bitcast.148, bf16[32,1024,16]{1,2,0:T(8,128)(2,1)} %param.18), kind=kOutput, calls=%fused_computation.115 | convolution fusion | flops 6291648 | bytes 1441944 | tf_op jit(solution)/shard_map/sa,adr->sdr/dot_general | solution.py:116
  30.0 0.6 gather_fusion
  30.5 0.1 compare_and_fusion
  30.6 0.1 min.12
  30.7 1.5 broadcast_select_fusion.3
  32.3 3.1 %fusion.104 = (bf16[3,512,512]{1,2,0:T(8,128)(2,1)}, f32[3,512,512]{1,2,0:T(8,128)S(1)}) fusion(bf16[3,1024,512]{2,1,0:T(8,128)(2,1)S(1)} %copy-done, bf16[256,1024]{1,0:T(8,128)(2,1)S(1)} %get-tuple-element.18, bf16[256,1024]{1,0:T(8,128)(2,1)S(1)} %get-tuple-element.17), kind=kOutput, calls=%fused_computation.163 | convolution fusion | flops 1613496320 | bytes 8912896 | tf_op jit(solution)/shard_map/td,kdc->ktc/dot_general | solution.py:106
  35.4 1.5 fusion.37
  36.9 0.1 copy.53
  37.1 0.5 fusion.55
  37.6 1.1 fusion.36
  38.7 44.7 %all-gather.2.cloned.1.call-done = bf16[64,4,128,128]{3,2,1,0:T(8,128)(2,1)} async-done(((bf16[4,4,128,128]{3,2,1,0:T(8,128)(2,1)}), bf16[64,4,128,128]{3,2,1,0:T(8,128)(2,1)}) %all-gather.2.cloned.1.call-update) | async-done | bytes 8388624 | tf_op jit(solution)/shard_map/all_gather | solution.py:94
  83.4 4.5 %gather_fusion.1 = bf16[24,4,128,128]{3,2,1,0:T(8,128)(2,1)S(1)} fusion(bf16[64,4,128,128]{3,2,1,0:T(8,128)(2,1)} %all-gather.2.cloned.1.call-done, s32[1024]{0:T(1024)S(1)} %pad_clamp_fusion), kind=kCustom, calls=%fused_computation.1 | custom fusion | bytes 6291552 | tf_op jit(solution)/shard_map/jit(_take)/gather | solution.py:145
  87.9 2.0 %fusion.7 = bf16[4,6,4,128,128]{4,3,1,2,0:T(8,128)(2,1)} fusion(bf16[4,6,4,128,128]{4,3,2,1,0:T(8,128)(2,1)S(1)} %bitcast.129, pred[4,6]{1,0:T(4,128)(4,1)S(1)} %get-tuple-element.11, bf16[4,6]{1,0:T(4,128)(2,1)S(1)} %get-tuple-element.21), kind=kLoop, calls=%fused_computation.12 | loop fusion | flops 3145728 | bytes 6291528 | tf_op jit(solution)/shard_map/mul | solution.py:147
  90.0 0.1 convert_reduce_fusion
  90.1 0.1 fusion.62
  90.2 0.2 fusion.51
  90.4 0.6 copy-done.8
  91.0 0.2 copy-done.10
  91.1 0.4 convolution_bitcast_fusion.2
  91.5 0.1 fusion.98
  91.6 1.4 reduce-window.18
  93.0 0.2 slice_reduce_fusion
  93.2 0.2 reduce-window.19
  93.4 0.1 add_bitcast_fusion
  93.5 0.1 bitcast_subtract_fusion.1
  93.6 0.1 multiply_reduce_fusion.3
  93.7 0.1 multiply_reduce_fusion.2
  93.8 0.1 fusion.102
  93.9 0.3 copy.61
  94.2 3.6 %fusion.105 = (f32[4,512]{1,0:T(4,128)S(1)}, f32[4,512,512]{1,2,0:T(8,128)}) fusion(pred[512,512]{0,1:T(8,128)(4,1)S(1)} %fusion.51, bf16[512,4,128]{0,2,1:T(8,128)(2,1)S(1)} %bitcast.131, bf16[512,4,128]{0,2,1:T(8,128)(2,1)S(1)} %bitcast.137), kind=kOutput, calls=%fused_computation.164 | convolution fusion | flops 272630272 | bytes 5513216 | tf_op jit(solution)/shard_map/sub | solution.py:171
  97.7 30.7 %reduce-scatter.2.cloned.1.call-done = bf16[1,6,4,128,128]{4,3,1,2,0:T(8,128)(2,1)} async-done(((bf16[4,6,4,128,128]{4,3,1,2,0:T(8,128)(2,1)}), bf16[1,6,4,128,128]{4,3,1,2,0:T(8,128)(2,1)}) %reduce-scatter.2.cloned.1.call-update) | async-done | bytes 786448 | tf_op jit(solution)/shard_map/reduce_scatter | solution.py:148
  128.4 2.6 %fusion.32 = f32[512,4,128]{0,2,1:T(8,128)S(1)} fusion(bf16[512,6]{0,1:T(8,128)(2,1)S(1)} %get-tuple-element.23, bf16[512,4,128]{2,0,1:T(8,128)(2,1)S(1)} %copy.61, bf16[1,6,4,128,128]{4,3,1,2,0:T(8,128)(2,1)} %reduce-scatter.2.cloned.1.call-done, f32[512,4]{0,1:T(4,128)S(1)} %fusion.70), kind=kOutput, calls=%fused_computation.43 | convolution fusion | flops 404488192 | bytes 2373632 | tf_op jit(solution)/shard_map/tshi,shji->thj/dot_general | solution.py:162
  131.0 2.8 %multiply_reduce_fusion = (f32[512,4]{0,1:T(4,128)S(1)}, f32[512,4,128]{0,2,1:T(8,128)}) fusion(f32[512,4,128]{0,2,1:T(8,128)S(1)} %fusion.32, bf16[512,4,128]{0,2,1:T(8,128)(2,1)S(1)} %bitcast.135, f32[4,512]{1,0:T(4,128)S(1)} %bitcast.146, pred[512,512]{0,1:T(8,128)(4,1)S(1)} %fusion.51, bf16[512,4,128]{0,2,1:T(8,128)(2,1)S(1)} %bitcast.132, ...), kind=kOutput, calls=%fused_computation.66 | convolution fusion | flops 542898176 | bytes 3948544 | tf_op jit(solution)/shard_map/hqk,khd->qhd/dot_general | solution.py:176
  133.8 3.1 %fusion.35 = bf16[512,4,128]{0,2,1:T(8,128)(2,1)S(1)} fusion(bf16[512,4,128]{0,2,1:T(8,128)(2,1)S(1)} %bitcast.136, f32[4,512,512]{1,2,0:T(8,128)} %get-tuple-element.27, f32[4,512]{1,0:T(4,128)S(1)} %get-tuple-element.26, f32[512,4,128]{0,2,1:T(8,128)} %get-tuple-element.29, f32[512,4]{0,1:T(4,128)S(1)} %add_rsqrt_fusion, f32[512,4]{0,1:T(4,128)S(1)} %fusion.69), kind=kOutput, calls=%fused_computation.44 | convolution fusion | flops 271581184 | bytes 6316032 | tf_op jit(solution)/shard_map/hqk,khd->qhd/dot_general | solution.py:173
  137.0 0.7 fusion.108
  137.7 1.1 constant_dynamic-slice_fusion.1
  138.8 0.6 collective-permute-start.5
  139.4 2.6 %collective-permute-done.5 = f32[256,1024]{1,0:T(8,128)} collective-permute-done((f32[256,1024]{1,0:T(8,128)}, f32[256,1024]{1,0:T(8,128)}, u32[]{:S(2)}, u32[]{:S(2)}) %collective-permute-start.5) | collective-permute-done | bytes 1048608 | tf_op jit(solution)/shard_map/ppermute | solution.py:23
  142.1 1.5 fusion.42
  143.6 0.2 fusion.44
  143.8 0.5 collective-permute-start.6
  144.2 1.5 collective-permute-done.6
  145.7 0.3 broadcast_select_fusion.1
  146.1 5.8 %fusion.3 = f32[2,512,1408]{2,1,0:T(8,128)S(1)} fusion(bf16[3,1024,1408]{2,1,0:T(8,128)(2,1)} %param.25, bf16[256,1024]{1,0:T(8,128)(2,1)S(1)} %get-tuple-element.16, bf16[256,1024]{1,0:T(8,128)(2,1)S(1)} %get-tuple-element.15), kind=kOutput, calls=%fused_computation.5 | convolution fusion | flops 2954887168 | bytes 12582912 | tf_op jit(solution)/shard_map/td,kdf->ktf/dot_general | solution.py:190
  151.9 3.8 %fusion.11 = f32[512,1024]{1,0:T(8,128)S(1)} fusion(bf16[3,1024,1408]{2,1,0:T(8,128)(2,1)} %param.25, f32[2,512,1408]{2,1,0:T(8,128)S(1)} %fusion.3), kind=kOutput, calls=%fused_computation.17 | convolution fusion | flops 1480720384 | bytes 10747904 | tf_op jit(solution)/shard_map/tf,df->td/dot_general | solution.py:194
  155.7 0.1 constant_dynamic-slice_fusion
  155.8 0.4 collective-permute-start.7
  156.2 2.3 %collective-permute-done.7 = f32[256,1024]{1,0:T(8,128)S(1)} collective-permute-done((f32[256,1024]{1,0:T(8,128)S(1)}, f32[256,1024]{1,0:T(8,128)S(1)}, u32[]{:S(2)}, u32[]{:S(2)}) %collective-permute-start.7) | collective-permute-done | bytes 1048608 | tf_op jit(solution)/shard_map/ppermute | solution.py:23
  158.5 1.1 fusion.45
  (56 shorter events, 0.3 us)
Async XLA Ops:
  6.5 25.7 %copy-start = (bf16[3,1024,512]{2,1,0:T(8,128)(2,1)S(1)}, bf16[3,1024,512]{2,1,0:T(8,128)(2,1)}, u32[]{:S(2)}) copy-start(bf16[3,1024,512]{2,1,0:T(8,128)(2,1)} %param.15) | copy-start | bytes 9437188
  6.5 17.2 %copy-start.15 = (s32[1,2,3]{2,1,0:T(2,128)S(1)}, s32[1,2,3]{2,1,0:T(2,128)}, u32[]{:S(2)}) copy-start(s32[1,2,3]{2,1,0:T(2,128)} %param.20) | copy-start | bytes 76
  6.5 17.7 %copy-start.11 = (s32[1,6]{1,0:T(1,128)S(1)}, s32[1,6]{1,0:T(1,128)}, u32[]{:S(2)}) copy-start(s32[1,6]{1,0:T(1,128)} %param.21) | copy-start | bytes 76
  6.5 76.8 %all-gather.2.cloned.1.call-start = ((), (), s32[]{:S(2)}) async-start(), calls=%async_computation.1 | async-start | bytes 8912896 | tf_op jit(solution)/shard_map/all_gather | solution.py:94
  8.8 119.6 %reduce-scatter.2.cloned.1.call-start = ((), (), s32[]{:S(2)}) async-start(), calls=%async_computation.2 | async-start | bytes 3932160 | tf_op jit(solution)/shard_map/reduce_scatter | solution.py:148
  8.8 21.1 %copy-start.13 = (s32[1,6]{1,0:T(1,128)S(1)}, s32[1,6]{1,0:T(1,128)}, u32[]{:S(2)}) copy-start(s32[1,6]{1,0:T(1,128)} %param.22) | copy-start | bytes 76
  8.8 21.1 %collective-permute-start.2 = (s32[6]{0:T(128)}, s32[6]{0:T(128)S(1)}, u32[]{:S(2)}, u32[]{:S(2)}) collective-permute-start(s32[6]{0:T(128)} %bitcast.152), channel_id=1, source_target_pairs={{0,32},{32,64},{64,96},{96,0},{1,33},{33,65},{65,97},{97,1},{2,34}... | collective-permute-start | bytes 80 | tf_op jit(solution)/shard_map/ppermute | solution.py:139
  11.4 18.6 %collective-permute-start.3 = (s32[6]{0:T(128)}, s32[6]{0:T(128)S(1)}, u32[]{:S(2)}, u32[]{:S(2)}) collective-permute-start(s32[6]{0:T(128)} %bitcast.153), channel_id=1, source_target_pairs={{0,64},{32,96},{64,0},{96,32},{1,65},{33,97},{65,1},{97,33},{2,66}... | collective-permute-start | bytes 80 | tf_op jit(solution)/shard_map/ppermute | solution.py:139
  14.7 15.3 %collective-permute-start.4 = (s32[6]{0:T(128)}, s32[6]{0:T(128)S(1)}, u32[]{:S(2)}, u32[]{:S(2)}) collective-permute-start(s32[6]{0:T(128)} %bitcast.154), channel_id=1, source_target_pairs={{0,96},{32,0},{64,32},{96,64},{1,97},{33,1},{65,33},{97,65},{2,98}... | collective-permute-start | bytes 80 | tf_op jit(solution)/shard_map/ppermute | solution.py:139
  19.5 11.3 %collective-permute-start = (bf16[256,1024]{1,0:T(8,128)(2,1)}, bf16[256,1024]{1,0:T(8,128)(2,1)}, u32[]{:S(2)}, u32[]{:S(2)}) collective-permute-start(bf16[256,1024]{1,0:T(8,128)(2,1)} %fusion.40), channel_id=1, source_target_pairs={{0,1},{1,0},{2,3},{3,2},{4,5},{5,4},{6,7},{7,6},{8,9},{9,8},{10,11... | collective-permute-start | bytes 1572872 | tf_op jit(solution)/shard_map/ppermute | solution.py:23
  23.8 11.6 %collective-permute-start.1 = (bf16[32,1024,16]{1,0,2:T(8,128)(2,1)}, bf16[32,1024,16]{1,0,2:T(8,128)(2,1)}, u32[]{:S(2)}, u32[]{:S(2)}) collective-permute-start(bf16[32,1024,16]{1,0,2:T(8,128)(2,1)} %copy.51), channel_id=1, source_target_pairs={{0,1},{1,0},{2,3},{3,2},{4,5},{5,4},{6,7},{7,6},{8,9},{9,8},{10,11... | collective-permute-start | bytes 3145736 | tf_op jit(solution)/shard_map/ppermute | solution.py:23
  32.3 4.8 %copy-start.7 = (bf16[256,1024]{1,0:T(8,128)(2,1)}, bf16[256,1024]{1,0:T(8,128)(2,1)S(1)}, u32[]{:S(2)}) copy-start(bf16[256,1024]{1,0:T(8,128)(2,1)S(1)} %get-tuple-element.17) | copy-start | bytes 1572868
  32.3 4.8 %copy-start.9 = (bf16[256,1024]{1,0:T(8,128)(2,1)}, bf16[256,1024]{1,0:T(8,128)(2,1)S(1)}, u32[]{:S(2)}) copy-start(bf16[256,1024]{1,0:T(8,128)(2,1)S(1)} %get-tuple-element.18) | copy-start | bytes 1572868
  32.3 3.1 %copy-start.4 = (f32[6,1024,16]{1,0,2:T(8,128)S(1)}, f32[6,1024,16]{1,0,2:T(8,128)}, u32[]{:S(2)}) copy-start(f32[6,1024,16]{1,0,2:T(8,128)} %fusion.75) | copy-start | bytes 1179652
  89.9 1.0 copy-start.8
  89.9 1.2 copy-start.10
  89.9 1.2 copy-start.14
  89.9 1.6 copy-start.12
  89.9 3.8 %copy-start.6 = (bf16[3,512,512]{1,2,0:T(8,128)(2,1)S(1)}, bf16[3,512,512]{1,2,0:T(8,128)(2,1)}, u32[]{:S(2)}) copy-start(bf16[3,512,512]{1,2,0:T(8,128)(2,1)} %get-tuple-element.24) | copy-start | bytes 4718596
  90.0 3.9 %copy-start.3 = (bf16[512,512]{0,1:T(8,128)(2,1)S(1)}, bf16[512,512]{0,1:T(8,128)(2,1)}, u32[]{:S(2)}) copy-start(bf16[512,512]{0,1:T(8,128)(2,1)} %fusion.36) | copy-start | bytes 1572868
  133.8 3.1 %copy-start.5 = (bf16[512,1024]{1,0:T(8,128)(2,1)S(1)}, bf16[512,1024]{1,0:T(8,128)(2,1)}, u32[]{:S(2)}) copy-start(bf16[512,1024]{1,0:T(8,128)(2,1)} %param.24) | copy-start | bytes 3145732
  136.9 5.1 %copy-start.2 = (bf16[256,1024]{1,0:T(8,128)(2,1)S(1)}, bf16[256,1024]{1,0:T(8,128)(2,1)}, u32[]{:S(2)}) copy-start(bf16[256,1024]{1,0:T(8,128)(2,1)} %param.13) | copy-start | bytes 1572868
  138.8 3.2 %collective-permute-start.5 = (f32[256,1024]{1,0:T(8,128)}, f32[256,1024]{1,0:T(8,128)}, u32[]{:S(2)}, u32[]{:S(2)}) collective-permute-start(f32[256,1024]{1,0:T(8,128)} %constant_dynamic-slice_fusion.1), channel_id=1, source_target_pairs={{0,1},{1,0},{2,3},{3,2},{4,5},{5,4},{6,7},{7,6},{8,9},{9,8},{10,11... | collective-permute-start | bytes 3145736 | tf_op jit(solution)/shard_map/ppermute | solution.py:23
  143.8 2.0 %collective-permute-start.6 = (bf16[256,1024]{1,0:T(8,128)(2,1)S(1)}, bf16[256,1024]{1,0:T(8,128)(2,1)S(1)}, u32[]{:S(2)}, u32[]{:S(2)}) collective-permute-start(bf16[256,1024]{1,0:T(8,128)(2,1)S(1)} %fusion.44), channel_id=1, source_target_pairs={{0,1},{1,0},{2,3},{3,2},{4,5},{5,4},{6,7},{7,6},{8,9},{9,8},{10,11... | collective-permute-start | bytes 1572872 | tf_op jit(solution)/shard_map/ppermute | solution.py:23
  151.9 7.7 %copy-start.1 = (bf16[3,1024,512]{2,1,0:T(8,128)(2,1)S(1)}, bf16[3,1024,512]{2,1,0:T(8,128)(2,1)}, u32[]{:S(2)}) copy-start(bf16[3,1024,512]{2,1,0:T(8,128)(2,1)} %param.15) | copy-start | bytes 9437188
  155.8 2.7 %collective-permute-start.7 = (f32[256,1024]{1,0:T(8,128)S(1)}, f32[256,1024]{1,0:T(8,128)S(1)}, u32[]{:S(2)}, u32[]{:S(2)}) collective-permute-start(f32[256,1024]{1,0:T(8,128)S(1)} %constant_dynamic-slice_fusion), channel_id=1, source_target_pairs={{0,1},{1,0},{2,3},{3,2},{4,5},{5,4},{6,7},{7,6},{8,9},{9,8},{10,11... | collective-permute-start | bytes 3145736 | tf_op jit(solution)/shard_map/ppermute | solution.py:23
Sparse Core Ops, SparseCore 0:
  9.5 73.8 all-gather.1
  90.1 38.2 reduce-scatter.1

commit v3 on v2

--- a/solution.py
+++ b/solution.py
@@ -62,6 +62,21 @@
             scratch_shapes=[pltpu.VMEM(block, plane.dtype), pltpu.SemaphoreType.DMA((slots,))],
         ),
     )(index, valid, plane)
+
+
+def ring_gather(value, axis):
+    count = lax.axis_size(axis)
+    here = lax.axis_index(axis)
+
+    def shift(v, d):
+        return lax.ppermute(v, axis, perm=[(i, (i + d) % count) for i in range(count)])
+
+    from_before = shift(value, 1)
+    from_after = shift(value, -1)
+    half = value.shape[0] // 2
+    two_away = jnp.concatenate([shift(from_before[:half], 1), shift(from_after[half:], -1)], axis=0)
+    by_offset = jnp.stack([value, from_after, two_away, from_before])
+    return jnp.take(by_offset, (jnp.arange(count, dtype=jnp.int32) - here) % count, axis=0)
 
 
 def on_device(
@@ -91,7 +106,10 @@
 
     down_other = swap(adapter_down_factor)
 
-    plane = lax.all_gather(jnp.swapaxes(caches, -1, -2), ("y", "x"), axis=0, tiled=True)
+    moved = jnp.swapaxes(caches, -1, -2)
+    split = moved.shape[1] // 2
+    plane = lax.all_gather(moved[:, :split], ("y", "x"), axis=0, tiled=True)
+    plane_two = ring_gather(ring_gather(moved[:, split:], "y"), "x")
     per_plane = plane.shape[0]
 
     normalized_rows = rms_scale(tokens, norm_gain_pair[0])
@@ -142,9 +160,17 @@
     line_rows = jnp.take(behind, (z_here - jnp.arange(z_count, dtype=jnp.int32)) % z_count, axis=0)
     local = line_rows - z_here * per_plane
     valid = ((local >= 0) & (local < per_plane)).astype(jnp.int32)
-    picked = jnp.take(plane, jnp.clip(local, 0, per_plane - 1).reshape(-1), axis=0)
+    flat = jnp.clip(local, 0, per_plane - 1).reshape(-1)
+    per_chip = caches.shape[0]
+    x_count = lax.axis_size("x")
+    y_count = lax.axis_size("y")
+    y_of = flat // (per_chip * x_count)
+    x_of = (flat // per_chip) % x_count
+    flat_two = (x_of * y_count + y_of) * per_chip + flat % per_chip
     keep = valid.reshape(-1).astype(plane.dtype)[:, None, None, None]
-    slots = (picked * keep).reshape((z_count, -1) + plane.shape[1:])
+    picked = jnp.take(plane, flat, axis=0) * keep
+    picked_two = jnp.take(plane_two.reshape((-1,) + plane_two.shape[3:]), flat_two, axis=0) * keep
+    slots = jnp.concatenate([picked, picked_two], axis=1).reshape((z_count, -1) + moved.shape[1:])
     states = lax.psum_scatter(slots, "z", scatter_dimension=0, tiled=True)[0]
     keys = projected[1].astype(jnp.bfloat16).reshape(group, local_heads, head_size)
     values = projected[2].astype(jnp.bfloat16).reshape(group, local_heads, head_size)

time: 167 us -> 206 us (1.23)
  other arithmetic: 12.8 us -> 34.7 us
  local copies, waits for them, and re-layouts: 13.8 us -> 35.3 us
  waiting for transfers between devices: 81.8 us -> 64.6 us
  starting transfers between devices: 9.64 us -> 21.7 us
    all_gather x1, waiting for transfers between devices: 44.7 us -> 0.02 us  [on_device(): plane = lax.all_gather(moved[:, :split], ('y', 'x'), axis=0, tiled=True)]
    ppermute x0 -> x8, waiting for transfers between devices: none -> 24.8 us  [shift(): lax.ppermute(v, axis, perm=[(i, (i + d) % count) for i in range(count)])]
    ppermute x0 -> x8, starting transfers between devices: none -> 12.1 us  [shift(): lax.ppermute(v, axis, perm=[(i, (i + d) % count) for i in range(count)])]
    gather x1 -> x4, local copies, waits for them, and re-layouts: 4.53 us -> 14.9 us  [the longest x2 8.54 us: ring_gather(): jnp.take(by_offset, (jnp.arange(count, dtype=jnp.int32) - here) % count,...]
    select_n x1 -> x6, other arithmetic: 0.01 us -> 8.69 us  [the longest x5 7.47 us: ring_gather(): jnp.take(by_offset, (jnp.arange(count, dtype=jnp.int32) - here) % count,...]
    another operation x3 -> x7, other arithmetic: 1.76 us -> 7.06 us  [the longest x4 5.47 us: ring_gather(): by_offset = jnp.stack([value, from_after, two_away, from_before])]
    slice x1 -> x5, local copies, waits for them, and re-layouts: 0.16 us -> 3.37 us  [the longest x2 1.61 us: ring_gather(): from_before[:half]]
    gather x1 -> x4, other arithmetic: 0.01 us -> 3.04 us  [on_device(): jnp.take(plane, jnp.clip(local, 0, per_plane - 1).reshape(-1), axis=0)]
  transfers between devices with their start and end apart: 10 -> 18, of which waited for: 5 -> 8; matrix products, arithmetic and copies ran while one was open for 17% -> 34% of each run, Pallas kernels for 0% -> 0%
where the time goes in v3:
time: 206 us; the launch traced here: 205 us
  waiting for transfers between devices  64.6 us (31%)
  local copies, waits for them, and re-layouts  35.3 us (17%)
  other arithmetic  34.7 us (17%)
  matrix products  34.4 us (17%)
  starting transfers between devices  21.7 us (11%)
  between operations  13.9 us (7%)
    reduce_scatter x1, waiting for transfers between devices, on_device(): states = lax.psum_scatter(slots, 'z', scatter_dimension=0, tiled=True)[0]  33.3 us
    ppermute x8, waiting for transfers between devices, shift(): lax.ppermute(v, axis, perm=[(i, (i + d) % count) for i in range(count)])  24.8 us
    ppermute x8, starting transfers between devices, shift(): lax.ppermute(v, axis, perm=[(i, (i + d) % count) for i in range(count)])  12.1 us
    gather x2, local copies, waits for them, and re-layouts, ring_gather(): jnp.take(by_offset, (jnp.arange(count, dtype=jnp.int32) - here) % count,...  8.54 us
    select_n x5, other arithmetic, ring_gather(): jnp.take(by_offset, (jnp.arange(count, dtype=jnp.int32) - here) % count,...  7.47 us
    ppermute x5, waiting for transfers between devices, swap(): return lax.ppermute(value, 'col', perm=[(0, 1), (1, 0)])  6.46 us
    unnamed x67, local copies, waits for them, and re-layouts  5.93 us
    dot_general x1, matrix products, on_device(): jnp.einsum('td,kdf->ktf', rows_two, feedforward_weight[:2], preferred_ele...  5.78 us
  transfers between devices with their start and end apart: 18, of which 8 were waited for; matrix products, arithmetic and copies ran while one was open for 34% of the time, Pallas kernels for 0%

profile of v3, /device:TPU:1, one launch (start us, length us, event | category | flops | bytes accessed | tf_op | source)
XLA Modules:
  0.0 204.7 jit_solution(6733692024441208771)
XLA Ops:
  6.5 2.2 %copy.50 = bf16[4,4,128,128]{2,3,1,0:T(8,128)(2,1)} copy(bf16[4,4,128,128]{3,2,1,0:T(8,128)(2,1)} %param.25) | data formatting | bytes 1048576 | tf_op args[10]
  8.7 2.0 slice_bitcast_fusion.2
  10.8 2.2 %collective-permute-start.6 = (bf16[4,2,128,128]{3,2,1,0:T(8,128)(2,1)}, bf16[4,2,128,128]{3,2,1,0:T(8,128)(2,1)}, u32[]{:S(2)}, u32[]{:S(2)}) collective-permute-start(bf16[4,2,128,128]{3,2,1,0:T(8,128)(2,1)} %get-tuple-element.21), channel_id=1, source_target_pairs={{0,8},{8,16},{16,24},{24,0},{1,9},{9,17},{17,25},{25,1},{2,10},{10... | collective-permute-start | bytes 786440 | tf_op jit(solution)/shard_map/ppermute | solution.py:72
  13.0 1.5 collective-permute-start.5
  14.6 1.6 collective-permute-start.2
  16.2 3.3 %collective-permute-start.3 = (s32[6]{0:T(128)}, s32[6]{0:T(128)}, u32[]{:S(2)}, u32[]{:S(2)}) collective-permute-start(s32[6]{0:T(128)} %bitcast.171), channel_id=1, source_target_pairs={{0,64},{32,96},{64,0},{96,32},{1,65},{33,97},{65,1},{97,33},{2,66}... | collective-permute-start | bytes 80 | tf_op jit(solution)/shard_map/ppermute | solution.py:157
  19.5 0.7 collective-permute-start.4
  20.2 0.8 reshape.526
  21.0 0.8 reshape_squeeze.3
  23.0 2.8 %copy.51 = bf16[32,1024,16]{1,0,2:T(8,128)(2,1)} copy(bf16[32,1024,16]{1,2,0:T(8,128)(2,1)} %param.20) | data formatting | bytes 2097152 | tf_op args[5]
  28.9 1.2 fusion.37
  30.8 0.7 fusion.60
  31.5 2.0 fusion.39
  33.5 2.4 %convolution_convert_fusion = bf16[6,16,512]{2,0,1:T(8,128)(2,1)S(1)} fusion(bf16[64,16,512]{2,1,0:T(8,128)(2,1)} %param.21, s32[6]{0:T(128)S(1)} %bitcast.165), kind=kOutput, calls=%fused_computation.54 | convolution fusion | flops 6340992 | bytes 1146904 | tf_op jit(solution)/shard_map/gq,qjl->gjl/dot_general | solution.py:144
  35.9 2.1 %fusion.74 = f32[6,1024,16]{1,0,2:T(8,128)} fusion(s32[32]{0:T(128)S(1)} %iota_add_fusion.1, s32[6]{0:T(128)S(1)} %bitcast.166, bf16[32,1024,16]{1,2,0:T(8,128)(2,1)S(1)} %copy-done.4), kind=kOutput, calls=%fused_computation.128 | convolution fusion | flops 6291648 | bytes 1441944 | tf_op jit(solution)/shard_map/sa,adr->sdr/dot_general | solution.py:134
  38.0 2.0 collective-permute-start.1
  40.1 0.7 pad_add_fusion
  40.7 0.7 gather_fusion
  41.4 0.7 fusion.83
  42.7 1.2 compare_and_fusion
  44.0 1.2 add_select_fusion
  45.2 1.2 convert_convert_fusion
  46.4 1.6 slice.96
  48.1 1.6 slice.97
  49.6 2.6 %collective-permute-start.8 = (bf16[2,2,128,128]{3,2,1,0:T(8,128)(2,1)}, bf16[2,2,128,128]{3,2,1,0:T(8,128)(2,1)}, u32[]{:S(2)}, u32[]{:S(2)}) collective-permute-start(bf16[2,2,128,128]{3,2,1,0:T(8,128)(2,1)} %slice.97), channel_id=1, source_target_pairs={{0,24},{8,0},{16,8},{24,16},{1,25},{9,1},{17,9},{25,17},{2,26},{10... | collective-permute-start | bytes 393224 | tf_op jit(solution)/shard_map/ppermute | solution.py:72
  52.8 1.3 reshape.534
  54.1 1.3 pad_clamp_fusion.3
  55.3 2.1 %collective-permute-done.7 = bf16[2,2,128,128]{3,2,1,0:T(8,128)(2,1)} collective-permute-done((bf16[2,2,128,128]{3,2,1,0:T(8,128)(2,1)}, bf16[2,2,128,128]{3,2,1,0:T(8,128)(2,1)}, u32[]{:S(2)}, u32[]{:S(2)}) %collective-permute-start.7) | collective-permute-done | bytes 131104 | tf_op jit(solution)/shard_map/ppermute | solution.py:72
  58.1 1.0 maximum_bitcast_fusion.3
  59.1 2.1 %pad_maximum_fusion.3 = bf16[4,4,2,128,128]{4,3,2,1,0:T(8,128)(2,1)} fusion(bf16[1,4,2,128,128]{4,3,2,1,0:T(8,128)(2,1)} %bitcast.31, bf16[1,4,2,128,128]{4,3,2,1,0:T(8,128)(2,1)S(1)} %maximum_bitcast_fusion.3, bf16[1,4,2,128,128]{4,3,2,1,0:T(8,128)(2,1)} %bitcast.29, bf16[1,4,2,128,128]{4,3,2,1,0:T(8,128)(2,1)S(1)} %get-tuple-element.20), kind=kLoop, calls=%fused_computation.66 | loop fusion | flops 1572864 | bytes 2097152 | tf_op jit(solution)/shard_map/stack | solution.py:78
  61.3 3.1 %gather_fusion.1 = bf16[4,4,2,128,128]{4,3,2,1,0:T(8,128)(2,1)} fusion(bf16[4,4,2,128,128]{4,3,2,1,0:T(8,128)(2,1)} %pad_maximum_fusion.3, s32[1024]{0:T(1024)} %pad_clamp_fusion.2), kind=kCustom, calls=%fused_computation.3 | custom fusion | bytes 2097168 | tf_op jit(solution)/shard_map/jit(_take)/gather | solution.py:79
  64.4 1.4 broadcast_select_fusion
  65.8 1.4 collective-permute-start.10
  67.3 1.3 collective-permute-start.9
  68.6 1.4 bitcast_select_fusion.1
  70.0 1.4 broadcast_select_fusion.4
  71.4 3.0 %fusion.111 = (bf16[3,512,512]{1,2,0:T(8,128)(2,1)}, f32[3,512,512]{1,2,0:T(8,128)S(1)}) fusion(bf16[3,1024,512]{2,1,0:T(8,128)(2,1)S(1)} %copy-done, bf16[256,1024]{1,0:T(8,128)(2,1)S(1)} %get-tuple-element.19, bf16[256,1024]{1,0:T(8,128)(2,1)S(1)} %get-tuple-element.18), kind=kOutput, calls=%fused_computation.217 | convolution fusion | flops 1613496320 | bytes 8912896 | tf_op jit(solution)/shard_map/td,kdc->ktc/dot_general | solution.py:124
  74.5 1.5 fusion.36
  76.1 14.3 %collective-permute-done.10 = bf16[4,4,2,128,128]{4,3,2,1,0:T(8,128)(2,1)S(1)} collective-permute-done((bf16[4,4,2,128,128]{4,3,2,1,0:T(8,128)(2,1)S(1)}, bf16[4,4,2,128,128]{4,3,2,1,0:T(8,128)(2,1)S(1)}, u32[]{:S(2)}, u32[]{:S(2)}) %collective-permute-start.10) | collective-permute-done | bytes 1048608 | tf_op jit(solution)/shard_map/ppermute | solution.py:72
  90.9 2.7 %collective-permute-start.12 = (bf16[2,4,2,128,128]{4,3,2,1,0:T(8,128)(2,1)S(1)}, bf16[2,4,2,128,128]{4,3,2,1,0:T(8,128)(2,1)S(1)}, u32[]{:S(2)}, u32[]{:S(2)}) collective-permute-start(bf16[2,4,2,128,128]{4,3,2,1,0:T(8,128)(2,1)S(1)} %slice.99), channel_id=1, source_target_pairs={{0,6},{2,0},{4,2},{6,4},{1,7},{3,1},{5,3},{7,5},{8,14},{10,8},{12,... | collective-permute-start | bytes 1572872 | tf_op jit(solution)/shard_map/ppermute | solution.py:72
  94.1 1.1 fusion.35
  95.2 7.7 %collective-permute-done.11 = bf16[2,4,2,128,128]{4,3,2,1,0:T(8,128)(2,1)S(1)} collective-permute-done((bf16[2,4,2,128,128]{4,3,2,1,0:T(8,128)(2,1)S(1)}, bf16[2,4,2,128,128]{4,3,2,1,0:T(8,128)(2,1)S(1)}, u32[]{:S(2)}, u32[]{:S(2)}) %collective-permute-start.11) | collective-permute-done | bytes 524320 | tf_op jit(solution)/shard_map/ppermute | solution.py:72
  103.0 2.3 %pad_maximum_fusion = bf16[4,4,4,2,128,128]{5,4,3,2,1,0:T(8,128)(2,1)} fusion(bf16[1,4,4,2,128,128]{5,4,3,2,1,0:T(8,128)(2,1)S(1)} %bitcast.146, bf16[1,4,4,2,128,128]{5,4,3,2,1,0:T(8,128)(2,1)S(1)} %maximum_bitcast_fusion, bf16[1,4,4,2,128,128]{5,4,3,2,1,0:T(8,128)(2,1)S(1)} %bitcast.147, bf16[1,4,4,2,128,128]{5,4,3,2,1,0:T(8,128)(2,1)S(1)} %bitcast_select_fusion.1), kind=kLoop, calls=%fused_computation.9 | loop fusion | flops 6291456 | bytes 8388608 | tf_op jit(solution)/shard_map/stack | solution.py:78
  105.3 5.4 %gather_fusion.2 = bf16[4,4,4,2,128,128]{5,4,3,2,1,0:T(8,128)(2,1)} fusion(bf16[4,4,4,2,128,128]{5,4,3,2,1,0:T(8,128)(2,1)} %pad_maximum_fusion, s32[1024]{0:T(1024)} %pad_clamp_fusion.1), kind=kCustom, calls=%fused_computation.4 | custom fusion | bytes 8388624 | tf_op jit(solution)/shard_map/jit(_take)/gather | solution.py:79
  110.7 4.6 %bitcast_select_fusion = bf16[64,2,128,128]{3,2,1,0:T(8,128)(2,1)} fusion(bf16[4,4,4,2,128,128]{5,4,3,2,1,0:T(8,128)(2,1)} %gather_fusion.2, pred[64]{0:T(512)(128)(4,1)S(1)} %copy-done.21), kind=kLoop, calls=%fused_computation.10 | loop fusion | flops 2097152 | bytes 8388672 | tf_op jit(solution)/shard_map/jit(_take)/select_n | solution.py:79
  115.3 3.2 %gather_fusion.4 = bf16[24,2,128,128]{3,2,1,0:T(8,128)(2,1)S(1)} fusion(bf16[64,2,128,128]{3,2,1,0:T(8,128)(2,1)} %bitcast_select_fusion, s32[1024]{0:T(1024)} %pad_clamp_fusion), kind=kCustom, calls=%fused_computation.1.clone | custom fusion | bytes 3145824 | tf_op jit(solution)/shard_map/jit(_take)/gather | solution.py:172
  118.5 3.2 %gather_fusion.3 = bf16[24,2,128,128]{3,2,1,0:T(8,128)(2,1)S(1)} fusion(bf16[64,2,128,128]{3,2,1,0:T(8,128)(2,1)} %all-gather.2.cloned.1.call-done, s32[1024]{0:T(1024)} %pad_clamp_fusion.3), kind=kCustom, calls=%fused_computation.clone | custom fusion | bytes 3145824 | tf_op jit(solution)/shard_map/jit(_take)/gather | solution.py:171
  122.4 2.1 %copy.60 = bf16[4,6,4,128,128]{4,3,1,2,0:T(8,128)(2,1)} copy(bf16[4,6,4,128,128]{4,3,2,1,0:T(8,128)(2,1)S(1)} %bitcast.145) | data formatting | bytes 6291456 | tf_op jit(solution)/shard_map/reshape | solution.py:173
  126.2 1.2 reduce-window.18
  128.6 3.6 %fusion.112 = (f32[4,512]{1,0:T(4,128)S(1)}, f32[4,512,512]{1,2,0:T(8,128)}) fusion(pred[512,512]{0,1:T(8,128)(4,1)S(1)} %fusion.50, bf16[512,4,128]{0,2,1:T(8,128)(2,1)S(1)} %bitcast.149, bf16[512,4,128]{0,2,1:T(8,128)(2,1)S(1)} %bitcast.155), kind=kOutput, calls=%fused_computation.218 | convolution fusion | flops 272630272 | bytes 5513216 | tf_op jit(solution)/shard_map/sub | solution.py:197
  132.2 33.3 %reduce-scatter.2.cloned.1.call-done = bf16[1,6,4,128,128]{4,3,1,2,0:T(8,128)(2,1)} async-done(((bf16[4,6,4,128,128]{4,3,1,2,0:T(8,128)(2,1)}), bf16[1,6,4,128,128]{4,3,1,2,0:T(8,128)(2,1)}) %reduce-scatter.2.cloned.1.call-update) | async-done | bytes 786448 | tf_op jit(solution)/shard_map/reduce_scatter | solution.py:174
  165.5 3.6 %fusion.31 = f32[512,4,128]{0,2,1:T(8,128)} fusion(bf16[512,6]{0,1:T(8,128)(2,1)S(1)} %copy-done.16, bf16[512,4,128]{2,0,1:T(8,128)(2,1)S(1)} %copy.61, bf16[1,6,4,128,128]{4,3,1,2,0:T(8,128)(2,1)} %reduce-scatter.2.cloned.1.call-done, f32[512,4]{0,1:T(4,128)S(1)} %fusion.69), kind=kOutput, calls=%fused_computation.49 | convolution fusion | flops 404488192 | bytes 2373632 | tf_op jit(solution)/shard_map/tshi,shji->thj/dot_general | solution.py:188
  169.1 3.1 %multiply_reduce_fusion = (f32[512,4]{0,1:T(4,128)S(1)}, f32[512,4,128]{0,2,1:T(8,128)S(1)}) fusion(f32[512,4,128]{0,2,1:T(8,128)} %fusion.31, bf16[512,4,128]{0,2,1:T(8,128)(2,1)S(1)} %bitcast.153, f32[4,512]{1,0:T(4,128)S(1)} %bitcast.164, pred[512,512]{0,1:T(8,128)(4,1)S(1)} %fusion.50, bf16[512,4,128]{0,2,1:T(8,128)(2,1)S(1)} %bitcast.150, ...), kind=kOutput, calls=%fused_computation.75 | convolution fusion | flops 542898176 | bytes 3948544 | tf_op jit(solution)/shard_map/hqk,khd->qhd/dot_general | solution.py:202
  172.2 2.8 %fusion.34 = bf16[512,4,128]{0,2,1:T(8,128)(2,1)S(1)} fusion(bf16[512,4,128]{0,2,1:T(8,128)(2,1)S(1)} %bitcast.154, f32[4,512,512]{1,2,0:T(8,128)} %get-tuple-element.33, f32[4,512]{1,0:T(4,128)S(1)} %get-tuple-element.32, f32[512,4,128]{0,2,1:T(8,128)S(1)} %get-tuple-element.35, f32[512,4]{0,1:T(4,128)S(1)} %add_rsqrt_fusion, f32[512,4]{0,1:T(4,128)S(1)} %fusion.68), kind=kOutput, calls=%fused_computation.50 | convolution fusion | flops 271581184 | bytes 6316032 | tf_op jit(solution)/shard_map/hqk,khd->qhd/dot_general | solution.py:199
  175.0 0.7 fusion.115
  175.8 1.1 constant_dynamic-slice_fusion.1
  177.5 2.6 %collective-permute-done.13 = f32[256,1024]{1,0:T(8,128)} collective-permute-done((f32[256,1024]{1,0:T(8,128)}, f32[256,1024]{1,0:T(8,128)}, u32[]{:S(2)}, u32[]{:S(2)}) %collective-permute-start.13) | collective-permute-done | bytes 1048608 | tf_op jit(solution)/shard_map/ppermute | solution.py:23
  180.1 1.5 fusion.41
  181.8 0.7 collective-permute-start.14
  182.5 1.5 collective-permute-done.14
  184.4 5.8 %fusion.3 = f32[2,512,1408]{2,1,0:T(8,128)S(1)} fusion(bf16[3,1024,1408]{2,1,0:T(8,128)(2,1)} %param.27, bf16[256,1024]{1,0:T(8,128)(2,1)S(1)} %get-tuple-element.17, bf16[256,1024]{1,0:T(8,128)(2,1)S(1)} %get-tuple-element.16), kind=kOutput, calls=%fused_computation.8 | convolution fusion | flops 2954887168 | bytes 12582912 | tf_op jit(solution)/shard_map/td,kdf->ktf/dot_general | solution.py:216
  190.2 3.8 %fusion.10 = f32[512,1024]{1,0:T(8,128)S(1)} fusion(bf16[3,1024,1408]{2,1,0:T(8,128)(2,1)} %param.27, f32[2,512,1408]{2,1,0:T(8,128)S(1)} %fusion.3), kind=kOutput, calls=%fused_computation.21 | convolution fusion | flops 1480720384 | bytes 10747904 | tf_op jit(solution)/shard_map/tf,df->td/dot_general | solution.py:220
  194.6 2.3 %collective-permute-done.15 = f32[256,1024]{1,0:T(8,128)S(1)} collective-permute-done((f32[256,1024]{1,0:T(8,128)S(1)}, f32[256,1024]{1,0:T(8,128)S(1)}, u32[]{:S(2)}, u32[]{:S(2)}) %collective-permute-start.15) | collective-permute-done | bytes 1048608 | tf_op jit(solution)/shard_map/ppermute | solution.py:23
  196.8 1.1 fusion.44
  (132 shorter events, 13.4 us)
Async XLA Ops:
  6.5 64.9 %copy-start = (bf16[3,1024,512]{2,1,0:T(8,128)(2,1)S(1)}, bf16[3,1024,512]{2,1,0:T(8,128)(2,1)}, u32[]{:S(2)}) copy-start(bf16[3,1024,512]{2,1,0:T(8,128)(2,1)} %param.17) | copy-start | bytes 9437188
  6.5 23.6 %copy-start.17 = (f32[2,1024]{1,0:T(2,128)S(1)}, f32[2,1024]{1,0:T(2,128)}, u32[]{:S(2)}) copy-start(f32[2,1024]{1,0:T(2,128)} %param.16) | copy-start | bytes 24580
  6.5 26.9 %copy-start.18 = (s32[1,6]{1,0:T(1,128)S(1)}, s32[1,6]{1,0:T(1,128)}, u32[]{:S(2)}) copy-start(s32[1,6]{1,0:T(1,128)} %param.23) | copy-start | bytes 76
  6.5 112.0 %all-gather.2.cloned.1.call-start = ((), (), s32[]{:S(2)}) async-start(), calls=%async_computation.1 | async-start | bytes 4456448 | tf_op jit(solution)/shard_map/all_gather | solution.py:111
  10.8 154.7 %reduce-scatter.2.cloned.1.call-start = ((), (), s32[]{:S(2)}) async-start(), calls=%async_computation.2 | async-start | bytes 3932160 | tf_op jit(solution)/shard_map/reduce_scatter | solution.py:174
  10.8 35.6 %collective-permute-start.6 = (bf16[4,2,128,128]{3,2,1,0:T(8,128)(2,1)}, bf16[4,2,128,128]{3,2,1,0:T(8,128)(2,1)}, u32[]{:S(2)}, u32[]{:S(2)}) collective-permute-start(bf16[4,2,128,128]{3,2,1,0:T(8,128)(2,1)} %get-tuple-element.21), channel_id=1, source_target_pairs={{0,8},{8,16},{16,24},{24,0},{1,9},{9,17},{17,25},{25,1},{2,10},{10... | collective-permute-start | bytes 786440 | tf_op jit(solution)/shard_map/ppermute | solution.py:72
  13.0 35.0 %collective-permute-start.5 = (bf16[4,2,128,128]{3,2,1,0:T(8,128)(2,1)}, bf16[4,2,128,128]{3,2,1,0:T(8,128)(2,1)}, u32[]{:S(2)}, u32[]{:S(2)}) collective-permute-start(bf16[4,2,128,128]{3,2,1,0:T(8,128)(2,1)} %get-tuple-element.21), channel_id=1, source_target_pairs={{0,24},{8,0},{16,8},{24,16},{1,25},{9,1},{17,9},{25,17},{2,26},{10... | collective-permute-start | bytes 786440 | tf_op jit(solution)/shard_map/ppermute | solution.py:72
  14.6 23.4 %collective-permute-start.2 = (s32[6]{0:T(128)}, s32[6]{0:T(128)}, u32[]{:S(2)}, u32[]{:S(2)}) collective-permute-start(s32[6]{0:T(128)} %bitcast.170), channel_id=1, source_target_pairs={{0,32},{32,64},{64,96},{96,0},{1,33},{33,65},{65,97},{97,1},{2,34}... | collective-permute-start | bytes 80 | tf_op jit(solution)/shard_map/ppermute | solution.py:157
  16.2 23.8 %collective-permute-start.3 = (s32[6]{0:T(128)}, s32[6]{0:T(128)}, u32[]{:S(2)}, u32[]{:S(2)}) collective-permute-start(s32[6]{0:T(128)} %bitcast.171), channel_id=1, source_target_pairs={{0,64},{32,96},{64,0},{96,32},{1,65},{33,97},{65,1},{97,33},{2,66}... | collective-permute-start | bytes 80 | tf_op jit(solution)/shard_map/ppermute | solution.py:157
  19.5 20.6 %collective-permute-start.4 = (s32[6]{0:T(128)}, s32[6]{0:T(128)}, u32[]{:S(2)}, u32[]{:S(2)}) collective-permute-start(s32[6]{0:T(128)} %bitcast.172), channel_id=1, source_target_pairs={{0,96},{32,0},{64,32},{96,64},{1,97},{33,1},{65,33},{97,65},{2,98}... | collective-permute-start | bytes 80 | tf_op jit(solution)/shard_map/ppermute | solution.py:157
  26.0 14.0 %copy-start.25 = (s32[6,1]{0,1:T(1,128)}, s32[6,1]{0,1:T(1,128)S(1)}, u32[]{:S(2)}) copy-start(s32[6,1]{0,1:T(1,128)S(1)} %reduce-window.14) | copy-start | bytes 76
  26.0 9.9 %copy-start.4 = (bf16[32,1024,16]{1,2,0:T(8,128)(2,1)S(1)}, bf16[32,1024,16]{1,2,0:T(8,128)(2,1)}, u32[]{:S(2)}) copy-start(bf16[32,1024,16]{1,2,0:T(8,128)(2,1)} %param.20) | copy-start | bytes 3145732
  30.1 3.3 %copy-start.27 = (s32[6]{0:T(128)}, s32[6]{0:T(128)S(1)}, u32[]{:S(2)}) copy-start(s32[6]{0:T(128)S(1)} %bitcast_subtract_fusion.2) | copy-start | bytes 76
  38.0 36.5 %collective-permute-start.1 = (bf16[32,1024,16]{1,0,2:T(8,128)(2,1)}, bf16[32,1024,16]{1,0,2:T(8,128)(2,1)}, u32[]{:S(2)}, u32[]{:S(2)}) collective-permute-start(bf16[32,1024,16]{1,0,2:T(8,128)(2,1)} %copy.51), channel_id=1, source_target_pairs={{0,1},{1,0},{2,3},{3,2},{4,5},{5,4},{6,7},{7,6},{8,9},{9,8},{10,11... | collective-permute-start | bytes 3145736 | tf_op jit(solution)/shard_map/ppermute | solution.py:23
  40.0 30.0 %collective-permute-start = (bf16[256,1024]{1,0:T(8,128)(2,1)}, bf16[256,1024]{1,0:T(8,128)(2,1)}, u32[]{:S(2)}, u32[]{:S(2)}) collective-permute-start(bf16[256,1024]{1,0:T(8,128)(2,1)} %fusion.39), channel_id=1, source_target_pairs={{0,1},{1,0},{2,3},{3,2},{4,5},{5,4},{6,7},{7,6},{8,9},{9,8},{10,11... | collective-permute-start | bytes 1572872 | tf_op jit(solution)/shard_map/ppermute | solution.py:23
  48.0 9.5 %collective-permute-start.7 = (bf16[2,2,128,128]{3,2,1,0:T(8,128)(2,1)}, bf16[2,2,128,128]{3,2,1,0:T(8,128)(2,1)}, u32[]{:S(2)}, u32[]{:S(2)}) collective-permute-start(bf16[2,2,128,128]{3,2,1,0:T(8,128)(2,1)} %slice.96), channel_id=1, source_target_pairs={{0,8},{8,16},{16,24},{24,0},{1,9},{9,17},{17,25},{25,1},{2,10},{10... | collective-permute-start | bytes 393224 | tf_op jit(solution)/shard_map/ppermute | solution.py:72
  49.6 8.5 %collective-permute-start.8 = (bf16[2,2,128,128]{3,2,1,0:T(8,128)(2,1)}, bf16[2,2,128,128]{3,2,1,0:T(8,128)(2,1)}, u32[]{:S(2)}, u32[]{:S(2)}) collective-permute-start(bf16[2,2,128,128]{3,2,1,0:T(8,128)(2,1)} %slice.97), channel_id=1, source_target_pairs={{0,24},{8,0},{16,8},{24,16},{1,25},{9,1},{17,9},{25,17},{2,26},{10... | collective-permute-start | bytes 393224 | tf_op jit(solution)/shard_map/ppermute | solution.py:72
  59.1 9.5 %copy-start.20 = (pred[4]{0:T(512)(128)(4,1)S(1)}, pred[4]{0:T(512)(128)(4,1)}, u32[]{:S(2)}) copy-start(pred[4]{0:T(512)(128)(4,1)} %get-tuple-element.36) | copy-start | bytes 16
  64.4 5.6 %copy-start.2 = (bf16[256,1024]{1,0:T(8,128)(2,1)S(1)}, bf16[256,1024]{1,0:T(8,128)(2,1)}, u32[]{:S(2)}) copy-start(bf16[256,1024]{1,0:T(8,128)(2,1)} %param.15) | copy-start | bytes 1572868
  65.8 24.6 %collective-permute-start.10 = (bf16[4,4,2,128,128]{4,3,2,1,0:T(8,128)(2,1)S(1)}, bf16[4,4,2,128,128]{4,3,2,1,0:T(8,128)(2,1)S(1)}, u32[]{:S(2)}, u32[]{:S(2)}) collective-permute-start(bf16[4,4,2,128,128]{4,3,2,1,0:T(8,128)(2,1)S(1)} %broadcast_select_fusion), channel_id=1, source_target_pairs={{0,2},{2,4},{4,6},{6,0},{1,3},{3,5},{5,7},{7,1},{8,10},{10,12},{12... | collective-permute-start | bytes 3145736 | tf_op jit(solution)/shard_map/ppermute | solution.py:72
  67.3 23.6 %collective-permute-start.9 = (bf16[4,4,2,128,128]{4,3,2,1,0:T(8,128)(2,1)S(1)}, bf16[4,4,2,128,128]{4,3,2,1,0:T(8,128)(2,1)S(1)}, u32[]{:S(2)}, u32[]{:S(2)}) collective-permute-start(bf16[4,4,2,128,128]{4,3,2,1,0:T(8,128)(2,1)S(1)} %broadcast_select_fusion), channel_id=1, source_target_pairs={{0,6},{2,0},{4,2},{6,4},{1,7},{3,1},{5,3},{7,5},{8,14},{10,8},{12,... | collective-permute-start | bytes 3145736 | tf_op jit(solution)/shard_map/ppermute | solution.py:72
  71.4 22.2 %copy-start.9 = (bf16[256,1024]{1,0:T(8,128)(2,1)}, bf16[256,1024]{1,0:T(8,128)(2,1)S(1)}, u32[]{:S(2)}) copy-start(bf16[256,1024]{1,0:T(8,128)(2,1)S(1)} %get-tuple-element.18) | copy-start | bytes 1572868
  71.4 22.2 %copy-start.11 = (bf16[256,1024]{1,0:T(8,128)(2,1)}, bf16[256,1024]{1,0:T(8,128)(2,1)S(1)}, u32[]{:S(2)}) copy-start(bf16[256,1024]{1,0:T(8,128)(2,1)S(1)} %get-tuple-element.19) | copy-start | bytes 1572868
  71.4 3.1 %copy-start.6 = (f32[6,1024,16]{1,0,2:T(8,128)S(1)}, f32[6,1024,16]{1,0,2:T(8,128)}, u32[]{:S(2)}) copy-start(f32[6,1024,16]{1,0,2:T(8,128)} %fusion.74) | copy-start | bytes 1179652
  71.4 3.1 %copy-start.19 = (s32[1,6]{1,0:T(1,128)S(1)}, s32[1,6]{1,0:T(1,128)}, u32[]{:S(2)}) copy-start(s32[1,6]{1,0:T(1,128)} %param.23) | copy-start | bytes 76
  71.4 3.0 %copy-start.29 = (s32[32]{0:T(128)S(1)}, s32[32]{0:T(128)}, u32[]{:S(2)}) copy-start(s32[32]{0:T(128)} %iota_add_fusion) | copy-start | bytes 388
  74.4 19.6 %copy-start.13 = (f32[512,6]{0,1:T(8,128)S(1)}, f32[512,6]{0,1:T(8,128)}, u32[]{:S(2)}) copy-start(f32[512,6]{0,1:T(8,128)} %get-tuple-element.25) | copy-start | bytes 36868
  74.4 19.6 %copy-start.15 = (bf16[512,6]{0,1:T(8,128)(2,1)S(1)}, bf16[512,6]{0,1:T(8,128)(2,1)}, u32[]{:S(2)}) copy-start(bf16[512,6]{0,1:T(8,128)(2,1)} %get-tuple-element.26) | copy-start | bytes 18436
  90.5 12.4 %collective-permute-start.11 = (bf16[2,4,2,128,128]{4,3,2,1,0:T(8,128)(2,1)S(1)}, bf16[2,4,2,128,128]{4,3,2,1,0:T(8,128)(2,1)S(1)}, u32[]{:S(2)}, u32[]{:S(2)}) collective-permute-start(bf16[2,4,2,128,128]{4,3,2,1,0:T(8,128)(2,1)S(1)} %slice.98), channel_id=1, source_target_pairs={{0,2},{2,4},{4,6},{6,0},{1,3},{3,5},{5,7},{7,1},{8,10},{10,12},{12... | collective-permute-start | bytes 1572872 | tf_op jit(solution)/shard_map/ppermute | solution.py:72
  90.9 12.1 %collective-permute-start.12 = (bf16[2,4,2,128,128]{4,3,2,1,0:T(8,128)(2,1)S(1)}, bf16[2,4,2,128,128]{4,3,2,1,0:T(8,128)(2,1)S(1)}, u32[]{:S(2)}, u32[]{:S(2)}) collective-permute-start(bf16[2,4,2,128,128]{4,3,2,1,0:T(8,128)(2,1)S(1)} %slice.99), channel_id=1, source_target_pairs={{0,6},{2,0},{4,2},{6,4},{1,7},{3,1},{5,3},{7,5},{8,14},{10,8},{12,... | collective-permute-start | bytes 1572872 | tf_op jit(solution)/shard_map/ppermute | solution.py:72
  105.3 5.4 %copy-start.21 = (pred[64]{0:T(512)(128)(4,1)S(1)}, pred[64]{0:T(512)(128)(4,1)}, u32[]{:S(2)}) copy-start(pred[64]{0:T(512)(128)(4,1)} %broadcast_in_dim.63) | copy-start | bytes 196
  115.3 6.4 %copy-start.22 = (pred[24]{0:T(512)(128)(4,1)S(1)}, pred[24]{0:T(512)(128)(4,1)}, u32[]{:S(2)}) copy-start(pred[24]{0:T(512)(128)(4,1)} %get-tuple-element.12) | copy-start | bytes 76
  115.3 6.4 %copy-start.23 = (pred[24]{0:T(512)(128)(4,1)S(1)}, pred[24]{0:T(512)(128)(4,1)}, u32[]{:S(2)}) copy-start(pred[24]{0:T(512)(128)(4,1)} %get-tuple-element.29) | copy-start | bytes 76
  115.3 6.4 %copy-start.30 = (bf16[24]{0:T(256)(128)(2,1)S(1)}, bf16[24]{0:T(256)(128)(2,1)}, u32[]{:S(2)}) copy-start(bf16[24]{0:T(256)(128)(2,1)} %reshape.534) | copy-start | bytes 148
  124.5 0.6 copy-start.26
  124.5 0.7 copy-start.28
  124.5 1.0 copy-start.10
  124.5 1.2 copy-start.12
  124.5 1.2 copy-start.31
  124.5 1.6 copy-start.24
  124.6 3.6 %copy-start.8 = (bf16[3,512,512]{1,2,0:T(8,128)(2,1)S(1)}, bf16[3,512,512]{1,2,0:T(8,128)(2,1)}, u32[]{:S(2)}) copy-start(bf16[3,512,512]{1,2,0:T(8,128)(2,1)} %get-tuple-element.30) | copy-start | bytes 4718596
  124.6 3.7 %copy-start.5 = (bf16[512,512]{0,1:T(8,128)(2,1)S(1)}, bf16[512,512]{0,1:T(8,128)(2,1)}, u32[]{:S(2)}) copy-start(bf16[512,512]{0,1:T(8,128)(2,1)} %fusion.35) | copy-start | bytes 1572868
  128.6 36.9 %copy-start.16 = (bf16[512,6]{0,1:T(8,128)(2,1)S(1)}, bf16[512,6]{0,1:T(8,128)(2,1)}, u32[]{:S(2)}) copy-start(bf16[512,6]{0,1:T(8,128)(2,1)} %get-tuple-element.26) | copy-start | bytes 18436
  172.2 2.8 %copy-start.7 = (bf16[512,1024]{1,0:T(8,128)(2,1)S(1)}, bf16[512,1024]{1,0:T(8,128)(2,1)}, u32[]{:S(2)}) copy-start(bf16[512,1024]{1,0:T(8,128)(2,1)} %param.26) | copy-start | bytes 3145732
  175.0 5.1 %copy-start.3 = (bf16[256,1024]{1,0:T(8,128)(2,1)S(1)}, bf16[256,1024]{1,0:T(8,128)(2,1)}, u32[]{:S(2)}) copy-start(bf16[256,1024]{1,0:T(8,128)(2,1)} %param.15) | copy-start | bytes 1572868
  175.7 5.9 %copy-start.14 = (f32[1,1024]{1,0:T(1,128)S(1)}, f32[1,1024]{1,0:T(1,128)}, u32[]{:S(2)}) copy-start(f32[1,1024]{1,0:T(1,128)} %get-tuple-element.23) | copy-start | bytes 12292
  176.9 3.3 %collective-permute-start.13 = (f32[256,1024]{1,0:T(8,128)}, f32[256,1024]{1,0:T(8,128)}, u32[]{:S(2)}, u32[]{:S(2)}) collective-permute-start(f32[256,1024]{1,0:T(8,128)} %constant_dynamic-slice_fusion.1), channel_id=1, source_target_pairs={{0,1},{1,0},{2,3},{3,2},{4,5},{5,4},{6,7},{7,6},{8,9},{9,8},{10,11... | collective-permute-start | bytes 3145736 | tf_op jit(solution)/shard_map/ppermute | solution.py:23
  181.8 2.2 %collective-permute-start.14 = (bf16[256,1024]{1,0:T(8,128)(2,1)S(1)}, bf16[256,1024]{1,0:T(8,128)(2,1)S(1)}, u32[]{:S(2)}, u32[]{:S(2)}) collective-permute-start(bf16[256,1024]{1,0:T(8,128)(2,1)S(1)} %fusion.43), channel_id=1, source_target_pairs={{0,1},{1,0},{2,3},{3,2},{4,5},{5,4},{6,7},{7,6},{8,9},{9,8},{10,11... | collective-permute-start | bytes 1572872 | tf_op jit(solution)/shard_map/ppermute | solution.py:23
  190.2 7.7 %copy-start.1 = (bf16[3,1024,512]{2,1,0:T(8,128)(2,1)S(1)}, bf16[3,1024,512]{2,1,0:T(8,128)(2,1)}, u32[]{:S(2)}) copy-start(bf16[3,1024,512]{2,1,0:T(8,128)(2,1)} %param.17) | copy-start | bytes 9437188
  194.1 2.7 %collective-permute-start.15 = (f32[256,1024]{1,0:T(8,128)S(1)}, f32[256,1024]{1,0:T(8,128)S(1)}, u32[]{:S(2)}, u32[]{:S(2)}) collective-permute-start(f32[256,1024]{1,0:T(8,128)S(1)} %constant_dynamic-slice_fusion), channel_id=1, source_target_pairs={{0,1},{1,0},{2,3},{3,2},{4,5},{5,4},{6,7},{7,6},{8,9},{9,8},{10,11... | collective-permute-start | bytes 3145736 | tf_op jit(solution)/shard_map/ppermute | solution.py:23
Sparse Core Ops, SparseCore 0:
  10.9 57.4 all-gather.1
  124.7 40.7 reduce-scatter.1

commit v4 on v0

--- a/solution.py
+++ b/solution.py
@@ -89,10 +89,9 @@
     group_lengths = lengths[0].reshape(-1)
     scale = 1.0 / math.sqrt(head_size)
 
-    ff_other = swap(feedforward_weight)
     down_other = swap(adapter_down_factor)
 
-    plane = lax.all_gather(caches, ("y", "x"), axis=0, tiled=True)
+    plane = lax.all_gather(jnp.swapaxes(caches, -1, -2), ("y", "x"), axis=0, tiled=True)
     per_plane = plane.shape[0]
 
     normalized_rows = rms_scale(tokens, norm_gain_pair[0])
@@ -143,7 +142,9 @@
     line_rows = jnp.take(behind, (z_here - jnp.arange(z_count, dtype=jnp.int32)) % z_count, axis=0)
     local = line_rows - z_here * per_plane
     valid = ((local >= 0) & (local < per_plane)).astype(jnp.int32)
-    slots = pick_states(jnp.clip(local, 0, per_plane - 1).reshape(-1), valid.reshape(-1), plane, z_count)
+    picked = jnp.take(plane, jnp.clip(local, 0, per_plane - 1).reshape(-1), axis=0)
+    keep = valid.reshape(-1).astype(plane.dtype)[:, None, None, None]
+    slots = (picked * keep).reshape((z_count, -1) + plane.shape[1:])
     states = lax.psum_scatter(slots, "z", scatter_dimension=0, tiled=True)[0]
     keys = projected[1].astype(jnp.bfloat16).reshape(group, local_heads, head_size)
     values = projected[2].astype(jnp.bfloat16).reshape(group, local_heads, head_size)
@@ -159,7 +160,7 @@
     level = running - jnp.sum(member[:, :, None] * start_level[None, :, :], axis=1)
     masked_queries = queries[:, None, :, :] * member.astype(jnp.bfloat16)[:, :, None, None]
     from_state = jnp.einsum(
-        "tshi,shij->thj", masked_queries, states, preferred_element_type=jnp.float32
+        "tshi,shji->thj", masked_queries, states, preferred_element_type=jnp.float32
     )
     carried = from_state * jnp.exp(level)[:, :, None]
 
@@ -178,21 +179,29 @@
     combined = attended + mix_gate[:, :, None] * recalled * factor
     head_out = combined.astype(jnp.bfloat16).reshape(group, head_cols)
 
-    partial = jnp.dot(head_out, head_output_weight, preferred_element_type=jnp.float32)
-    own = lax.dynamic_slice_in_dim(partial, col * tok_rows, tok_rows, axis=0)
-    sent = lax.dynamic_slice_in_dim(partial, (1 - col) * tok_rows, tok_rows, axis=0)
-    attn_proj = own + swap(sent)
+    head_partner = lax.dynamic_slice_in_dim(head_out, (1 - col) * tok_rows, tok_rows, axis=0)
+    head_own = lax.dynamic_slice_in_dim(head_out, col * tok_rows, tok_rows, axis=0)
+    proj_partner = swap(jnp.dot(head_partner, head_output_weight, preferred_element_type=jnp.float32))
+    attn_proj = jnp.dot(head_own, head_output_weight, preferred_element_type=jnp.float32) + proj_partner
     mixed = (tokens.astype(jnp.float32) + attn_proj).astype(jnp.bfloat16)
     normed_two = rms_scale(mixed, norm_gain_pair[1])
 
-    def feed_half(weight):
+    def feed_part(rows):
         gate_up = jnp.einsum(
-            "td,kdf->ktf", normed_two, weight[:2], preferred_element_type=jnp.float32
+            "td,kdf->ktf", rows, feedforward_weight[:2], preferred_element_type=jnp.float32
         )
         hidden = (jax.nn.silu(gate_up[0]) * gate_up[1]).astype(jnp.bfloat16)
-        return jnp.einsum("tf,df->td", hidden, weight[2], preferred_element_type=jnp.float32)
-
-    feed = feed_half(feedforward_weight) + feed_half(ff_other)
+        return jnp.einsum(
+            "tf,df->td", hidden, feedforward_weight[2], preferred_element_type=jnp.float32
+        )
+
+    partner_two = swap(normed_two)
+    half = tok_rows // 2
+    for_partner = [
+        swap(feed_part(partner_two[:half])),
+        swap(feed_part(partner_two[half:])),
+    ]
+    feed = feed_part(normed_two) + jnp.concatenate(for_partner, axis=0)
     return (mixed.astype(jnp.float32) + feed).astype(jnp.bfloat16)
 
 

time: 189 us -> 174 us (0.921); the launches traced: 190 us -> 173 us
  waiting for transfers between devices: 93.3 us -> 73.5 us
  Pallas kernels: 17.9 us -> 0 us
  local copies, waits for them, and re-layouts: 7.35 us -> 17.9 us
  matrix products: 40 us -> 46.1 us
  other arithmetic: 9.03 us -> 11.8 us
    reduce_scatter x1, waiting for transfers between devices: 43 us -> 24.6 us  [on_device(): states = lax.psum_scatter(slots, 'z', scatter_dimension=0, tiled=True)[0]]
    pallas_call x1 -> x0, Pallas kernels: 17.9 us -> none  [pick_states(): pl.pallas_call(body, out_shape=jax.ShapeDtypeStruct((lines, per_line) + b...]
    gather x0 -> x1, local copies, waits for them, and re-layouts: none -> 6.19 us  [on_device(): jnp.take(plane, jnp.clip(local, 0, per_plane - 1).reshape(-1), axis=0)]
    mul x0 -> x1, other arithmetic: none -> 3.91 us  [on_device(): slots = (picked * keep).reshape((z_count, -1) + plane.shape[1:])]
    unnamed x32 -> x31, local copies, waits for them, and re-layouts: 2.85 us -> 5.43 us
    all_gather x1, waiting for transfers between devices: 47 us -> 44.6 us  [on_device(): lax.all_gather(jnp.swapaxes(caches, -1, -2), ('y', 'x'), axis=0, tiled=True)]
    slice x1, local copies, waits for them, and re-layouts: 0.07 us -> 2.28 us  [on_device(): projected[1].astype(jnp.bfloat16).reshape(group, local_heads, head_size)]
    ppermute x4 -> x6, waiting for transfers between devices: 2.64 us -> 4.25 us  [swap(): return lax.ppermute(value, 'col', perm=[(0, 1), (1, 0)])]
  transfers between devices with their start and end apart: 9 -> 11, of which waited for: 3 -> 5; matrix products, arithmetic and copies ran while one was open for 25% -> 22% of each run, Pallas kernels for 0% -> 0%
where the time goes in v4:
time: 174 us; the launch traced here: 173 us
  waiting for transfers between devices  73.5 us (42%)
  matrix products  46.1 us (26%)
  local copies, waits for them, and re-layouts  17.9 us (10%)
  between operations  13.7 us (8%)
  other arithmetic  11.8 us (7%)
  starting transfers between devices  9.9 us (6%)
    all_gather x1, waiting for transfers between devices, on_device(): lax.all_gather(jnp.swapaxes(caches, -1, -2), ('y', 'x'), axis=0, tiled=True)  44.6 us
    reduce_scatter x1, waiting for transfers between devices, on_device(): states = lax.psum_scatter(slots, 'z', scatter_dimension=0, tiled=True)[0]  24.6 us
    ppermute x3, starting transfers between devices, along_z(): lax.ppermute(value, 'z', perm=[(i, (i + d) % z_count) for i in range(z_co...  6.57 us
    dot_general x3, matrix products, feed_part(): jnp.einsum('td,kdf->ktf', rows, feedforward_weight[:2], preferred_element...  6.3 us
    dot_general x3, matrix products, feed_part(): jnp.einsum('tf,df->td', hidden, feedforward_weight[2], preferred_element_...  6.22 us
    gather x1, local copies, waits for them, and re-layouts, on_device(): jnp.take(plane, jnp.clip(local, 0, per_plane - 1).reshape(-1), axis=0)  6.19 us
    unnamed x31, local copies, waits for them, and re-layouts  5.43 us
    sub x1, matrix products, on_device(): weights = jnp.exp(masked - peak)  4.86 us
  transfers between devices with their start and end apart: 11, of which 5 were waited for; matrix products, arithmetic and copies ran while one was open for 22% of the time, Pallas kernels for 0%

profile of v4, /device:TPU:1, one launch (start us, length us, event | category | flops | bytes accessed | tf_op | source)
XLA Modules:
  0.0 172.9 jit_solution(7628561367293123131)
XLA Ops:
  6.5 2.2 %copy.50 = bf16[4,4,128,128]{2,3,1,0:T(8,128)(2,1)} copy(bf16[4,4,128,128]{3,2,1,0:T(8,128)(2,1)} %param.23) | data formatting | bytes 1048576 | tf_op args[10]
  8.8 0.0 reduce-scatter.2.cloned.1.call-start
  8.9 2.5 %collective-permute-start.2 = (s32[6]{0:T(128)}, s32[6]{0:T(128)S(1)}, u32[]{:S(2)}, u32[]{:S(2)}) collective-permute-start(s32[6]{0:T(128)} %bitcast.178), channel_id=1, source_target_pairs={{0,32},{32,64},{64,96},{96,0},{1,33},{33,65},{65,97},{97,1},{2,34}... | collective-permute-start | bytes 80 | tf_op jit(solution)/shard_map/ppermute | solution.py:139
  11.4 3.3 %collective-permute-start.3 = (s32[6]{0:T(128)}, s32[6]{0:T(128)S(1)}, u32[]{:S(2)}, u32[]{:S(2)}) collective-permute-start(s32[6]{0:T(128)} %bitcast.179), channel_id=1, source_target_pairs={{0,64},{32,96},{64,0},{96,32},{1,65},{33,97},{65,1},{97,33},{2,66}... | collective-permute-start | bytes 80 | tf_op jit(solution)/shard_map/ppermute | solution.py:139
  14.7 0.7 collective-permute-start.4
  15.4 1.2 fusion.53
  16.7 0.8 fusion.133
  17.4 2.0 %fusion.55 = bf16[256,1024]{1,0:T(8,128)(2,1)} fusion(bf16[256,1024]{1,0:T(8,128)(2,1)} %param.13, f32[1024]{0:T(1024)S(1)} %bitcast.168, f32[256]{0:T(256)S(1)} %add_rsqrt_fusion.2), kind=kLoop, calls=%fused_computation.65 | loop fusion | flops 1048576 | bytes 1053696 | tf_op jit(solution)/shard_map/convert_element_type | solution.py:19
  19.5 1.5 collective-permute-start
  21.0 2.8 %copy.51 = bf16[32,1024,16]{1,0,2:T(8,128)(2,1)} copy(bf16[32,1024,16]{1,2,0:T(8,128)(2,1)} %param.18) | data formatting | bytes 2097152 | tf_op args[5]
  23.8 0.1 reshape.440
  23.9 0.1 reshape_squeeze.3
  24.0 0.2 reduce-window.14
  24.2 0.1 fusion.89
  24.3 2.4 %convolution_convert_fusion = bf16[6,16,512]{2,0,1:T(8,128)(2,1)S(1)} fusion(bf16[64,16,512]{2,1,0:T(8,128)(2,1)} %param.19, s32[6]{0:T(128)S(1)} %bitcast.173), kind=kOutput, calls=%fused_computation.61 | convolution fusion | flops 6340992 | bytes 1146904 | tf_op jit(solution)/shard_map/gq,qjl->gjl/dot_general | solution.py:126
  26.7 3.2 %fusion.103 = f32[6,1024,16]{1,0,2:T(8,128)} fusion(s32[32]{0:T(128)S(1)} %iota_add_fusion.1, s32[6]{0:T(128)S(1)} %bitcast.174, bf16[32,1024,16]{1,2,0:T(8,128)(2,1)} %param.18), kind=kOutput, calls=%fused_computation.136 | convolution fusion | flops 6291648 | bytes 1441944 | tf_op jit(solution)/shard_map/sa,adr->sdr/dot_general | solution.py:116
  30.0 0.6 gather_fusion
  30.6 0.1 compare_and_fusion
  30.7 0.1 min.12
  30.8 1.5 broadcast_select_fusion.1
  32.4 3.0 %fusion.134 = (bf16[3,512,512]{1,2,0:T(8,128)(2,1)}, f32[3,512,512]{1,2,0:T(8,128)S(1)}) fusion(bf16[3,1024,512]{2,1,0:T(8,128)(2,1)S(1)} %copy-done, bf16[256,1024]{1,0:T(8,128)(2,1)S(1)} %get-tuple-element.14, bf16[256,1024]{1,0:T(8,128)(2,1)S(1)} %get-tuple-element.13), kind=kOutput, calls=%fused_computation.185 | convolution fusion | flops 1613496320 | bytes 8912896 | tf_op jit(solution)/shard_map/td,kdc->ktc/dot_general | solution.py:106
  35.4 1.5 fusion.52
  36.9 0.1 copy.53
  37.1 0.5 fusion.80
  37.6 1.2 fusion.50
  38.8 44.6 %all-gather.2.cloned.1.call-done = bf16[64,4,128,128]{3,2,1,0:T(8,128)(2,1)} async-done(((bf16[4,4,128,128]{3,2,1,0:T(8,128)(2,1)}), bf16[64,4,128,128]{3,2,1,0:T(8,128)(2,1)}) %all-gather.2.cloned.1.call-update) | async-done | bytes 8388624 | tf_op jit(solution)/shard_map/all_gather | solution.py:94
  83.4 6.2 %gather_fusion.1 = bf16[24,4,128,128]{3,2,1,0:T(8,128)(2,1)} fusion(bf16[64,4,128,128]{3,2,1,0:T(8,128)(2,1)} %all-gather.2.cloned.1.call-done, s32[1024]{0:T(1024)S(1)} %pad_clamp_fusion), kind=kCustom, calls=%fused_computation.1 | custom fusion | bytes 6291552 | tf_op jit(solution)/shard_map/jit(_take)/gather | solution.py:145
  89.6 3.9 %fusion.11 = bf16[4,6,4,128,128]{4,3,1,2,0:T(8,128)(2,1)} fusion(bf16[4,6,4,128,128]{4,3,2,1,0:T(8,128)(2,1)} %bitcast.155, pred[4,6]{1,0:T(4,128)(4,1)S(1)} %get-tuple-element.9, bf16[4,6]{1,0:T(4,128)(2,1)S(1)} %get-tuple-element.17), kind=kLoop, calls=%fused_computation.16 | loop fusion | flops 3145728 | bytes 6291528 | tf_op jit(solution)/shard_map/mul | solution.py:147
  93.5 0.1 convert_reduce_fusion
  93.6 0.1 fusion.90
  93.7 0.2 fusion.63
  93.9 0.3 copy-done.9
  94.2 1.6 convolution_bitcast_fusion.2
  95.8 0.1 fusion.129
  95.9 1.4 reduce-window.18
  97.3 0.2 slice_reduce_fusion
  97.4 0.2 reduce-window.19
  97.6 0.1 add_bitcast_fusion
  97.7 0.1 bitcast_subtract_fusion.1
  97.8 0.1 multiply_reduce_fusion.3
  97.9 0.1 multiply_reduce_fusion.2
  98.0 2.3 %fusion.132 = (bf16[1,512,512]{1,2,0:T(8,128)(2,1)}, bf16[1,512,512]{1,2,0:T(8,128)(2,1)}) fusion(bf16[3,512,512]{1,2,0:T(8,128)(2,1)} %get-tuple-element.20), kind=kLoop, calls=%fused_computation.183 | loop fusion | bytes 2097152 | tf_op jit(solution)/shard_map/slice | solution.py:149
  100.3 2.1 %copy.61 = bf16[512,4,128]{2,0,1:T(8,128)(2,1)} copy(bf16[512,4,128]{0,2,1:T(8,128)(2,1)} %bitcast.156) | data formatting | bytes 1048576 | tf_op jit(solution)/shard_map/optimization_barrier | solution.py:132
  102.4 4.9 %fusion.135 = (f32[4,512]{1,0:T(4,128)S(1)}, f32[4,512,512]{1,2,0:T(8,128)}) fusion(pred[512,512]{0,1:T(8,128)(4,1)S(1)} %fusion.63, bf16[512,4,128]{0,2,1:T(8,128)(2,1)} %bitcast.157, bf16[512,4,128]{0,2,1:T(8,128)(2,1)} %bitcast.164), kind=kOutput, calls=%fused_computation.186 | convolution fusion | flops 272630272 | bytes 5513216 | tf_op jit(solution)/shard_map/sub | solution.py:171
  107.2 24.6 %reduce-scatter.2.cloned.1.call-done = bf16[1,6,4,128,128]{4,3,1,2,0:T(8,128)(2,1)} async-done(((bf16[4,6,4,128,128]{4,3,1,2,0:T(8,128)(2,1)}), bf16[1,6,4,128,128]{4,3,1,2,0:T(8,128)(2,1)}) %reduce-scatter.2.cloned.1.call-update) | async-done | bytes 786448 | tf_op jit(solution)/shard_map/reduce_scatter | solution.py:148
  131.9 3.7 %fusion.46 = f32[512,4,128]{0,2,1:T(8,128)} fusion(bf16[512,6]{0,1:T(8,128)(2,1)S(1)} %get-tuple-element.19, bf16[512,4,128]{2,0,1:T(8,128)(2,1)} %copy.61, bf16[1,6,4,128,128]{4,3,1,2,0:T(8,128)(2,1)} %reduce-scatter.2.cloned.1.call-done, f32[512,4]{0,1:T(4,128)S(1)} %fusion.98), kind=kOutput, calls=%fused_computation.55 | convolution fusion | flops 404488192 | bytes 2373632 | tf_op jit(solution)/shard_map/tshi,shji->thj/dot_general | solution.py:162
  135.6 4.5 %multiply_reduce_fusion = (f32[512,4]{0,1:T(4,128)S(1)}, f32[512,4,128]{0,2,1:T(8,128)}) fusion(f32[512,4,128]{0,2,1:T(8,128)} %fusion.46, bf16[512,4,128]{0,2,1:T(8,128)(2,1)} %bitcast.162, f32[4,512]{1,0:T(4,128)S(1)} %bitcast.172, pred[512,512]{0,1:T(8,128)(4,1)S(1)} %fusion.63, bf16[512,4,128]{0,2,1:T(8,128)(2,1)} %bitcast.158, ...), kind=kOutput, calls=%fused_computation.76 | convolution fusion | flops 542898176 | bytes 3948544 | tf_op jit(solution)/shard_map/hqk,khd->qhd/dot_general | solution.py:176
  140.1 3.3 %fusion.49 = bf16[512,4,128]{0,2,1:T(8,128)(2,1)S(1)} fusion(bf16[512,4,128]{0,2,1:T(8,128)(2,1)} %bitcast.163, f32[4,512,512]{1,2,0:T(8,128)} %get-tuple-element.23, f32[4,512]{1,0:T(4,128)S(1)} %get-tuple-element.22, f32[512,4,128]{0,2,1:T(8,128)} %get-tuple-element.25, f32[512,4]{0,1:T(4,128)S(1)} %add_rsqrt_fusion, f32[512,4]{0,1:T(4,128)S(1)} %fusion.97), kind=kOutput, calls=%fused_computation.56 | convolution fusion | flops 271581184 | bytes 6316032 | tf_op jit(solution)/shard_map/hqk,khd->qhd/dot_general | solution.py:173
  143.4 1.5 fusion.81
  144.9 0.6 collective-permute-start.5
  145.5 2.6 %collective-permute-done.5 = f32[256,1024]{1,0:T(8,128)} collective-permute-done((f32[256,1024]{1,0:T(8,128)}, f32[256,1024]{1,0:T(8,128)}, u32[]{:S(2)}, u32[]{:S(2)}) %collective-permute-start.5) | collective-permute-done | bytes 1048608 | tf_op jit(solution)/shard_map/ppermute | solution.py:23
  148.1 2.3 %fusion.56 = (f32[256]{0:T(256)S(1)}, bf16[256,1024]{1,0:T(8,128)(2,1)S(1)}) fusion(f32[256,1024]{1,0:T(8,128)} %collective-permute-done.5, bf16[512,1024]{1,0:T(8,128)(2,1)} %param.24, bf16[512,512]{0,1:T(8,128)(2,1)} %bitcast.161, s32[]{:T(128)S(6)} %select_n.121, bf16[256,1024]{1,0:T(8,128)(2,1)} %param.13), kind=kOutput, calls=%fused_computation.66 | convolution fusion | flops 270270208 | bytes 3408900 | tf_op jit(solution)/shard_map/dot_general | solution.py:185
  150.5 0.2 fusion.58
  150.7 0.5 collective-permute-start.6
  151.2 1.5 collective-permute-done.6
  152.7 3.7 %fusion.20 = f32[2,128,1408]{2,1,0:T(8,128)S(1)} fusion(bf16[3,1024,1408]{2,1,0:T(8,128)(2,1)} %param.25, bf16[256,1024]{1,0:T(8,128)(2,1)S(1)} %collective-permute-done.6), kind=kOutput, calls=%fused_computation.25 | convolution fusion | flops 738197504 | bytes 7471104 | tf_op jit(solution)/shard_map/td,kdf->ktf/dot_general | solution.py:190
  156.4 3.3 %fusion.16 = f32[128,1024]{1,0:T(8,128)S(1)} fusion(bf16[3,1024,1408]{2,1,0:T(8,128)(2,1)} %param.25, f32[2,128,1408]{2,1,0:T(8,128)S(1)} %fusion.20), kind=kOutput, calls=%fused_computation.21 | convolution fusion | flops 370180096 | bytes 4849664 | tf_op jit(solution)/shard_map/tf,df->td/dot_general | solution.py:194
  159.8 0.5 collective-permute-start.7
  160.2 0.9 fusion.23
  161.2 1.1 fusion.14
  162.3 0.2 collective-permute-start.8
  162.5 1.7 fusion.7
  164.2 0.1 collective-permute-done.8
  164.2 1.8 %fusion.59 = bf16[256,1024]{1,0:T(8,128)(2,1)} fusion(bf16[256,1024]{1,0:T(8,128)(2,1)S(1)} %get-tuple-element.27, f32[128,1024]{1,0:T(8,128)S(1)} %collective-permute-done.8, f32[128,1024]{1,0:T(8,128)S(1)} %collective-permute-done.7, bf16[3,1024,1408]{2,1,0:T(8,128)(2,1)S(1)} %bitcast.154, f32[2,256,1408]{2,1,0:T(8,128)S(1)} %fusion.7), kind=kOutput, calls=%fused_computation.69 | convolution fusion | flops 741670912 | bytes 7864320 | tf_op jit(solution)/shard_map/tf,df->td/dot_general | solution.py:194
  (55 shorter events, 0.3 us)
Async XLA Ops:
  6.5 25.8 %copy-start = (bf16[3,1024,512]{2,1,0:T(8,128)(2,1)S(1)}, bf16[3,1024,512]{2,1,0:T(8,128)(2,1)}, u32[]{:S(2)}) copy-start(bf16[3,1024,512]{2,1,0:T(8,128)(2,1)} %param.15) | copy-start | bytes 9437188
  6.5 17.3 %copy-start.10 = (s32[1,2,3]{2,1,0:T(2,128)S(1)}, s32[1,2,3]{2,1,0:T(2,128)}, u32[]{:S(2)}) copy-start(s32[1,2,3]{2,1,0:T(2,128)} %param.20) | copy-start | bytes 76
  6.5 17.8 %copy-start.6 = (s32[1,6]{1,0:T(1,128)S(1)}, s32[1,6]{1,0:T(1,128)}, u32[]{:S(2)}) copy-start(s32[1,6]{1,0:T(1,128)} %param.21) | copy-start | bytes 76
  6.5 76.8 %all-gather.2.cloned.1.call-start = ((), (), s32[]{:S(2)}) async-start(), calls=%async_computation.1 | async-start | bytes 8912896 | tf_op jit(solution)/shard_map/all_gather | solution.py:94
  8.8 123.1 %reduce-scatter.2.cloned.1.call-start = ((), (), s32[]{:S(2)}) async-start(), calls=%async_computation.2 | async-start | bytes 3932160 | tf_op jit(solution)/shard_map/reduce_scatter | solution.py:148
  8.8 21.1 %copy-start.8 = (s32[1,6]{1,0:T(1,128)S(1)}, s32[1,6]{1,0:T(1,128)}, u32[]{:S(2)}) copy-start(s32[1,6]{1,0:T(1,128)} %param.22) | copy-start | bytes 76
  8.9 21.1 %collective-permute-start.2 = (s32[6]{0:T(128)}, s32[6]{0:T(128)S(1)}, u32[]{:S(2)}, u32[]{:S(2)}) collective-permute-start(s32[6]{0:T(128)} %bitcast.178), channel_id=1, source_target_pairs={{0,32},{32,64},{64,96},{96,0},{1,33},{33,65},{65,97},{97,1},{2,34}... | collective-permute-start | bytes 80 | tf_op jit(solution)/shard_map/ppermute | solution.py:139
  11.4 18.6 %collective-permute-start.3 = (s32[6]{0:T(128)}, s32[6]{0:T(128)S(1)}, u32[]{:S(2)}, u32[]{:S(2)}) collective-permute-start(s32[6]{0:T(128)} %bitcast.179), channel_id=1, source_target_pairs={{0,64},{32,96},{64,0},{96,32},{1,65},{33,97},{65,1},{97,33},{2,66}... | collective-permute-start | bytes 80 | tf_op jit(solution)/shard_map/ppermute | solution.py:139
  14.7 15.3 %collective-permute-start.4 = (s32[6]{0:T(128)}, s32[6]{0:T(128)S(1)}, u32[]{:S(2)}, u32[]{:S(2)}) collective-permute-start(s32[6]{0:T(128)} %bitcast.180), channel_id=1, source_target_pairs={{0,96},{32,0},{64,32},{96,64},{1,97},{33,1},{65,33},{97,65},{2,98}... | collective-permute-start | bytes 80 | tf_op jit(solution)/shard_map/ppermute | solution.py:139
  19.5 11.3 %collective-permute-start = (bf16[256,1024]{1,0:T(8,128)(2,1)}, bf16[256,1024]{1,0:T(8,128)(2,1)}, u32[]{:S(2)}, u32[]{:S(2)}) collective-permute-start(bf16[256,1024]{1,0:T(8,128)(2,1)} %fusion.55), channel_id=1, source_target_pairs={{0,1},{1,0},{2,3},{3,2},{4,5},{5,4},{6,7},{7,6},{8,9},{9,8},{10,11... | collective-permute-start | bytes 1572872 | tf_op jit(solution)/shard_map/ppermute | solution.py:23
  23.8 11.6 %collective-permute-start.1 = (bf16[32,1024,16]{1,0,2:T(8,128)(2,1)}, bf16[32,1024,16]{1,0,2:T(8,128)(2,1)}, u32[]{:S(2)}, u32[]{:S(2)}) collective-permute-start(bf16[32,1024,16]{1,0,2:T(8,128)(2,1)} %copy.51), channel_id=1, source_target_pairs={{0,1},{1,0},{2,3},{3,2},{4,5},{5,4},{6,7},{7,6},{8,9},{9,8},{10,11... | collective-permute-start | bytes 3145736 | tf_op jit(solution)/shard_map/ppermute | solution.py:23
  32.3 4.7 %copy-start.3 = (bf16[256,1024]{1,0:T(8,128)(2,1)}, bf16[256,1024]{1,0:T(8,128)(2,1)S(1)}, u32[]{:S(2)}) copy-start(bf16[256,1024]{1,0:T(8,128)(2,1)S(1)} %get-tuple-element.13) | copy-start | bytes 1572868
  32.3 4.7 %copy-start.4 = (bf16[256,1024]{1,0:T(8,128)(2,1)}, bf16[256,1024]{1,0:T(8,128)(2,1)S(1)}, u32[]{:S(2)}) copy-start(bf16[256,1024]{1,0:T(8,128)(2,1)S(1)} %get-tuple-element.14) | copy-start | bytes 1572868
  32.3 3.0 %copy-start.2 = (f32[6,1024,16]{1,0,2:T(8,128)S(1)}, f32[6,1024,16]{1,0,2:T(8,128)}, u32[]{:S(2)}) copy-start(f32[6,1024,16]{1,0,2:T(8,128)} %fusion.103) | copy-start | bytes 1179652
  93.5 0.7 copy-start.9
  93.5 2.3 %copy-start.7 = (f32[4]{0:T(128)S(1)}, f32[4]{0:T(128)}, u32[]{:S(2)}) copy-start(f32[4]{0:T(128)} %param.17) | copy-start | bytes 52
  140.1 3.3 %copy-start.1 = (bf16[512,1024]{1,0:T(8,128)(2,1)S(1)}, bf16[512,1024]{1,0:T(8,128)(2,1)}, u32[]{:S(2)}) copy-start(bf16[512,1024]{1,0:T(8,128)(2,1)} %param.24) | copy-start | bytes 3145732
  143.4 1.5 copy-start.5
  144.9 3.3 %collective-permute-start.5 = (f32[256,1024]{1,0:T(8,128)}, f32[256,1024]{1,0:T(8,128)}, u32[]{:S(2)}, u32[]{:S(2)}) collective-permute-start(f32[256,1024]{1,0:T(8,128)} %fusion.81), channel_id=1, source_target_pairs={{0,1},{1,0},{2,3},{3,2},{4,5},{5,4},{6,7},{7,6},{8,9},{9,8},{10,11... | collective-permute-start | bytes 3145736 | tf_op jit(solution)/shard_map/ppermute | solution.py:23
  150.7 2.0 %collective-permute-start.6 = (bf16[256,1024]{1,0:T(8,128)(2,1)S(1)}, bf16[256,1024]{1,0:T(8,128)(2,1)S(1)}, u32[]{:S(2)}, u32[]{:S(2)}) collective-permute-start(bf16[256,1024]{1,0:T(8,128)(2,1)S(1)} %fusion.58), channel_id=1, source_target_pairs={{0,1},{1,0},{2,3},{3,2},{4,5},{5,4},{6,7},{7,6},{8,9},{9,8},{10,11... | collective-permute-start | bytes 1572872 | tf_op jit(solution)/shard_map/ppermute | solution.py:23
  152.7 7.5 %slice-start = ((s8[8650752]{0:T(1024)(128)(4,1)}), s8[4194304]{0:T(1024)(128)(4,1)S(1)}, s32[]{:S(2)}) async-start(s8[8650752]{0:T(1024)(128)(4,1)} %bitcast.153), calls=%async_computation.3 | async-start | bytes 8388608
  152.7 7.5 %slice-start.1 = ((s8[8650752]{0:T(1024)(128)(4,1)}), s8[4194304]{0:T(1024)(128)(4,1)S(1)}, s32[]{:S(2)}) async-start(s8[8650752]{0:T(1024)(128)(4,1)} %bitcast.153), calls=%async_computation.4 | async-start | bytes 8388608
  156.4 3.8 %slice-start.2 = ((s8[8650752]{0:T(1024)(128)(4,1)}), s8[262144]{0:T(1024)(128)(4,1)S(1)}, s32[]{:S(2)}) async-start(s8[8650752]{0:T(1024)(128)(4,1)} %bitcast.153), calls=%async_computation.5 | async-start | bytes 524288
  159.8 4.4 %collective-permute-start.7 = (f32[128,1024]{1,0:T(8,128)S(1)}, f32[128,1024]{1,0:T(8,128)S(1)}, u32[]{:S(2)}, u32[]{:S(2)}) collective-permute-start(f32[128,1024]{1,0:T(8,128)S(1)} %fusion.16), channel_id=1, source_target_pairs={{0,1},{1,0},{2,3},{3,2},{4,5},{5,4},{6,7},{7,6},{8,9},{9,8},{10,11... | collective-permute-start | bytes 1572872 | tf_op jit(solution)/shard_map/ppermute | solution.py:23
  162.3 2.0 %collective-permute-start.8 = (f32[128,1024]{1,0:T(8,128)S(1)}, f32[128,1024]{1,0:T(8,128)S(1)}, u32[]{:S(2)}, u32[]{:S(2)}) collective-permute-start(f32[128,1024]{1,0:T(8,128)S(1)} %fusion.14), channel_id=1, source_target_pairs={{0,1},{1,0},{2,3},{3,2},{4,5},{5,4},{6,7},{7,6},{8,9},{9,8},{10,11... | collective-permute-start | bytes 1572872 | tf_op jit(solution)/shard_map/ppermute | solution.py:23
Sparse Core Ops, SparseCore 0:
  9.5 73.8 all-gather.1
  93.6 38.2 reduce-scatter.1

commit v5 on v2

--- a/solution.py
+++ b/solution.py
@@ -90,6 +90,7 @@
     scale = 1.0 / math.sqrt(head_size)
 
     down_other = swap(adapter_down_factor)
+    out_weight_other = swap(head_output_weight)
 
     plane = lax.all_gather(jnp.swapaxes(caches, -1, -2), ("y", "x"), axis=0, tiled=True)
     per_plane = plane.shape[0]
@@ -179,10 +180,11 @@
     combined = attended + mix_gate[:, :, None] * recalled * factor
     head_out = combined.astype(jnp.bfloat16).reshape(group, head_cols)
 
-    partial = jnp.dot(head_out, head_output_weight, preferred_element_type=jnp.float32)
-    own = lax.dynamic_slice_in_dim(partial, col * tok_rows, tok_rows, axis=0)
-    sent = lax.dynamic_slice_in_dim(partial, (1 - col) * tok_rows, tok_rows, axis=0)
-    attn_proj = own + swap(sent)
+    head_own = lax.dynamic_slice_in_dim(head_out, col * tok_rows, tok_rows, axis=0)
+    head_sent = lax.dynamic_slice_in_dim(head_out, (1 - col) * tok_rows, tok_rows, axis=0)
+    attn_proj = jnp.dot(head_own, head_output_weight, preferred_element_type=jnp.float32) + jnp.dot(
+        swap(head_sent), out_weight_other, preferred_element_type=jnp.float32
+    )
     mixed = (tokens.astype(jnp.float32) + attn_proj).astype(jnp.bfloat16)
     normed_two = rms_scale(mixed, norm_gain_pair[1])
 

time: 167 us -> 162 us (0.970)
  waiting for transfers between devices: 81.8 us -> 75.7 us
  other arithmetic: 12.8 us -> 11.1 us
    reduce_scatter x1, waiting for transfers between devices: 30.7 us -> 26.5 us  [on_device(): states = lax.psum_scatter(slots, 'z', scatter_dimension=0, tiled=True)[0]]
    dot_general x1, matrix products: 5.79 us -> 3.18 us  [on_device(): jnp.einsum('td,kdf->ktf', rows_two, feedforward_weight[:2], preferred_ele...]
    dot_general x1, matrix products: 3.83 us -> 1.83 us  [on_device(): jnp.einsum('tf,df->td', hidden, feedforward_weight[2], preferred_element_...]
    ppermute x5 -> x6, waiting for transfers between devices: 6.46 us -> 4.51 us  [swap(): return lax.ppermute(value, 'col', perm=[(0, 1), (1, 0)])]
    ppermute x5 -> x6, starting transfers between devices: 3.03 us -> 3.9 us  [swap(): return lax.ppermute(value, 'col', perm=[(0, 1), (1, 0)])]
    unnamed x35 -> x41, local copies, waits for them, and re-layouts: 5.86 us -> 6.28 us
  transfers between devices with their start and end apart: 10 -> 11, of which waited for: 5 -> 5; matrix products, arithmetic and copies ran while one was open for 17% -> 27% of each run, Pallas kernels for 0% -> 0%
where the time goes in v5:
time: 162 us; the launch traced here: 161 us
  waiting for transfers between devices  75.7 us (47%)
  matrix products  36.2 us (22%)
  local copies, waits for them, and re-layouts  14.1 us (9%)
  between operations  13.8 us (9%)
  other arithmetic  11.1 us (7%)
  starting transfers between devices  10.5 us (6%)
    all_gather x1, waiting for transfers between devices, on_device(): lax.all_gather(jnp.swapaxes(caches, -1, -2), ('y', 'x'), axis=0, tiled=True)  44.6 us
    reduce_scatter x1, waiting for transfers between devices, on_device(): states = lax.psum_scatter(slots, 'z', scatter_dimension=0, tiled=True)[0]  26.5 us
    ppermute x3, starting transfers between devices, along_z(): lax.ppermute(value, 'z', perm=[(i, (i + d) % z_count) for i in range(z_co...  6.57 us
    unnamed x41, local copies, waits for them, and re-layouts  6.28 us
    sub x1, matrix products, on_device(): weights = jnp.exp(masked - peak)  4.64 us
    gather x1, local copies, waits for them, and re-layouts, on_device(): jnp.take(plane, jnp.clip(local, 0, per_plane - 1).reshape(-1), axis=0)  4.53 us
    ppermute x6, waiting for transfers between devices, swap(): return lax.ppermute(value, 'col', perm=[(0, 1), (1, 0)])  4.51 us
    dot_general x1, matrix products, on_device(): jnp.einsum('hqk,khd->qhd', memory_w, values, preferred_element_type=jnp.f...  4.04 us
  transfers between devices with their start and end apart: 11, of which 5 were waited for; matrix products, arithmetic and copies ran while one was open for 27% of the time, Pallas kernels for 0%

profile of v5, /device:TPU:1, one launch (start us, length us, event | category | flops | bytes accessed | tf_op | source)
XLA Modules:
  0.0 161.4 jit_solution(13017941887375313044)
XLA Ops:
  6.5 2.2 %copy.50 = bf16[4,4,128,128]{2,3,1,0:T(8,128)(2,1)} copy(bf16[4,4,128,128]{3,2,1,0:T(8,128)(2,1)} %param.23) | data formatting | bytes 1048576 | tf_op args[10]
  8.8 0.0 reduce-scatter.2.cloned.1.call-start
  8.8 2.5 %collective-permute-start.2 = (s32[6]{0:T(128)}, s32[6]{0:T(128)S(1)}, u32[]{:S(2)}, u32[]{:S(2)}) collective-permute-start(s32[6]{0:T(128)} %bitcast.154), channel_id=1, source_target_pairs={{0,32},{32,64},{64,96},{96,0},{1,33},{33,65},{65,97},{97,1},{2,34}... | collective-permute-start | bytes 80 | tf_op jit(solution)/shard_map/ppermute | solution.py:140
  11.4 3.3 %collective-permute-start.3 = (s32[6]{0:T(128)}, s32[6]{0:T(128)S(1)}, u32[]{:S(2)}, u32[]{:S(2)}) collective-permute-start(s32[6]{0:T(128)} %bitcast.155), channel_id=1, source_target_pairs={{0,64},{32,96},{64,0},{96,32},{1,65},{33,97},{65,1},{97,33},{2,66}... | collective-permute-start | bytes 80 | tf_op jit(solution)/shard_map/ppermute | solution.py:140
  14.7 0.7 collective-permute-start.4
  15.4 1.2 fusion.39
  16.6 0.8 fusion.105
  17.4 2.0 %fusion.41 = bf16[256,1024]{1,0:T(8,128)(2,1)} fusion(bf16[256,1024]{1,0:T(8,128)(2,1)} %param.13, f32[1024]{0:T(1024)S(1)} %bitcast.145, f32[256]{0:T(256)S(1)} %add_rsqrt_fusion.2), kind=kLoop, calls=%fused_computation.54 | loop fusion | flops 1048576 | bytes 1053696 | tf_op jit(solution)/shard_map/convert_element_type | solution.py:19
  19.4 1.5 collective-permute-start
  21.0 2.8 %copy.51 = bf16[32,1024,16]{1,0,2:T(8,128)(2,1)} copy(bf16[32,1024,16]{1,2,0:T(8,128)(2,1)} %param.18) | data formatting | bytes 2097152 | tf_op args[5]
  23.8 0.1 reshape.438
  23.9 0.1 reshape_squeeze.3
  23.9 0.2 reduce-window.14
  24.2 0.1 fusion.63
  24.3 2.4 %convolution_convert_fusion = bf16[6,16,512]{2,0,1:T(8,128)(2,1)S(1)} fusion(bf16[64,16,512]{2,1,0:T(8,128)(2,1)} %param.19, s32[6]{0:T(128)S(1)} %bitcast.149), kind=kOutput, calls=%fused_computation.50 | convolution fusion | flops 6340992 | bytes 1146904 | tf_op jit(solution)/shard_map/gq,qjl->gjl/dot_general | solution.py:127
  26.7 3.2 %fusion.77 = f32[6,1024,16]{1,0,2:T(8,128)} fusion(s32[32]{0:T(128)S(1)} %iota_add_fusion.1, s32[6]{0:T(128)S(1)} %bitcast.150, bf16[32,1024,16]{1,2,0:T(8,128)(2,1)} %param.18), kind=kOutput, calls=%fused_computation.118 | convolution fusion | flops 6291648 | bytes 1441944 | tf_op jit(solution)/shard_map/sa,adr->sdr/dot_general | solution.py:117
  30.0 0.6 gather_fusion
  30.6 0.1 compare_and_fusion
  30.6 0.1 min.12
  30.7 1.5 broadcast_select_fusion.3
  32.3 3.1 %fusion.106 = (bf16[3,512,512]{1,2,0:T(8,128)(2,1)}, f32[3,512,512]{1,2,0:T(8,128)S(1)}) fusion(bf16[3,1024,512]{2,1,0:T(8,128)(2,1)S(1)} %copy-done, bf16[256,1024]{1,0:T(8,128)(2,1)S(1)} %get-tuple-element.16, bf16[256,1024]{1,0:T(8,128)(2,1)S(1)} %get-tuple-element.15), kind=kOutput, calls=%fused_computation.167 | convolution fusion | flops 1613496320 | bytes 8912896 | tf_op jit(solution)/shard_map/td,kdc->ktc/dot_general | solution.py:107
  35.4 1.5 fusion.38
  36.9 0.1 copy.53
  37.1 0.5 fusion.55
  37.6 1.1 fusion.36
  38.7 44.6 %all-gather.2.cloned.1.call-done = bf16[64,4,128,128]{3,2,1,0:T(8,128)(2,1)} async-done(((bf16[4,4,128,128]{3,2,1,0:T(8,128)(2,1)}), bf16[64,4,128,128]{3,2,1,0:T(8,128)(2,1)}) %all-gather.2.cloned.1.call-update) | async-done | bytes 8388624 | tf_op jit(solution)/shard_map/all_gather | solution.py:95
  83.4 4.5 %gather_fusion.1 = bf16[24,4,128,128]{3,2,1,0:T(8,128)(2,1)S(1)} fusion(bf16[64,4,128,128]{3,2,1,0:T(8,128)(2,1)} %all-gather.2.cloned.1.call-done, s32[1024]{0:T(1024)S(1)} %pad_clamp_fusion), kind=kCustom, calls=%fused_computation.1 | custom fusion | bytes 6291552 | tf_op jit(solution)/shard_map/jit(_take)/gather | solution.py:146
  87.9 2.0 %fusion.7 = bf16[4,6,4,128,128]{4,3,1,2,0:T(8,128)(2,1)} fusion(bf16[4,6,4,128,128]{4,3,2,1,0:T(8,128)(2,1)S(1)} %bitcast.130, pred[4,6]{1,0:T(4,128)(4,1)S(1)} %get-tuple-element.9, bf16[4,6]{1,0:T(4,128)(2,1)S(1)} %get-tuple-element.19), kind=kLoop, calls=%fused_computation.12 | loop fusion | flops 3145728 | bytes 6291528 | tf_op jit(solution)/shard_map/mul | solution.py:148
  90.0 0.0 reduce-scatter.2.cloned.1.call-update
  90.0 1.2 copy-done.5
  91.2 0.7 collective-permute-start.6
  91.8 0.1 convert_reduce_fusion
  91.9 0.1 fusion.64
  92.0 0.2 fusion.51
  92.2 1.6 convolution_bitcast_fusion.2
  93.8 0.1 fusion.101
  93.9 1.2 reduce-window.18
  95.1 0.2 slice_reduce_fusion
  95.3 0.2 reduce-window.19
  95.5 0.1 add_bitcast_fusion
  95.6 0.1 bitcast_subtract_fusion.1
  95.7 0.1 multiply_reduce_fusion.3
  95.8 0.1 multiply_reduce_fusion.2
  95.9 1.1 fusion.104
  97.0 0.3 copy.61
  97.2 4.6 %fusion.107 = (f32[4,512]{1,0:T(4,128)S(1)}, f32[4,512,512]{1,2,0:T(8,128)}) fusion(pred[512,512]{0,1:T(8,128)(4,1)S(1)} %fusion.51, bf16[512,4,128]{0,2,1:T(8,128)(2,1)S(1)} %bitcast.132, bf16[512,4,128]{0,2,1:T(8,128)(2,1)} %bitcast.139), kind=kOutput, calls=%fused_computation.168 | convolution fusion | flops 272630272 | bytes 5513216 | tf_op jit(solution)/shard_map/sub | solution.py:172
  101.9 26.5 %reduce-scatter.2.cloned.1.call-done = bf16[1,6,4,128,128]{4,3,1,2,0:T(8,128)(2,1)} async-done(((bf16[4,6,4,128,128]{4,3,1,2,0:T(8,128)(2,1)}), bf16[1,6,4,128,128]{4,3,1,2,0:T(8,128)(2,1)}) %reduce-scatter.2.cloned.1.call-update) | async-done | bytes 786448 | tf_op jit(solution)/shard_map/reduce_scatter | solution.py:149
  128.4 3.5 %fusion.32 = f32[512,4,128]{0,2,1:T(8,128)} fusion(bf16[512,6]{0,1:T(8,128)(2,1)S(1)} %get-tuple-element.21, bf16[512,4,128]{2,0,1:T(8,128)(2,1)S(1)} %copy.61, bf16[1,6,4,128,128]{4,3,1,2,0:T(8,128)(2,1)} %reduce-scatter.2.cloned.1.call-done, f32[512,4]{0,1:T(4,128)S(1)} %fusion.72), kind=kOutput, calls=%fused_computation.44 | convolution fusion | flops 404488192 | bytes 2373632 | tf_op jit(solution)/shard_map/tshi,shji->thj/dot_general | solution.py:163
  131.9 4.0 %multiply_reduce_fusion = (f32[512,4]{0,1:T(4,128)S(1)}, f32[512,4,128]{0,2,1:T(8,128)}) fusion(f32[512,4,128]{0,2,1:T(8,128)} %fusion.32, bf16[512,4,128]{0,2,1:T(8,128)(2,1)S(1)} %bitcast.137, f32[4,512]{1,0:T(4,128)S(1)} %bitcast.148, pred[512,512]{0,1:T(8,128)(4,1)S(1)} %fusion.51, bf16[512,4,128]{0,2,1:T(8,128)(2,1)S(1)} %bitcast.133, ...), kind=kOutput, calls=%fused_computation.67 | convolution fusion | flops 542898176 | bytes 3948544 | tf_op jit(solution)/shard_map/hqk,khd->qhd/dot_general | solution.py:177
  136.0 3.2 %fusion.35 = bf16[512,4,128]{0,2,1:T(8,128)(2,1)S(1)} fusion(bf16[512,4,128]{0,2,1:T(8,128)(2,1)S(1)} %bitcast.138, f32[4,512,512]{1,2,0:T(8,128)} %get-tuple-element.25, f32[4,512]{1,0:T(4,128)S(1)} %get-tuple-element.24, f32[512,4,128]{0,2,1:T(8,128)} %get-tuple-element.27, f32[512,4]{0,1:T(4,128)S(1)} %add_rsqrt_fusion, f32[512,4]{0,1:T(4,128)S(1)} %fusion.71), kind=kOutput, calls=%fused_computation.45 | convolution fusion | flops 271581184 | bytes 6316032 | tf_op jit(solution)/shard_map/hqk,khd->qhd/dot_general | solution.py:174
  139.2 0.7 collective-permute-start.5
  139.9 0.5 fusion.56
  140.4 0.7 collective-permute-done.5
  141.1 1.8 %fusion.42 = (f32[256]{0:T(256)S(1)}, bf16[256,1024]{1,0:T(8,128)(2,1)S(1)}) fusion(f32[256,1024]{1,0:T(8,128)S(1)} %fusion.56, bf16[256,512]{0,1:T(8,128)(2,1)S(1)} %collective-permute-done.5, bf16[512,1024]{1,0:T(8,128)(2,1)} %collective-permute-done.6, bf16[256,1024]{1,0:T(8,128)(2,1)S(1)} %copy-done.2), kind=kOutput, calls=%fused_computation.55 | convolution fusion | flops 270270208 | bytes 3408896 | tf_op jit(solution)/shard_map/dot_general | solution.py:185
  142.9 0.2 fusion.44
  143.1 0.6 collective-permute-start.7
  143.7 1.5 collective-permute-done.7
  145.2 0.3 broadcast_select_fusion.1
  145.6 3.2 %fusion.3 = f32[2,512,1408]{2,1,0:T(8,128)S(1)} fusion(bf16[3,1024,1408]{2,1,0:T(8,128)(2,1)S(1)} %bitcast.161, bf16[256,1024]{1,0:T(8,128)(2,1)S(1)} %get-tuple-element.14, bf16[256,1024]{1,0:T(8,128)(2,1)S(1)} %get-tuple-element.13), kind=kOutput, calls=%fused_computation.5 | convolution fusion | flops 2954887168 | bytes 12582912 | tf_op jit(solution)/shard_map/td,kdf->ktf/dot_general | solution.py:192
  148.8 1.8 %fusion.11 = f32[512,1024]{1,0:T(8,128)S(1)} fusion(bf16[3,1024,1408]{2,1,0:T(8,128)(2,1)S(1)} %bitcast.161, f32[2,512,1408]{2,1,0:T(8,128)S(1)} %fusion.3), kind=kOutput, calls=%fused_computation.17 | convolution fusion | flops 1480720384 | bytes 10747904 | tf_op jit(solution)/shard_map/tf,df->td/dot_general | solution.py:196
  150.6 0.1 constant_dynamic-slice_fusion
  150.7 0.5 collective-permute-start.8
  151.2 2.3 %collective-permute-done.8 = f32[256,1024]{1,0:T(8,128)S(1)} collective-permute-done((f32[256,1024]{1,0:T(8,128)S(1)}, f32[256,1024]{1,0:T(8,128)S(1)}, u32[]{:S(2)}, u32[]{:S(2)}) %collective-permute-start.8) | collective-permute-done | bytes 1048608 | tf_op jit(solution)/shard_map/ppermute | solution.py:23
  153.5 1.1 fusion.45
  (65 shorter events, 0.3 us)
Async XLA Ops:
  6.5 25.8 %copy-start = (bf16[3,1024,512]{2,1,0:T(8,128)(2,1)S(1)}, bf16[3,1024,512]{2,1,0:T(8,128)(2,1)}, u32[]{:S(2)}) copy-start(bf16[3,1024,512]{2,1,0:T(8,128)(2,1)} %param.15) | copy-start | bytes 9437188
  6.5 17.2 %copy-start.15 = (s32[1,2,3]{2,1,0:T(2,128)S(1)}, s32[1,2,3]{2,1,0:T(2,128)}, u32[]{:S(2)}) copy-start(s32[1,2,3]{2,1,0:T(2,128)} %param.20) | copy-start | bytes 76
  6.5 17.7 %copy-start.11 = (s32[1,6]{1,0:T(1,128)S(1)}, s32[1,6]{1,0:T(1,128)}, u32[]{:S(2)}) copy-start(s32[1,6]{1,0:T(1,128)} %param.21) | copy-start | bytes 76
  6.5 76.8 %all-gather.2.cloned.1.call-start = ((), (), s32[]{:S(2)}) async-start(), calls=%async_computation.1 | async-start | bytes 8912896 | tf_op jit(solution)/shard_map/all_gather | solution.py:95
  8.8 119.6 %reduce-scatter.2.cloned.1.call-start = ((), (), s32[]{:S(2)}) async-start(), calls=%async_computation.2 | async-start | bytes 3932160 | tf_op jit(solution)/shard_map/reduce_scatter | solution.py:149
  8.8 21.1 %copy-start.13 = (s32[1,6]{1,0:T(1,128)S(1)}, s32[1,6]{1,0:T(1,128)}, u32[]{:S(2)}) copy-start(s32[1,6]{1,0:T(1,128)} %param.22) | copy-start | bytes 76
  8.8 21.1 %collective-permute-start.2 = (s32[6]{0:T(128)}, s32[6]{0:T(128)S(1)}, u32[]{:S(2)}, u32[]{:S(2)}) collective-permute-start(s32[6]{0:T(128)} %bitcast.154), channel_id=1, source_target_pairs={{0,32},{32,64},{64,96},{96,0},{1,33},{33,65},{65,97},{97,1},{2,34}... | collective-permute-start | bytes 80 | tf_op jit(solution)/shard_map/ppermute | solution.py:140
  11.4 18.6 %collective-permute-start.3 = (s32[6]{0:T(128)}, s32[6]{0:T(128)S(1)}, u32[]{:S(2)}, u32[]{:S(2)}) collective-permute-start(s32[6]{0:T(128)} %bitcast.155), channel_id=1, source_target_pairs={{0,64},{32,96},{64,0},{96,32},{1,65},{33,97},{65,1},{97,33},{2,66}... | collective-permute-start | bytes 80 | tf_op jit(solution)/shard_map/ppermute | solution.py:140
  14.7 15.3 %collective-permute-start.4 = (s32[6]{0:T(128)}, s32[6]{0:T(128)S(1)}, u32[]{:S(2)}, u32[]{:S(2)}) collective-permute-start(s32[6]{0:T(128)} %bitcast.156), channel_id=1, source_target_pairs={{0,96},{32,0},{64,32},{96,64},{1,97},{33,1},{65,33},{97,65},{2,98}... | collective-permute-start | bytes 80 | tf_op jit(solution)/shard_map/ppermute | solution.py:140
  19.4 11.3 %collective-permute-start = (bf16[256,1024]{1,0:T(8,128)(2,1)}, bf16[256,1024]{1,0:T(8,128)(2,1)}, u32[]{:S(2)}, u32[]{:S(2)}) collective-permute-start(bf16[256,1024]{1,0:T(8,128)(2,1)} %fusion.41), channel_id=1, source_target_pairs={{0,1},{1,0},{2,3},{3,2},{4,5},{5,4},{6,7},{7,6},{8,9},{9,8},{10,11... | collective-permute-start | bytes 1572872 | tf_op jit(solution)/shard_map/ppermute | solution.py:23
  23.8 11.6 %collective-permute-start.1 = (bf16[32,1024,16]{1,0,2:T(8,128)(2,1)}, bf16[32,1024,16]{1,0,2:T(8,128)(2,1)}, u32[]{:S(2)}, u32[]{:S(2)}) collective-permute-start(bf16[32,1024,16]{1,0,2:T(8,128)(2,1)} %copy.51), channel_id=1, source_target_pairs={{0,1},{1,0},{2,3},{3,2},{4,5},{5,4},{6,7},{7,6},{8,9},{9,8},{10,11... | collective-permute-start | bytes 3145736 | tf_op jit(solution)/shard_map/ppermute | solution.py:23
  32.3 4.8 %copy-start.7 = (bf16[256,1024]{1,0:T(8,128)(2,1)}, bf16[256,1024]{1,0:T(8,128)(2,1)S(1)}, u32[]{:S(2)}) copy-start(bf16[256,1024]{1,0:T(8,128)(2,1)S(1)} %get-tuple-element.15) | copy-start | bytes 1572868
  32.3 4.8 %copy-start.8 = (bf16[256,1024]{1,0:T(8,128)(2,1)}, bf16[256,1024]{1,0:T(8,128)(2,1)S(1)}, u32[]{:S(2)}) copy-start(bf16[256,1024]{1,0:T(8,128)(2,1)S(1)} %get-tuple-element.16) | copy-start | bytes 1572868
  32.3 3.1 %copy-start.4 = (f32[6,1024,16]{1,0,2:T(8,128)S(1)}, f32[6,1024,16]{1,0,2:T(8,128)}, u32[]{:S(2)}) copy-start(f32[6,1024,16]{1,0,2:T(8,128)} %fusion.77) | copy-start | bytes 1179652
  89.9 1.2 copy-start.5
  89.9 2.3 %copy-start.14 = (bf16[2,1024,4]{1,2,0:T(4,128)(2,1)S(1)}, bf16[2,1024,4]{1,2,0:T(4,128)(2,1)}, u32[]{:S(2)}) copy-start(bf16[2,1024,4]{1,2,0:T(4,128)(2,1)} %param.16) | copy-start | bytes 49156
  89.9 3.9 %copy-start.12 = (f32[4]{0:T(128)S(1)}, f32[4]{0:T(128)}, u32[]{:S(2)}) copy-start(f32[4]{0:T(128)} %param.17) | copy-start | bytes 52
  89.9 5.9 %copy-start.6 = (bf16[3,512,512]{1,2,0:T(8,128)(2,1)S(1)}, bf16[3,512,512]{1,2,0:T(8,128)(2,1)}, u32[]{:S(2)}) copy-start(bf16[3,512,512]{1,2,0:T(8,128)(2,1)} %get-tuple-element.22) | copy-start | bytes 4718596
  90.0 7.0 %copy-start.3 = (bf16[512,512]{0,1:T(8,128)(2,1)S(1)}, bf16[512,512]{0,1:T(8,128)(2,1)}, u32[]{:S(2)}) copy-start(bf16[512,512]{0,1:T(8,128)(2,1)} %fusion.36) | copy-start | bytes 1572868
  91.2 49.3 %collective-permute-start.6 = (bf16[512,1024]{1,0:T(8,128)(2,1)S(1)}, bf16[512,1024]{1,0:T(8,128)(2,1)}, u32[]{:S(2)}, u32[]{:S(2)}) collective-permute-start(bf16[512,1024]{1,0:T(8,128)(2,1)S(1)} %copy-done.5), channel_id=1, source_target_pairs={{0,1},{1,0},{2,3},{3,2},{4,5},{5,4},{6,7},{7,6},{8,9},{9,8},{10,11... | collective-permute-start | bytes 3145736 | tf_op jit(solution)/shard_map/ppermute | solution.py:23
  101.9 30.0 %copy-start.9 = (bf16[1,512,512]{1,2,0:T(8,128)(2,1)S(1)}, bf16[1,512,512]{1,2,0:T(8,128)(2,1)}, u32[]{:S(2)}) copy-start(bf16[1,512,512]{1,2,0:T(8,128)(2,1)} %get-tuple-element.12) | copy-start | bytes 1572868
  101.9 30.0 %copy-start.10 = (bf16[1,512,512]{1,2,0:T(8,128)(2,1)S(1)}, bf16[1,512,512]{1,2,0:T(8,128)(2,1)}, u32[]{:S(2)}) copy-start(bf16[1,512,512]{1,2,0:T(8,128)(2,1)} %get-tuple-element.11) | copy-start | bytes 1572868
  136.0 9.6 %slice-start = ((s8[8650752]{0:T(1024)(128)(4,1)}), s8[4194304]{0:T(1024)(128)(4,1)S(1)}, s32[]{:S(2)}) async-start(s8[8650752]{0:T(1024)(128)(4,1)} %bitcast.160), calls=%async_computation.3 | async-start | bytes 8388608
  136.0 9.6 %slice-start.1 = ((s8[8650752]{0:T(1024)(128)(4,1)}), s8[4194304]{0:T(1024)(128)(4,1)S(1)}, s32[]{:S(2)}) async-start(s8[8650752]{0:T(1024)(128)(4,1)} %bitcast.160), calls=%async_computation.4 | async-start | bytes 8388608
  139.2 1.9 %copy-start.2 = (bf16[256,1024]{1,0:T(8,128)(2,1)S(1)}, bf16[256,1024]{1,0:T(8,128)(2,1)}, u32[]{:S(2)}) copy-start(bf16[256,1024]{1,0:T(8,128)(2,1)} %param.13) | copy-start | bytes 1572868
  139.2 6.4 %slice-start.2 = ((s8[8650752]{0:T(1024)(128)(4,1)}), s8[262144]{0:T(1024)(128)(4,1)S(1)}, s32[]{:S(2)}) async-start(s8[8650752]{0:T(1024)(128)(4,1)} %bitcast.160), calls=%async_computation.5 | async-start | bytes 524288
  139.2 1.9 %collective-permute-start.5 = (bf16[256,512]{0,1:T(8,128)(2,1)S(1)}, bf16[256,512]{0,1:T(8,128)(2,1)S(1)}, u32[]{:S(2)}, u32[]{:S(2)}) collective-permute-start(bf16[256,512]{0,1:T(8,128)(2,1)S(1)} %constant_dynamic-slice_fusion.1), channel_id=1, source_target_pairs={{0,1},{1,0},{2,3},{3,2},{4,5},{5,4},{6,7},{7,6},{8,9},{9,8},{10,11... | collective-permute-start | bytes 786440 | tf_op jit(solution)/shard_map/ppermute | solution.py:23
  143.1 2.1 %collective-permute-start.7 = (bf16[256,1024]{1,0:T(8,128)(2,1)S(1)}, bf16[256,1024]{1,0:T(8,128)(2,1)S(1)}, u32[]{:S(2)}, u32[]{:S(2)}) collective-permute-start(bf16[256,1024]{1,0:T(8,128)(2,1)S(1)} %fusion.44), channel_id=1, source_target_pairs={{0,1},{1,0},{2,3},{3,2},{4,5},{5,4},{6,7},{7,6},{8,9},{9,8},{10,11... | collective-permute-start | bytes 1572872 | tf_op jit(solution)/shard_map/ppermute | solution.py:23
  148.8 5.7 %copy-start.1 = (bf16[3,1024,512]{2,1,0:T(8,128)(2,1)S(1)}, bf16[3,1024,512]{2,1,0:T(8,128)(2,1)}, u32[]{:S(2)}) copy-start(bf16[3,1024,512]{2,1,0:T(8,128)(2,1)} %param.15) | copy-start | bytes 9437188
  150.7 2.7 %collective-permute-start.8 = (f32[256,1024]{1,0:T(8,128)S(1)}, f32[256,1024]{1,0:T(8,128)S(1)}, u32[]{:S(2)}, u32[]{:S(2)}) collective-permute-start(f32[256,1024]{1,0:T(8,128)S(1)} %constant_dynamic-slice_fusion), channel_id=1, source_target_pairs={{0,1},{1,0},{2,3},{3,2},{4,5},{5,4},{6,7},{7,6},{8,9},{9,8},{10,11... | collective-permute-start | bytes 3145736 | tf_op jit(solution)/shard_map/ppermute | solution.py:23
Sparse Core Ops, SparseCore 0:
  9.5 73.8 all-gather.1
  90.1 38.2 reduce-scatter.1

commit v6 on v5

--- a/solution.py
+++ b/solution.py
@@ -160,6 +160,7 @@
     start_level = jnp.sum(start_hot[:, :, None] * before[None, :, :], axis=1)
     level = running - jnp.sum(member[:, :, None] * start_level[None, :, :], axis=1)
     masked_queries = queries[:, None, :, :] * member.astype(jnp.bfloat16)[:, :, None, None]
+    masked_queries, mix_gate = lax.optimization_barrier((masked_queries, mix_gate))
     from_state = jnp.einsum(
         "tshi,shji->thj", masked_queries, states, preferred_element_type=jnp.float32
     )

time: 162 us -> 156 us (0.963)
  waiting for transfers between devices: 75.7 us -> 71.1 us
  matrix products: 36.2 us -> 33.8 us
    reduce_scatter x1, waiting for transfers between devices: 26.5 us -> 22 us  [on_device(): states = lax.psum_scatter(slots, 'z', scatter_dimension=0, tiled=True)[0]]
    dot_general x1, matrix products: 3.17 us -> 0.59 us  [on_device(): jnp.einsum('hqk,khd->qhd', probs, values, preferred_element_type=jnp.floa...]
    dot_general x1, matrix products: 0.47 us -> 2.31 us  [on_device(): jnp.dot(head_own, head_output_weight, preferred_element_type=jnp.float32)]
    unnamed x41 -> x43, local copies, waits for them, and re-layouts: 6.28 us -> 5.22 us
  transfers between devices with their start and end apart: 11 -> 11, of which waited for: 5 -> 4; matrix products, arithmetic and copies ran while one was open for 27% -> 28% of each run, Pallas kernels for 0% -> 0%
where the time goes in v6:
time: 156 us; the launch traced here: 155 us
  waiting for transfers between devices  71.1 us (46%)
  matrix products  33.8 us (22%)
  local copies, waits for them, and re-layouts  13.8 us (9%)
  between operations  13.8 us (9%)
  other arithmetic  12.6 us (8%)
  starting transfers between devices  10.1 us (6%)
    all_gather x1, waiting for transfers between devices, on_device(): lax.all_gather(jnp.swapaxes(caches, -1, -2), ('y', 'x'), axis=0, tiled=True)  44.6 us
    reduce_scatter x1, waiting for transfers between devices, on_device(): states = lax.psum_scatter(slots, 'z', scatter_dimension=0, tiled=True)[0]  22 us
    ppermute x3, starting transfers between devices, along_z(): lax.ppermute(value, 'z', perm=[(i, (i + d) % z_count) for i in range(z_co...  6.57 us
    unnamed x43, local copies, waits for them, and re-layouts  5.22 us
    sub x1, matrix products, on_device(): weights = jnp.exp(masked - peak)  4.79 us
    gather x1, local copies, waits for them, and re-layouts, on_device(): jnp.take(plane, jnp.clip(local, 0, per_plane - 1).reshape(-1), axis=0)  4.53 us
    ppermute x6, waiting for transfers between devices, swap(): return lax.ppermute(value, 'col', perm=[(0, 1), (1, 0)])  4.43 us
    dot_general x1, matrix products, on_device(): jnp.einsum('hqk,khd->qhd', memory_w, values, preferred_element_type=jnp.f...  4.23 us
  transfers between devices with their start and end apart: 11, of which 4 were waited for; matrix products, arithmetic and copies ran while one was open for 28% of the time, Pallas kernels for 0%

profile of v6, /device:TPU:1, one launch (start us, length us, event | category | flops | bytes accessed | tf_op | source)
XLA Modules:
  0.0 155.1 jit_solution(5127266728118954497)
XLA Ops:
  6.5 2.2 %copy.50 = bf16[4,4,128,128]{2,3,1,0:T(8,128)(2,1)} copy(bf16[4,4,128,128]{3,2,1,0:T(8,128)(2,1)} %param.23) | data formatting | bytes 1048576 | tf_op args[10]
  8.8 0.0 reduce-scatter.2.cloned.1.call-start
  8.8 2.5 %collective-permute-start.2 = (s32[6]{0:T(128)}, s32[6]{0:T(128)S(1)}, u32[]{:S(2)}, u32[]{:S(2)}) collective-permute-start(s32[6]{0:T(128)} %bitcast.157), channel_id=1, source_target_pairs={{0,32},{32,64},{64,96},{96,0},{1,33},{33,65},{65,97},{97,1},{2,34}... | collective-permute-start | bytes 80 | tf_op jit(solution)/shard_map/ppermute | solution.py:140
  11.4 3.3 %collective-permute-start.3 = (s32[6]{0:T(128)}, s32[6]{0:T(128)S(1)}, u32[]{:S(2)}, u32[]{:S(2)}) collective-permute-start(s32[6]{0:T(128)} %bitcast.158), channel_id=1, source_target_pairs={{0,64},{32,96},{64,0},{96,32},{1,65},{33,97},{65,1},{97,33},{2,66}... | collective-permute-start | bytes 80 | tf_op jit(solution)/shard_map/ppermute | solution.py:140
  14.7 0.7 collective-permute-start.4
  15.4 1.2 fusion.30
  16.6 0.8 fusion.96
  17.4 2.0 %fusion.32 = bf16[256,1024]{1,0:T(8,128)(2,1)} fusion(bf16[256,1024]{1,0:T(8,128)(2,1)} %param.13, f32[1024]{0:T(1024)S(1)} %bitcast.148, f32[256]{0:T(256)S(1)} %add_rsqrt_fusion.2), kind=kLoop, calls=%fused_computation.51 | loop fusion | flops 1048576 | bytes 1053696 | tf_op jit(solution)/shard_map/convert_element_type | solution.py:19
  19.5 1.5 collective-permute-start
  21.0 2.8 %copy.51 = bf16[32,1024,16]{1,0,2:T(8,128)(2,1)} copy(bf16[32,1024,16]{1,2,0:T(8,128)(2,1)} %param.18) | data formatting | bytes 2097152 | tf_op args[5]
  23.8 0.1 reshape.431
  23.9 0.1 reshape_squeeze.3
  24.0 0.2 reduce-window.14
  24.2 0.1 fusion.54
  24.3 2.4 %convolution_convert_fusion = bf16[6,16,512]{2,0,1:T(8,128)(2,1)S(1)} fusion(bf16[64,16,512]{2,1,0:T(8,128)(2,1)} %param.19, s32[6]{0:T(128)S(1)} %bitcast.152), kind=kOutput, calls=%fused_computation.47 | convolution fusion | flops 6340992 | bytes 1146904 | tf_op jit(solution)/shard_map/gq,qjl->gjl/dot_general | solution.py:127
  26.7 3.2 %fusion.68 = f32[6,1024,16]{1,0,2:T(8,128)} fusion(s32[32]{0:T(128)S(1)} %iota_add_fusion.1, s32[6]{0:T(128)S(1)} %bitcast.153, bf16[32,1024,16]{1,2,0:T(8,128)(2,1)} %param.18), kind=kOutput, calls=%fused_computation.115 | convolution fusion | flops 6291648 | bytes 1441944 | tf_op jit(solution)/shard_map/sa,adr->sdr/dot_general | solution.py:117
  30.0 0.6 gather_fusion
  30.6 0.1 compare_and_fusion
  30.6 0.1 min.12
  30.8 1.5 broadcast_select_fusion.3
  32.3 3.1 %fusion.97 = (bf16[3,512,512]{1,2,0:T(8,128)(2,1)}, f32[3,512,512]{1,2,0:T(8,128)S(1)}) fusion(bf16[3,1024,512]{2,1,0:T(8,128)(2,1)S(1)} %copy-done, bf16[256,1024]{1,0:T(8,128)(2,1)S(1)} %get-tuple-element.20, bf16[256,1024]{1,0:T(8,128)(2,1)S(1)} %get-tuple-element.19), kind=kOutput, calls=%fused_computation.164 | convolution fusion | flops 1613496320 | bytes 8912896 | tf_op jit(solution)/shard_map/td,kdc->ktc/dot_general | solution.py:107
  35.4 1.5 fusion.29
  36.9 0.1 copy.53
  37.1 0.5 fusion.46
  37.6 1.2 fusion.27
  38.7 44.6 %all-gather.2.cloned.1.call-done = bf16[64,4,128,128]{3,2,1,0:T(8,128)(2,1)} async-done(((bf16[4,4,128,128]{3,2,1,0:T(8,128)(2,1)}), bf16[64,4,128,128]{3,2,1,0:T(8,128)(2,1)}) %all-gather.2.cloned.1.call-update) | async-done | bytes 8388624 | tf_op jit(solution)/shard_map/all_gather | solution.py:95
  83.4 4.5 %gather_fusion.1 = bf16[24,4,128,128]{3,2,1,0:T(8,128)(2,1)S(1)} fusion(bf16[64,4,128,128]{3,2,1,0:T(8,128)(2,1)} %all-gather.2.cloned.1.call-done, s32[1024]{0:T(1024)S(1)} %pad_clamp_fusion), kind=kCustom, calls=%fused_computation.1 | custom fusion | bytes 6291552 | tf_op jit(solution)/shard_map/jit(_take)/gather | solution.py:146
  87.9 2.0 %fusion.7 = bf16[4,6,4,128,128]{4,3,1,2,0:T(8,128)(2,1)} fusion(bf16[4,6,4,128,128]{4,3,2,1,0:T(8,128)(2,1)S(1)} %bitcast.133, pred[4,6]{1,0:T(4,128)(4,1)S(1)} %get-tuple-element.13, bf16[4,6]{1,0:T(4,128)(2,1)S(1)} %get-tuple-element.23), kind=kLoop, calls=%fused_computation.12 | loop fusion | flops 3145728 | bytes 6291528 | tf_op jit(solution)/shard_map/mul | solution.py:148
  90.0 0.0 reduce-scatter.2.cloned.1.call-update
  90.0 0.9 collective-permute-start.6
  90.9 0.1 convert_reduce_fusion
  91.0 0.1 fusion.55
  91.1 0.2 fusion.42
  91.3 0.4 convolution_bitcast_fusion.3
  91.7 0.1 fusion.92
  91.8 1.2 reduce-window.18
  93.1 0.2 slice_reduce_fusion
  93.2 0.2 reduce-window.19
  93.4 0.1 add_bitcast_fusion
  93.5 0.1 bitcast_subtract_fusion.1
  93.6 0.1 multiply_reduce_fusion.3
  93.7 0.1 multiply_reduce_fusion.2
  93.8 1.0 fusion.95
  94.8 1.0 copy.59
  95.9 1.5 broadcast_multiply_fusion
  97.4 4.8 %fusion.98 = (f32[4,512]{1,0:T(4,128)S(1)}, f32[4,512,512]{1,2,0:T(8,128)}) fusion(pred[512,512]{0,1:T(8,128)(4,1)S(1)} %fusion.42, bf16[512,4,128]{0,2,1:T(8,128)(2,1)} %bitcast.134, bf16[512,4,128]{0,2,1:T(8,128)(2,1)} %bitcast.142), kind=kOutput, calls=%fused_computation.165 | convolution fusion | flops 272630272 | bytes 5513216 | tf_op jit(solution)/shard_map/sub | solution.py:173
  102.2 4.2 %fusion.21 = f32[512,4,128]{0,2,1:T(8,128)} fusion(bf16[512,4,128]{0,2,1:T(8,128)(2,1)} %bitcast.140, f32[4,512]{1,0:T(4,128)S(1)} %bitcast.151, pred[512,512]{0,1:T(8,128)(4,1)S(1)} %fusion.42, bf16[512,4,128]{0,2,1:T(8,128)(2,1)} %bitcast.135, bf16[512,4,128]{0,2,1:T(8,128)(2,1)} %bitcast.143), kind=kOutput, calls=%fused_computation.34 | convolution fusion | flops 542113792 | bytes 2891776 | tf_op jit(solution)/shard_map/hqk,khd->qhd/dot_general | solution.py:178
  106.4 22.0 %reduce-scatter.2.cloned.1.call-done = bf16[1,6,4,128,128]{4,3,1,2,0:T(8,128)(2,1)} async-done(((bf16[4,6,4,128,128]{4,3,1,2,0:T(8,128)(2,1)}), bf16[1,6,4,128,128]{4,3,1,2,0:T(8,128)(2,1)}) %reduce-scatter.2.cloned.1.call-update) | async-done | bytes 786448 | tf_op jit(solution)/shard_map/reduce_scatter | solution.py:149
  128.4 2.8 %multiply_reduce_fusion = (f32[512,4]{0,1:T(4,128)S(1)}, f32[512,4,128]{0,2,1:T(8,128)S(1)}) fusion(f32[512,4,128]{0,2,1:T(8,128)} %fusion.21, f32[512,4]{0,1:T(4,128)S(1)} %fusion.63, bf16[512,6,4,128]{3,0,1,2:T(8,128)(2,1)S(1)} %broadcast_multiply_fusion, bf16[1,6,4,128,128]{4,3,1,2,0:T(8,128)(2,1)} %reduce-scatter.2.cloned.1.call-done), kind=kOutput, calls=%fused_computation.64 | convolution fusion | flops 403699712 | bytes 6045696 | tf_op jit(solution)/shard_map/tshi,shji->thj/dot_general | solution.py:164
  131.2 0.1 copy-done.16
  131.3 0.6 fusion.26
  132.0 0.7 collective-permute-start.5
  132.7 2.3 %fusion.47 = f32[256,1024]{1,0:T(8,128)S(1)} fusion(bf16[512,1024]{1,0:T(8,128)(2,1)} %param.24, bf16[512,512]{0,1:T(8,128)(2,1)S(1)} %bitcast.139, s32[]{:T(128)S(6)} %select_n.131), kind=kOutput, calls=%fused_computation.74 | convolution fusion | flops 268435456 | bytes 2359300 | tf_op jit(solution)/shard_map/dot_general | solution.py:186
  135.0 1.8 %fusion.33 = (f32[256]{0:T(256)S(1)}, bf16[256,1024]{1,0:T(8,128)(2,1)S(1)}) fusion(f32[256,1024]{1,0:T(8,128)S(1)} %fusion.47, bf16[256,512]{0,1:T(8,128)(2,1)S(1)} %collective-permute-done.5, bf16[512,1024]{1,0:T(8,128)(2,1)} %collective-permute-done.6, bf16[256,1024]{1,0:T(8,128)(2,1)S(1)} %copy-done.2), kind=kOutput, calls=%fused_computation.52 | convolution fusion | flops 270270208 | bytes 3408896 | tf_op jit(solution)/shard_map/dot_general | solution.py:186
  136.8 0.2 fusion.35
  137.0 0.1 collective-permute-start.7
  137.1 1.9 %collective-permute-done.7 = bf16[256,1024]{1,0:T(8,128)(2,1)S(1)} collective-permute-done((bf16[256,1024]{1,0:T(8,128)(2,1)S(1)}, bf16[256,1024]{1,0:T(8,128)(2,1)S(1)}, u32[]{:S(2)}, u32[]{:S(2)}) %collective-permute-start.7) | collective-permute-done | bytes 524320 | tf_op jit(solution)/shard_map/ppermute | solution.py:23
  139.0 0.3 broadcast_select_fusion.1
  139.4 3.2 %fusion.3 = f32[2,512,1408]{2,1,0:T(8,128)S(1)} fusion(bf16[3,1024,1408]{2,1,0:T(8,128)(2,1)S(1)} %bitcast.164, bf16[256,1024]{1,0:T(8,128)(2,1)S(1)} %get-tuple-element.18, bf16[256,1024]{1,0:T(8,128)(2,1)S(1)} %get-tuple-element.17), kind=kOutput, calls=%fused_computation.5 | convolution fusion | flops 2954887168 | bytes 12582912 | tf_op jit(solution)/shard_map/td,kdf->ktf/dot_general | solution.py:193
  142.6 1.8 %fusion.9 = f32[512,1024]{1,0:T(8,128)S(1)} fusion(bf16[3,1024,1408]{2,1,0:T(8,128)(2,1)S(1)} %bitcast.164, f32[2,512,1408]{2,1,0:T(8,128)S(1)} %fusion.3), kind=kOutput, calls=%fused_computation.15 | convolution fusion | flops 1480720384 | bytes 10747904 | tf_op jit(solution)/shard_map/tf,df->td/dot_general | solution.py:197
  144.4 0.1 constant_dynamic-slice_fusion
  144.5 0.2 collective-permute-start.8
  144.7 2.5 %collective-permute-done.8 = f32[256,1024]{1,0:T(8,128)S(1)} collective-permute-done((f32[256,1024]{1,0:T(8,128)S(1)}, f32[256,1024]{1,0:T(8,128)S(1)}, u32[]{:S(2)}, u32[]{:S(2)}) %collective-permute-start.8) | collective-permute-done | bytes 1048608 | tf_op jit(solution)/shard_map/ppermute | solution.py:23
  147.3 1.1 fusion.36
  (68 shorter events, 0.3 us)
Async XLA Ops:
  6.5 25.8 %copy-start = (bf16[3,1024,512]{2,1,0:T(8,128)(2,1)S(1)}, bf16[3,1024,512]{2,1,0:T(8,128)(2,1)}, u32[]{:S(2)}) copy-start(bf16[3,1024,512]{2,1,0:T(8,128)(2,1)} %param.15) | copy-start | bytes 9437188
  6.5 17.3 %copy-start.15 = (s32[1,2,3]{2,1,0:T(2,128)S(1)}, s32[1,2,3]{2,1,0:T(2,128)}, u32[]{:S(2)}) copy-start(s32[1,2,3]{2,1,0:T(2,128)} %param.20) | copy-start | bytes 76
  6.5 17.8 %copy-start.11 = (s32[1,6]{1,0:T(1,128)S(1)}, s32[1,6]{1,0:T(1,128)}, u32[]{:S(2)}) copy-start(s32[1,6]{1,0:T(1,128)} %param.21) | copy-start | bytes 76
  6.5 76.8 %all-gather.2.cloned.1.call-start = ((), (), s32[]{:S(2)}) async-start(), calls=%async_computation.1 | async-start | bytes 8912896 | tf_op jit(solution)/shard_map/all_gather | solution.py:95
  8.8 119.6 %reduce-scatter.2.cloned.1.call-start = ((), (), s32[]{:S(2)}) async-start(), calls=%async_computation.2 | async-start | bytes 3932160 | tf_op jit(solution)/shard_map/reduce_scatter | solution.py:149
  8.8 21.2 %copy-start.13 = (s32[1,6]{1,0:T(1,128)S(1)}, s32[1,6]{1,0:T(1,128)}, u32[]{:S(2)}) copy-start(s32[1,6]{1,0:T(1,128)} %param.22) | copy-start | bytes 76
  8.8 21.1 %collective-permute-start.2 = (s32[6]{0:T(128)}, s32[6]{0:T(128)S(1)}, u32[]{:S(2)}, u32[]{:S(2)}) collective-permute-start(s32[6]{0:T(128)} %bitcast.157), channel_id=1, source_target_pairs={{0,32},{32,64},{64,96},{96,0},{1,33},{33,65},{65,97},{97,1},{2,34}... | collective-permute-start | bytes 80 | tf_op jit(solution)/shard_map/ppermute | solution.py:140
  11.4 18.6 %collective-permute-start.3 = (s32[6]{0:T(128)}, s32[6]{0:T(128)S(1)}, u32[]{:S(2)}, u32[]{:S(2)}) collective-permute-start(s32[6]{0:T(128)} %bitcast.158), channel_id=1, source_target_pairs={{0,64},{32,96},{64,0},{96,32},{1,65},{33,97},{65,1},{97,33},{2,66}... | collective-permute-start | bytes 80 | tf_op jit(solution)/shard_map/ppermute | solution.py:140
  14.7 15.3 %collective-permute-start.4 = (s32[6]{0:T(128)}, s32[6]{0:T(128)S(1)}, u32[]{:S(2)}, u32[]{:S(2)}) collective-permute-start(s32[6]{0:T(128)} %bitcast.159), channel_id=1, source_target_pairs={{0,96},{32,0},{64,32},{96,64},{1,97},{33,1},{65,33},{97,65},{2,98}... | collective-permute-start | bytes 80 | tf_op jit(solution)/shard_map/ppermute | solution.py:140
  19.5 11.3 %collective-permute-start = (bf16[256,1024]{1,0:T(8,128)(2,1)}, bf16[256,1024]{1,0:T(8,128)(2,1)}, u32[]{:S(2)}, u32[]{:S(2)}) collective-permute-start(bf16[256,1024]{1,0:T(8,128)(2,1)} %fusion.32), channel_id=1, source_target_pairs={{0,1},{1,0},{2,3},{3,2},{4,5},{5,4},{6,7},{7,6},{8,9},{9,8},{10,11... | collective-permute-start | bytes 1572872 | tf_op jit(solution)/shard_map/ppermute | solution.py:23
  23.8 11.6 %collective-permute-start.1 = (bf16[32,1024,16]{1,0,2:T(8,128)(2,1)}, bf16[32,1024,16]{1,0,2:T(8,128)(2,1)}, u32[]{:S(2)}, u32[]{:S(2)}) collective-permute-start(bf16[32,1024,16]{1,0,2:T(8,128)(2,1)} %copy.51), channel_id=1, source_target_pairs={{0,1},{1,0},{2,3},{3,2},{4,5},{5,4},{6,7},{7,6},{8,9},{9,8},{10,11... | collective-permute-start | bytes 3145736 | tf_op jit(solution)/shard_map/ppermute | solution.py:23
  32.3 4.8 %copy-start.6 = (bf16[256,1024]{1,0:T(8,128)(2,1)}, bf16[256,1024]{1,0:T(8,128)(2,1)S(1)}, u32[]{:S(2)}) copy-start(bf16[256,1024]{1,0:T(8,128)(2,1)S(1)} %get-tuple-element.19) | copy-start | bytes 1572868
  32.3 4.8 %copy-start.8 = (bf16[256,1024]{1,0:T(8,128)(2,1)}, bf16[256,1024]{1,0:T(8,128)(2,1)S(1)}, u32[]{:S(2)}) copy-start(bf16[256,1024]{1,0:T(8,128)(2,1)S(1)} %get-tuple-element.20) | copy-start | bytes 1572868
  32.3 3.1 %copy-start.4 = (f32[6,1024,16]{1,0,2:T(8,128)S(1)}, f32[6,1024,16]{1,0,2:T(8,128)}, u32[]{:S(2)}) copy-start(f32[6,1024,16]{1,0,2:T(8,128)} %fusion.68) | copy-start | bytes 1179652
  89.9 1.4 copy-start.7
  89.9 1.4 copy-start.9
  89.9 1.4 copy-start.14
  89.9 1.8 %copy-start.12 = (f32[4]{0:T(128)S(1)}, f32[4]{0:T(128)}, u32[]{:S(2)}) copy-start(f32[4]{0:T(128)} %param.17) | copy-start | bytes 52
  89.9 3.8 %copy-start.5 = (bf16[3,512,512]{1,2,0:T(8,128)(2,1)S(1)}, bf16[3,512,512]{1,2,0:T(8,128)(2,1)}, u32[]{:S(2)}) copy-start(bf16[3,512,512]{1,2,0:T(8,128)(2,1)} %get-tuple-element.26) | copy-start | bytes 4718596
  90.0 4.9 %copy-start.3 = (bf16[512,512]{0,1:T(8,128)(2,1)S(1)}, bf16[512,512]{0,1:T(8,128)(2,1)}, u32[]{:S(2)}) copy-start(bf16[512,512]{0,1:T(8,128)(2,1)} %fusion.27) | copy-start | bytes 1572868
  90.0 45.0 %collective-permute-start.6 = (bf16[512,1024]{1,0:T(8,128)(2,1)}, bf16[512,1024]{1,0:T(8,128)(2,1)}, u32[]{:S(2)}, u32[]{:S(2)}) collective-permute-start(bf16[512,1024]{1,0:T(8,128)(2,1)} %param.24), channel_id=1, source_target_pairs={{0,1},{1,0},{2,3},{3,2},{4,5},{5,4},{6,7},{7,6},{8,9},{9,8},{10,11... | collective-permute-start | bytes 3145736 | tf_op jit(solution)/shard_map/ppermute | solution.py:23
  128.4 2.8 %copy-start.10 = (bf16[1,512,512]{1,2,0:T(8,128)(2,1)S(1)}, bf16[1,512,512]{1,2,0:T(8,128)(2,1)}, u32[]{:S(2)}) copy-start(bf16[1,512,512]{1,2,0:T(8,128)(2,1)} %get-tuple-element.16) | copy-start | bytes 1572868
  128.4 2.9 %copy-start.16 = (f32[4,512,512]{1,2,0:T(8,128)S(1)}, f32[4,512,512]{1,2,0:T(8,128)}, u32[]{:S(2)}) copy-start(f32[4,512,512]{1,2,0:T(8,128)} %get-tuple-element.29) | copy-start | bytes 12582916
  131.3 8.1 %slice-start = ((s8[8650752]{0:T(1024)(128)(4,1)}), s8[4194304]{0:T(1024)(128)(4,1)S(1)}, s32[]{:S(2)}) async-start(s8[8650752]{0:T(1024)(128)(4,1)} %bitcast.163), calls=%async_computation.3 | async-start | bytes 8388608
  131.3 8.1 %slice-start.1 = ((s8[8650752]{0:T(1024)(128)(4,1)}), s8[4194304]{0:T(1024)(128)(4,1)S(1)}, s32[]{:S(2)}) async-start(s8[8650752]{0:T(1024)(128)(4,1)} %bitcast.163), calls=%async_computation.4 | async-start | bytes 8388608
  131.9 3.1 %copy-start.2 = (bf16[256,1024]{1,0:T(8,128)(2,1)S(1)}, bf16[256,1024]{1,0:T(8,128)(2,1)}, u32[]{:S(2)}) copy-start(bf16[256,1024]{1,0:T(8,128)(2,1)} %param.13) | copy-start | bytes 1572868
  131.9 7.4 %slice-start.2 = ((s8[8650752]{0:T(1024)(128)(4,1)}), s8[262144]{0:T(1024)(128)(4,1)S(1)}, s32[]{:S(2)}) async-start(s8[8650752]{0:T(1024)(128)(4,1)} %bitcast.163), calls=%async_computation.5 | async-start | bytes 524288
  132.0 3.0 %collective-permute-start.5 = (bf16[256,512]{0,1:T(8,128)(2,1)S(1)}, bf16[256,512]{0,1:T(8,128)(2,1)S(1)}, u32[]{:S(2)}, u32[]{:S(2)}) collective-permute-start(bf16[256,512]{0,1:T(8,128)(2,1)S(1)} %constant_dynamic-slice_fusion.1), channel_id=1, source_target_pairs={{0,1},{1,0},{2,3},{3,2},{4,5},{5,4},{6,7},{7,6},{8,9},{9,8},{10,11... | collective-permute-start | bytes 786440 | tf_op jit(solution)/shard_map/ppermute | solution.py:23
  137.0 2.0 %collective-permute-start.7 = (bf16[256,1024]{1,0:T(8,128)(2,1)S(1)}, bf16[256,1024]{1,0:T(8,128)(2,1)S(1)}, u32[]{:S(2)}, u32[]{:S(2)}) collective-permute-start(bf16[256,1024]{1,0:T(8,128)(2,1)S(1)} %fusion.35), channel_id=1, source_target_pairs={{0,1},{1,0},{2,3},{3,2},{4,5},{5,4},{6,7},{7,6},{8,9},{9,8},{10,11... | collective-permute-start | bytes 1572872 | tf_op jit(solution)/shard_map/ppermute | solution.py:23
  142.6 5.7 %copy-start.1 = (bf16[3,1024,512]{2,1,0:T(8,128)(2,1)S(1)}, bf16[3,1024,512]{2,1,0:T(8,128)(2,1)}, u32[]{:S(2)}) copy-start(bf16[3,1024,512]{2,1,0:T(8,128)(2,1)} %param.15) | copy-start | bytes 9437188
  144.5 2.7 %collective-permute-start.8 = (f32[256,1024]{1,0:T(8,128)S(1)}, f32[256,1024]{1,0:T(8,128)S(1)}, u32[]{:S(2)}, u32[]{:S(2)}) collective-permute-start(f32[256,1024]{1,0:T(8,128)S(1)} %constant_dynamic-slice_fusion), channel_id=1, source_target_pairs={{0,1},{1,0},{2,3},{3,2},{4,5},{5,4},{6,7},{7,6},{8,9},{9,8},{10,11... | collective-permute-start | bytes 3145736 | tf_op jit(solution)/shard_map/ppermute | solution.py:23
Sparse Core Ops, SparseCore 0:
  9.5 73.8 all-gather.1
  90.1 38.2 reduce-scatter.1

commit v7 on v4

--- a/solution.py
+++ b/solution.py
@@ -90,6 +90,7 @@
     scale = 1.0 / math.sqrt(head_size)
 
     down_other = swap(adapter_down_factor)
+    out_weight_other = swap(head_output_weight)
 
     plane = lax.all_gather(jnp.swapaxes(caches, -1, -2), ("y", "x"), axis=0, tiled=True)
     per_plane = plane.shape[0]
@@ -159,6 +160,7 @@
     start_level = jnp.sum(start_hot[:, :, None] * before[None, :, :], axis=1)
     level = running - jnp.sum(member[:, :, None] * start_level[None, :, :], axis=1)
     masked_queries = queries[:, None, :, :] * member.astype(jnp.bfloat16)[:, :, None, None]
+    masked_queries, mix_gate = lax.optimization_barrier((masked_queries, mix_gate))
     from_state = jnp.einsum(
         "tshi,shji->thj", masked_queries, states, preferred_element_type=jnp.float32
     )
@@ -179,10 +181,11 @@
     combined = attended + mix_gate[:, :, None] * recalled * factor
     head_out = combined.astype(jnp.bfloat16).reshape(group, head_cols)
 
-    head_partner = lax.dynamic_slice_in_dim(head_out, (1 - col) * tok_rows, tok_rows, axis=0)
     head_own = lax.dynamic_slice_in_dim(head_out, col * tok_rows, tok_rows, axis=0)
-    proj_partner = swap(jnp.dot(head_partner, head_output_weight, preferred_element_type=jnp.float32))
-    attn_proj = jnp.dot(head_own, head_output_weight, preferred_element_type=jnp.float32) + proj_partner
+    head_sent = lax.dynamic_slice_in_dim(head_out, (1 - col) * tok_rows, tok_rows, axis=0)
+    attn_proj = jnp.dot(head_own, head_output_weight, preferred_element_type=jnp.float32) + jnp.dot(
+        swap(head_sent), out_weight_other, preferred_element_type=jnp.float32
+    )
     mixed = (tokens.astype(jnp.float32) + attn_proj).astype(jnp.bfloat16)
     normed_two = rms_scale(mixed, norm_gain_pair[1])
 
@@ -195,13 +198,8 @@
             "tf,df->td", hidden, feedforward_weight[2], preferred_element_type=jnp.float32
         )
 
-    partner_two = swap(normed_two)
-    half = tok_rows // 2
-    for_partner = [
-        swap(feed_part(partner_two[:half])),
-        swap(feed_part(partner_two[half:])),
-    ]
-    feed = feed_part(normed_two) + jnp.concatenate(for_partner, axis=0)
+    from_partner = swap(feed_part(swap(normed_two)))
+    feed = feed_part(normed_two) + from_partner
     return (mixed.astype(jnp.float32) + feed).astype(jnp.bfloat16)
 
 

time: 174 us -> 154 us (0.89)
  matrix products: 46.1 us -> 35.1 us
  local copies, waits for them, and re-layouts: 17.9 us -> 13 us
  waiting for transfers between devices: 73.5 us -> 70 us
    dot_general x3 -> x2, matrix products: 6.22 us -> 2.85 us  [feed_part(): jnp.einsum('tf,df->td', hidden, feedforward_weight[2], preferred_element_...]
    dot_general x3 -> x2, matrix products: 6.3 us -> 3.4 us  [feed_part(): jnp.einsum('td,kdf->ktf', rows, feedforward_weight[:2], preferred_element...]
    reduce_scatter x1, waiting for transfers between devices: 24.6 us -> 22 us  [on_device(): states = lax.psum_scatter(slots, 'z', scatter_dimension=0, tiled=True)[0]]
    dot_general x1, matrix products: 3.26 us -> 0.58 us  [on_device(): jnp.einsum('hqk,khd->qhd', probs, values, preferred_element_type=jnp.floa...]
    mul x1, other arithmetic: 3.91 us -> 2.04 us  [on_device(): slots = (picked * keep).reshape((z_count, -1) + plane.shape[1:])]
    unnamed x31 -> x45, local copies, waits for them, and re-layouts: 5.43 us -> 5.22 us
  transfers between devices with their start and end apart: 11 -> 11, of which waited for: 5 -> 4; matrix products, arithmetic and copies ran while one was open for 22% -> 29% of each run, Pallas kernels for 0% -> 0%
where the time goes in v7:
time: 154 us; the launch traced here: 153 us
  waiting for transfers between devices  70 us (45%)
  matrix products  35.1 us (23%)
  between operations  13.8 us (9%)
  local copies, waits for them, and re-layouts  13 us (8%)
  other arithmetic  11.2 us (7%)
  starting transfers between devices  10.1 us (7%)
    all_gather x1, waiting for transfers between devices, on_device(): lax.all_gather(jnp.swapaxes(caches, -1, -2), ('y', 'x'), axis=0, tiled=True)  45.3 us
    reduce_scatter x1, waiting for transfers between devices, on_device(): states = lax.psum_scatter(slots, 'z', scatter_dimension=0, tiled=True)[0]  22 us
    ppermute x3, starting transfers between devices, along_z(): lax.ppermute(value, 'z', perm=[(i, (i + d) % z_count) for i in range(z_co...  6.57 us
    unnamed x45, local copies, waits for them, and re-layouts  5.22 us
    sub x1, matrix products, on_device(): weights = jnp.exp(masked - peak)  4.8 us
    gather x1, local copies, waits for them, and re-layouts, on_device(): jnp.take(plane, jnp.clip(local, 0, per_plane - 1).reshape(-1), axis=0)  4.53 us
    dot_general x1, matrix products, on_device(): jnp.einsum('hqk,khd->qhd', memory_w, values, preferred_element_type=jnp.f...  4.23 us
    ppermute x6, starting transfers between devices, swap(): return lax.ppermute(value, 'col', perm=[(0, 1), (1, 0)])  3.44 us
  transfers between devices with their start and end apart: 11, of which 4 were waited for; matrix products, arithmetic and copies ran while one was open for 29% of the time, Pallas kernels for 0%

profile of v7, /device:TPU:1, one launch (start us, length us, event | category | flops | bytes accessed | tf_op | source)
XLA Modules:
  0.0 153.2 jit_solution(6804957367423842180)
XLA Ops:
  6.5 0.0 all-gather.2.cloned.1.call-start
  6.6 2.2 %copy.50 = bf16[4,4,128,128]{2,3,1,0:T(8,128)(2,1)} copy(bf16[4,4,128,128]{3,2,1,0:T(8,128)(2,1)} %param.23) | data formatting | bytes 1048576 | tf_op args[10]
  8.8 0.0 reduce-scatter.2.cloned.1.call-start
  8.9 2.5 %collective-permute-start.2 = (s32[6]{0:T(128)}, s32[6]{0:T(128)S(1)}, u32[]{:S(2)}, u32[]{:S(2)}) collective-permute-start(s32[6]{0:T(128)} %bitcast.172), channel_id=1, source_target_pairs={{0,32},{32,64},{64,96},{96,0},{1,33},{33,65},{65,97},{97,1},{2,34}... | collective-permute-start | bytes 80 | tf_op jit(solution)/shard_map/ppermute | solution.py:140
  11.4 3.3 %collective-permute-start.3 = (s32[6]{0:T(128)}, s32[6]{0:T(128)S(1)}, u32[]{:S(2)}, u32[]{:S(2)}) collective-permute-start(s32[6]{0:T(128)} %bitcast.173), channel_id=1, source_target_pairs={{0,64},{32,96},{64,0},{96,32},{1,65},{33,97},{65,1},{97,33},{2,66}... | collective-permute-start | bytes 80 | tf_op jit(solution)/shard_map/ppermute | solution.py:140
  14.7 0.7 collective-permute-start.4
  15.4 2.8 %copy.51 = bf16[32,1024,16]{1,0,2:T(8,128)(2,1)} copy(bf16[32,1024,16]{1,2,0:T(8,128)(2,1)} %param.18) | data formatting | bytes 2097152 | tf_op args[5]
  18.2 1.5 collective-permute-start.1
  19.7 1.2 fusion.45
  21.0 2.0 %fusion.47 = bf16[256,1024]{1,0:T(8,128)(2,1)} fusion(bf16[256,1024]{1,0:T(8,128)(2,1)} %param.13, f32[1024]{0:T(1024)S(1)} %bitcast.162, f32[256]{0:T(256)S(1)} %add_rsqrt_fusion.2), kind=kLoop, calls=%fused_computation.60 | loop fusion | flops 1048576 | bytes 1053696 | tf_op jit(solution)/shard_map/convert_element_type | solution.py:19
  23.0 0.1 reshape.432
  23.1 0.1 reshape_squeeze.3
  23.2 0.2 reduce-window.14
  23.5 0.1 fusion.72
  23.5 2.6 %convolution_convert_fusion = bf16[6,16,512]{2,0,1:T(8,128)(2,1)S(1)} fusion(bf16[64,16,512]{2,1,0:T(8,128)(2,1)} %param.19, s32[6]{0:T(128)S(1)} %bitcast.167), kind=kOutput, calls=%fused_computation.56 | convolution fusion | flops 6340992 | bytes 1146904 | tf_op jit(solution)/shard_map/gq,qjl->gjl/dot_general | solution.py:127
  26.1 3.2 %fusion.86 = f32[6,1024,16]{1,0,2:T(8,128)} fusion(s32[32]{0:T(128)S(1)} %iota_add_fusion.1, s32[6]{0:T(128)S(1)} %bitcast.168, bf16[32,1024,16]{1,2,0:T(8,128)(2,1)} %param.18), kind=kOutput, calls=%fused_computation.122 | convolution fusion | flops 6291648 | bytes 1441944 | tf_op jit(solution)/shard_map/sa,adr->sdr/dot_general | solution.py:117
  29.4 0.6 gather_fusion
  30.0 0.1 compare_and_fusion
  30.0 0.1 min.12
  30.1 1.5 %broadcast_select_fusion.1 = (bf16[256,1024]{1,0:T(8,128)(2,1)S(1)}, bf16[256,1024]{1,0:T(8,128)(2,1)S(1)}) fusion(bf16[256,1024]{1,0:T(8,128)(2,1)} %collective-permute-done, pred[]{:T(512)S(6)} %eq.79, f32[1024]{0:T(1024)S(1)} %bitcast.163, f32[256]{0:T(256)S(1)} %add_rsqrt_fusion.2, bf16[256,1024]{1,0:T(8,128)(2,1)} %param.13), kind=kLoop, calls=%fused_computation.78 | loop fusion | flops 1572864 | bytes 2102273 | tf_op jit(solution)/shard_map/jit(_where)/select_n | solution.py:27
  31.7 3.1 %fusion.115 = (bf16[3,512,512]{1,2,0:T(8,128)(2,1)}, f32[3,512,512]{1,2,0:T(8,128)S(1)}) fusion(bf16[3,1024,512]{2,1,0:T(8,128)(2,1)S(1)} %copy-done, bf16[256,1024]{1,0:T(8,128)(2,1)S(1)} %get-tuple-element.18, bf16[256,1024]{1,0:T(8,128)(2,1)S(1)} %get-tuple-element.17), kind=kOutput, calls=%fused_computation.170 | convolution fusion | flops 1613496320 | bytes 8912896 | tf_op jit(solution)/shard_map/td,kdc->ktc/dot_general | solution.py:107
  34.8 1.5 %fusion.44 = bf16[6,1024,16]{1,0,2:T(8,128)(2,1)S(1)} fusion(f32[6,1024,16]{1,0,2:T(8,128)S(1)} %copy-done.4, bf16[32,1024,16]{1,0,2:T(8,128)(2,1)} %collective-permute-done.1, s32[32]{0:T(128)S(1)} %iota_add_fusion, s32[6]{0:T(128)S(1)} %bitcast.169), kind=kOutput, calls=%fused_computation.55 | convolution fusion | flops 6488256 | bytes 1638552 | tf_op jit(solution)/shard_map/sa,adr->sdr/dot_general | solution.py:118
  36.3 0.1 copy.53
  36.5 0.5 fusion.64
  37.0 1.1 fusion.39
  38.1 45.3 %all-gather.2.cloned.1.call-done = bf16[64,4,128,128]{3,2,1,0:T(8,128)(2,1)} async-done(((bf16[4,4,128,128]{3,2,1,0:T(8,128)(2,1)}), bf16[64,4,128,128]{3,2,1,0:T(8,128)(2,1)}) %all-gather.2.cloned.1.call-update) | async-done | bytes 8388624 | tf_op jit(solution)/shard_map/all_gather | solution.py:95
  83.4 4.5 %gather_fusion.1 = bf16[24,4,128,128]{3,2,1,0:T(8,128)(2,1)S(1)} fusion(bf16[64,4,128,128]{3,2,1,0:T(8,128)(2,1)} %all-gather.2.cloned.1.call-done, s32[1024]{0:T(1024)S(1)} %pad_clamp_fusion), kind=kCustom, calls=%fused_computation.1 | custom fusion | bytes 6291552 | tf_op jit(solution)/shard_map/jit(_take)/gather | solution.py:146
  87.9 2.0 %fusion.12 = bf16[4,6,4,128,128]{4,3,1,2,0:T(8,128)(2,1)} fusion(bf16[4,6,4,128,128]{4,3,2,1,0:T(8,128)(2,1)S(1)} %bitcast.149, pred[4,6]{1,0:T(4,128)(4,1)S(1)} %get-tuple-element.13, bf16[4,6]{1,0:T(4,128)(2,1)S(1)} %get-tuple-element.21), kind=kLoop, calls=%fused_computation.15 | loop fusion | flops 3145728 | bytes 6291528 | tf_op jit(solution)/shard_map/mul | solution.py:148
  90.0 0.0 reduce-scatter.2.cloned.1.call-update
  90.0 0.9 collective-permute-start.6
  91.0 0.1 convert_reduce_fusion
  91.0 0.1 fusion.73
  91.1 0.2 fusion.54
  91.4 0.4 convolution_bitcast_fusion.3
  91.7 0.1 fusion.110
  91.9 1.2 reduce-window.18
  93.1 0.2 slice_reduce_fusion
  93.2 0.2 reduce-window.19
  93.4 0.1 add_bitcast_fusion
  93.5 0.1 bitcast_subtract_fusion.1
  93.6 0.1 multiply_reduce_fusion.3
  93.7 0.1 multiply_reduce_fusion.2
  93.8 1.0 fusion.113
  94.9 1.0 copy.59
  95.9 1.5 broadcast_multiply_fusion
  97.4 4.8 %fusion.116 = (f32[4,512]{1,0:T(4,128)S(1)}, f32[4,512,512]{1,2,0:T(8,128)}) fusion(pred[512,512]{0,1:T(8,128)(4,1)S(1)} %fusion.54, bf16[512,4,128]{0,2,1:T(8,128)(2,1)} %bitcast.150, bf16[512,4,128]{0,2,1:T(8,128)(2,1)} %bitcast.158), kind=kOutput, calls=%fused_computation.171 | convolution fusion | flops 272630272 | bytes 5513216 | tf_op jit(solution)/shard_map/sub | solution.py:173
  102.2 4.2 %fusion.28 = f32[512,4,128]{0,2,1:T(8,128)} fusion(bf16[512,4,128]{0,2,1:T(8,128)(2,1)} %bitcast.156, f32[4,512]{1,0:T(4,128)S(1)} %bitcast.166, pred[512,512]{0,1:T(8,128)(4,1)S(1)} %fusion.54, bf16[512,4,128]{0,2,1:T(8,128)(2,1)} %bitcast.151, bf16[512,4,128]{0,2,1:T(8,128)(2,1)} %bitcast.159), kind=kOutput, calls=%fused_computation.41 | convolution fusion | flops 542113792 | bytes 2891776 | tf_op jit(solution)/shard_map/hqk,khd->qhd/dot_general | solution.py:178
  106.5 22.0 %reduce-scatter.2.cloned.1.call-done = bf16[1,6,4,128,128]{4,3,1,2,0:T(8,128)(2,1)} async-done(((bf16[4,6,4,128,128]{4,3,1,2,0:T(8,128)(2,1)}), bf16[1,6,4,128,128]{4,3,1,2,0:T(8,128)(2,1)}) %reduce-scatter.2.cloned.1.call-update) | async-done | bytes 786448 | tf_op jit(solution)/shard_map/reduce_scatter | solution.py:149
  128.4 2.8 %multiply_reduce_fusion = (f32[512,4]{0,1:T(4,128)S(1)}, f32[512,4,128]{0,2,1:T(8,128)S(1)}) fusion(f32[512,4,128]{0,2,1:T(8,128)} %fusion.28, f32[512,4]{0,1:T(4,128)S(1)} %fusion.81, bf16[512,6,4,128]{3,0,1,2:T(8,128)(2,1)S(1)} %broadcast_multiply_fusion, bf16[1,6,4,128,128]{4,3,1,2,0:T(8,128)(2,1)} %reduce-scatter.2.cloned.1.call-done), kind=kOutput, calls=%fused_computation.69 | convolution fusion | flops 403699712 | bytes 6045696 | tf_op jit(solution)/shard_map/tshi,shji->thj/dot_general | solution.py:164
  131.2 0.1 copy-done.17
  131.3 0.6 fusion.38
  132.0 0.7 collective-permute-start.5
  132.7 2.3 %fusion.65 = f32[256,1024]{1,0:T(8,128)S(1)} fusion(bf16[512,1024]{1,0:T(8,128)(2,1)} %param.24, bf16[512,512]{0,1:T(8,128)(2,1)S(1)} %bitcast.155, s32[]{:T(128)S(6)} %select_n.121), kind=kOutput, calls=%fused_computation.81 | convolution fusion | flops 268435456 | bytes 2359300 | tf_op jit(solution)/shard_map/dot_general | solution.py:186
  135.0 1.8 %fusion.48 = (f32[256]{0:T(256)S(1)}, bf16[256,1024]{1,0:T(8,128)(2,1)S(1)}) fusion(f32[256,1024]{1,0:T(8,128)S(1)} %fusion.65, bf16[256,512]{0,1:T(8,128)(2,1)S(1)} %collective-permute-done.5, bf16[512,1024]{1,0:T(8,128)(2,1)} %collective-permute-done.6, bf16[256,1024]{1,0:T(8,128)(2,1)S(1)} %copy-done.2), kind=kOutput, calls=%fused_computation.61 | convolution fusion | flops 270270208 | bytes 3408896 | tf_op jit(solution)/shard_map/dot_general | solution.py:186
  136.8 0.2 fusion.50
  137.0 0.1 collective-permute-start.7
  137.1 1.9 %collective-permute-done.7 = bf16[256,1024]{1,0:T(8,128)(2,1)S(1)} collective-permute-done((bf16[256,1024]{1,0:T(8,128)(2,1)S(1)}, bf16[256,1024]{1,0:T(8,128)(2,1)S(1)}, u32[]{:S(2)}, u32[]{:S(2)}) %collective-permute-start.7) | collective-permute-done | bytes 524320 | tf_op jit(solution)/shard_map/ppermute | solution.py:23
  139.0 1.7 %fusion.8 = f32[2,256,1408]{2,1,0:T(8,128)S(1)} fusion(bf16[3,1024,1408]{2,1,0:T(8,128)(2,1)S(1)} %bitcast.179, bf16[256,1024]{1,0:T(8,128)(2,1)S(1)} %collective-permute-done.7), kind=kOutput, calls=%fused_computation.12 | convolution fusion | flops 1476395008 | bytes 9175040 | tf_op jit(solution)/shard_map/td,kdf->ktf/dot_general | solution.py:193
  140.7 1.0 fusion.13
  141.8 0.2 collective-permute-start.8
  142.0 1.7 %fusion.5 = f32[2,256,1408]{2,1,0:T(8,128)S(1)} fusion(bf16[3,1024,1408]{2,1,0:T(8,128)(2,1)S(1)} %bitcast.179, bf16[256,1024]{1,0:T(8,128)(2,1)S(1)} %fusion.50), kind=kOutput, calls=%fused_computation.11 | convolution fusion | flops 1476395008 | bytes 9175040 | tf_op jit(solution)/shard_map/td,kdf->ktf/dot_general | solution.py:193
  143.7 0.8 collective-permute-done.8
  144.5 1.8 %fusion.41 = bf16[256,1024]{1,0:T(8,128)(2,1)} fusion(f32[256,1024]{1,0:T(8,128)S(1)} %collective-permute-done.8, bf16[3,1024,1408]{2,1,0:T(8,128)(2,1)S(1)} %bitcast.179, bf16[256,1024]{1,0:T(8,128)(2,1)S(1)} %get-tuple-element.31, f32[2,256,1408]{2,1,0:T(8,128)S(1)} %fusion.5), kind=kOutput, calls=%fused_computation.53 | convolution fusion | flops 741408768 | bytes 7864320 | tf_op jit(solution)/shard_map/tf,df->td/dot_general | solution.py:197
  146.3 0.1 copy-done.1
  (69 shorter events, 0.3 us)
Async XLA Ops:
  6.5 25.2 %copy-start = (bf16[3,1024,512]{2,1,0:T(8,128)(2,1)S(1)}, bf16[3,1024,512]{2,1,0:T(8,128)(2,1)}, u32[]{:S(2)}) copy-start(bf16[3,1024,512]{2,1,0:T(8,128)(2,1)} %param.15) | copy-start | bytes 9437188
  6.5 14.4 %copy-start.11 = (f32[2,1024]{1,0:T(2,128)S(1)}, f32[2,1024]{1,0:T(2,128)}, u32[]{:S(2)}) copy-start(f32[2,1024]{1,0:T(2,128)} %param.14) | copy-start | bytes 24580
  6.5 16.5 %copy-start.16 = (s32[1,2,3]{2,1,0:T(2,128)S(1)}, s32[1,2,3]{2,1,0:T(2,128)}, u32[]{:S(2)}) copy-start(s32[1,2,3]{2,1,0:T(2,128)} %param.20) | copy-start | bytes 76
  6.5 17.0 %copy-start.12 = (s32[1,6]{1,0:T(1,128)S(1)}, s32[1,6]{1,0:T(1,128)}, u32[]{:S(2)}) copy-start(s32[1,6]{1,0:T(1,128)} %param.21) | copy-start | bytes 76
  6.5 76.8 %all-gather.2.cloned.1.call-start = ((), (), s32[]{:S(2)}) async-start(), calls=%async_computation.1 | async-start | bytes 8912896 | tf_op jit(solution)/shard_map/all_gather | solution.py:95
  8.8 119.6 %reduce-scatter.2.cloned.1.call-start = ((), (), s32[]{:S(2)}) async-start(), calls=%async_computation.2 | async-start | bytes 3932160 | tf_op jit(solution)/shard_map/reduce_scatter | solution.py:149
  8.9 20.5 %copy-start.14 = (s32[1,6]{1,0:T(1,128)S(1)}, s32[1,6]{1,0:T(1,128)}, u32[]{:S(2)}) copy-start(s32[1,6]{1,0:T(1,128)} %param.22) | copy-start | bytes 76
  8.9 20.5 %collective-permute-start.2 = (s32[6]{0:T(128)}, s32[6]{0:T(128)S(1)}, u32[]{:S(2)}, u32[]{:S(2)}) collective-permute-start(s32[6]{0:T(128)} %bitcast.172), channel_id=1, source_target_pairs={{0,32},{32,64},{64,96},{96,0},{1,33},{33,65},{65,97},{97,1},{2,34}... | collective-permute-start | bytes 80 | tf_op jit(solution)/shard_map/ppermute | solution.py:140
  11.4 17.9 %collective-permute-start.3 = (s32[6]{0:T(128)}, s32[6]{0:T(128)S(1)}, u32[]{:S(2)}, u32[]{:S(2)}) collective-permute-start(s32[6]{0:T(128)} %bitcast.173), channel_id=1, source_target_pairs={{0,64},{32,96},{64,0},{96,32},{1,65},{33,97},{65,1},{97,33},{2,66}... | collective-permute-start | bytes 80 | tf_op jit(solution)/shard_map/ppermute | solution.py:140
  14.7 14.6 %collective-permute-start.4 = (s32[6]{0:T(128)}, s32[6]{0:T(128)S(1)}, u32[]{:S(2)}, u32[]{:S(2)}) collective-permute-start(s32[6]{0:T(128)} %bitcast.174), channel_id=1, source_target_pairs={{0,96},{32,0},{64,32},{96,64},{1,97},{33,1},{65,33},{97,65},{2,98}... | collective-permute-start | bytes 80 | tf_op jit(solution)/shard_map/ppermute | solution.py:140
  18.2 16.6 %collective-permute-start.1 = (bf16[32,1024,16]{1,0,2:T(8,128)(2,1)}, bf16[32,1024,16]{1,0,2:T(8,128)(2,1)}, u32[]{:S(2)}, u32[]{:S(2)}) collective-permute-start(bf16[32,1024,16]{1,0,2:T(8,128)(2,1)} %copy.51), channel_id=1, source_target_pairs={{0,1},{1,0},{2,3},{3,2},{4,5},{5,4},{6,7},{7,6},{8,9},{9,8},{10,11... | collective-permute-start | bytes 3145736 | tf_op jit(solution)/shard_map/ppermute | solution.py:23
  23.0 7.1 %collective-permute-start = (bf16[256,1024]{1,0:T(8,128)(2,1)}, bf16[256,1024]{1,0:T(8,128)(2,1)}, u32[]{:S(2)}, u32[]{:S(2)}) collective-permute-start(bf16[256,1024]{1,0:T(8,128)(2,1)} %fusion.47), channel_id=1, source_target_pairs={{0,1},{1,0},{2,3},{3,2},{4,5},{5,4},{6,7},{7,6},{8,9},{9,8},{10,11... | collective-permute-start | bytes 1572872 | tf_op jit(solution)/shard_map/ppermute | solution.py:23
  31.7 4.8 %copy-start.6 = (bf16[256,1024]{1,0:T(8,128)(2,1)}, bf16[256,1024]{1,0:T(8,128)(2,1)S(1)}, u32[]{:S(2)}) copy-start(bf16[256,1024]{1,0:T(8,128)(2,1)S(1)} %get-tuple-element.17) | copy-start | bytes 1572868
  31.7 4.8 %copy-start.8 = (bf16[256,1024]{1,0:T(8,128)(2,1)}, bf16[256,1024]{1,0:T(8,128)(2,1)S(1)}, u32[]{:S(2)}) copy-start(bf16[256,1024]{1,0:T(8,128)(2,1)S(1)} %get-tuple-element.18) | copy-start | bytes 1572868
  31.7 3.1 %copy-start.4 = (f32[6,1024,16]{1,0,2:T(8,128)S(1)}, f32[6,1024,16]{1,0,2:T(8,128)}, u32[]{:S(2)}) copy-start(f32[6,1024,16]{1,0,2:T(8,128)} %fusion.86) | copy-start | bytes 1179652
  90.0 1.4 copy-start.7
  90.0 1.4 copy-start.9
  90.0 1.4 copy-start.15
  90.0 1.8 %copy-start.13 = (f32[4]{0:T(128)S(1)}, f32[4]{0:T(128)}, u32[]{:S(2)}) copy-start(f32[4]{0:T(128)} %param.17) | copy-start | bytes 52
  90.0 3.8 %copy-start.5 = (bf16[3,512,512]{1,2,0:T(8,128)(2,1)S(1)}, bf16[3,512,512]{1,2,0:T(8,128)(2,1)}, u32[]{:S(2)}) copy-start(bf16[3,512,512]{1,2,0:T(8,128)(2,1)} %get-tuple-element.24) | copy-start | bytes 4718596
  90.0 4.9 %copy-start.3 = (bf16[512,512]{0,1:T(8,128)(2,1)S(1)}, bf16[512,512]{0,1:T(8,128)(2,1)}, u32[]{:S(2)}) copy-start(bf16[512,512]{0,1:T(8,128)(2,1)} %fusion.39) | copy-start | bytes 1572868
  90.0 44.9 %collective-permute-start.6 = (bf16[512,1024]{1,0:T(8,128)(2,1)}, bf16[512,1024]{1,0:T(8,128)(2,1)}, u32[]{:S(2)}, u32[]{:S(2)}) collective-permute-start(bf16[512,1024]{1,0:T(8,128)(2,1)} %param.24), channel_id=1, source_target_pairs={{0,1},{1,0},{2,3},{3,2},{4,5},{5,4},{6,7},{7,6},{8,9},{9,8},{10,11... | collective-permute-start | bytes 3145736 | tf_op jit(solution)/shard_map/ppermute | solution.py:23
  128.4 2.8 %copy-start.10 = (bf16[1,512,512]{1,2,0:T(8,128)(2,1)S(1)}, bf16[1,512,512]{1,2,0:T(8,128)(2,1)}, u32[]{:S(2)}) copy-start(bf16[1,512,512]{1,2,0:T(8,128)(2,1)} %get-tuple-element.16) | copy-start | bytes 1572868
  128.4 2.9 %copy-start.17 = (f32[4,512,512]{1,2,0:T(8,128)S(1)}, f32[4,512,512]{1,2,0:T(8,128)}, u32[]{:S(2)}) copy-start(f32[4,512,512]{1,2,0:T(8,128)} %get-tuple-element.27) | copy-start | bytes 12582916
  131.2 7.8 %slice-start = ((s8[8650752]{0:T(1024)(128)(4,1)}), s8[4194304]{0:T(1024)(128)(4,1)S(1)}, s32[]{:S(2)}) async-start(s8[8650752]{0:T(1024)(128)(4,1)} %bitcast.178), calls=%async_computation.3 | async-start | bytes 8388608
  131.3 7.7 %slice-start.1 = ((s8[8650752]{0:T(1024)(128)(4,1)}), s8[4194304]{0:T(1024)(128)(4,1)S(1)}, s32[]{:S(2)}) async-start(s8[8650752]{0:T(1024)(128)(4,1)} %bitcast.178), calls=%async_computation.4 | async-start | bytes 8388608
  131.3 7.7 %slice-start.2 = ((s8[8650752]{0:T(1024)(128)(4,1)}), s8[262144]{0:T(1024)(128)(4,1)S(1)}, s32[]{:S(2)}) async-start(s8[8650752]{0:T(1024)(128)(4,1)} %bitcast.178), calls=%async_computation.5 | async-start | bytes 524288
  131.9 3.1 %copy-start.2 = (bf16[256,1024]{1,0:T(8,128)(2,1)S(1)}, bf16[256,1024]{1,0:T(8,128)(2,1)}, u32[]{:S(2)}) copy-start(bf16[256,1024]{1,0:T(8,128)(2,1)} %param.13) | copy-start | bytes 1572868
  132.0 3.0 %collective-permute-start.5 = (bf16[256,512]{0,1:T(8,128)(2,1)S(1)}, bf16[256,512]{0,1:T(8,128)(2,1)S(1)}, u32[]{:S(2)}, u32[]{:S(2)}) collective-permute-start(bf16[256,512]{0,1:T(8,128)(2,1)S(1)} %constant_dynamic-slice_fusion), channel_id=1, source_target_pairs={{0,1},{1,0},{2,3},{3,2},{4,5},{5,4},{6,7},{7,6},{8,9},{9,8},{10,11... | collective-permute-start | bytes 786440 | tf_op jit(solution)/shard_map/ppermute | solution.py:23
  137.0 2.0 %collective-permute-start.7 = (bf16[256,1024]{1,0:T(8,128)(2,1)S(1)}, bf16[256,1024]{1,0:T(8,128)(2,1)S(1)}, u32[]{:S(2)}, u32[]{:S(2)}) collective-permute-start(bf16[256,1024]{1,0:T(8,128)(2,1)S(1)} %fusion.50), channel_id=1, source_target_pairs={{0,1},{1,0},{2,3},{3,2},{4,5},{5,4},{6,7},{7,6},{8,9},{9,8},{10,11... | collective-permute-start | bytes 1572872 | tf_op jit(solution)/shard_map/ppermute | solution.py:23
  141.8 2.7 %collective-permute-start.8 = (f32[256,1024]{1,0:T(8,128)S(1)}, f32[256,1024]{1,0:T(8,128)S(1)}, u32[]{:S(2)}, u32[]{:S(2)}) collective-permute-start(f32[256,1024]{1,0:T(8,128)S(1)} %fusion.13), channel_id=1, source_target_pairs={{0,1},{1,0},{2,3},{3,2},{4,5},{5,4},{6,7},{7,6},{8,9},{9,8},{10,11... | collective-permute-start | bytes 3145736 | tf_op jit(solution)/shard_map/ppermute | solution.py:23
  144.5 1.9 %copy-start.1 = (bf16[3,1024,512]{2,1,0:T(8,128)(2,1)S(1)}, bf16[3,1024,512]{2,1,0:T(8,128)(2,1)}, u32[]{:S(2)}) copy-start(bf16[3,1024,512]{2,1,0:T(8,128)(2,1)} %param.15) | copy-start | bytes 9437188
Sparse Core Ops, SparseCore 0:
  9.5 73.8 all-gather.1
  90.1 38.2 reduce-scatter.1

commit v8 on v7

--- a/solution.py
+++ b/solution.py
@@ -146,7 +146,8 @@
     picked = jnp.take(plane, jnp.clip(local, 0, per_plane - 1).reshape(-1), axis=0)
     keep = valid.reshape(-1).astype(plane.dtype)[:, None, None, None]
     slots = (picked * keep).reshape((z_count, -1) + plane.shape[1:])
-    states = lax.psum_scatter(slots, "z", scatter_dimension=0, tiled=True)[0]
+    received = lax.all_to_all(slots, "z", 0, 0, tiled=True)
+    states = jnp.sum(received.astype(jnp.float32), axis=0).astype(jnp.bfloat16)
     keys = projected[1].astype(jnp.bfloat16).reshape(group, local_heads, head_size)
     values = projected[2].astype(jnp.bfloat16).reshape(group, local_heads, head_size)
     gate_terms = jnp.einsum(

time: 154 us -> 165 us (1.071)
  waiting for transfers between devices: 70 us -> 54.4 us
  other arithmetic: 11.2 us -> 23.2 us
  local copies, waits for them, and re-layouts: 13 us -> 20.3 us
  starting transfers between devices: 10.1 us -> 16.3 us
    reduce_scatter x1 -> x0, waiting for transfers between devices: 22 us -> none  [on_device(): states = lax.psum_scatter(slots, 'z', scatter_dimension=0, tiled=True)[0]]
    all_to_all x0 -> x1, waiting for transfers between devices: none -> 19.8 us  [on_device(): received = lax.all_to_all(slots, 'z', 0, 0, tiled=True)]
    all_gather x1, waiting for transfers between devices: 45.3 us -> 31.8 us  [on_device(): lax.all_gather(jnp.swapaxes(caches, -1, -2), ('y', 'x'), axis=0, tiled=True)]
    all_to_all x0 -> x1, starting transfers between devices: none -> 4.28 us  [on_device(): received = lax.all_to_all(slots, 'z', 0, 0, tiled=True)]
    gather x1 -> x2, local copies, waits for them, and re-layouts: 4.53 us -> 7.51 us  [on_device(): jnp.take(plane, jnp.clip(local, 0, per_plane - 1).reshape(-1), axis=0)]
    ppermute x6, starting transfers between devices: 3.44 us -> 5.4 us  [swap(): return lax.ppermute(value, 'col', perm=[(0, 1), (1, 0)])]
    mul x1, other arithmetic: 2.04 us -> 3.96 us  [on_device(): slots = (picked * keep).reshape((z_count, -1) + plane.shape[1:])]
    dot_general x1, matrix products: 2.28 us -> 0.48 us  [on_device(): jnp.dot(head_own, head_output_weight, preferred_element_type=jnp.float32)]
  transfers between devices with their start and end apart: 11 -> 11, of which waited for: 4 -> 5; matrix products, arithmetic and copies ran while one was open for 29% -> 42% of each run, Pallas kernels for 0% -> 0%
where the time goes in v8:
time: 165 us; the launch traced here: 164 us
  waiting for transfers between devices  54.4 us (33%)
  matrix products  36.1 us (22%)
  other arithmetic  23.2 us (14%)
  local copies, waits for them, and re-layouts  20.3 us (12%)
  starting transfers between devices  16.3 us (10%)
  between operations  13.8 us (8%)
    all_gather x1, waiting for transfers between devices, on_device(): lax.all_gather(jnp.swapaxes(caches, -1, -2), ('y', 'x'), axis=0, tiled=True)  31.8 us
    all_to_all x1, waiting for transfers between devices, on_device(): received = lax.all_to_all(slots, 'z', 0, 0, tiled=True)  19.8 us
    gather x2, local copies, waits for them, and re-layouts, on_device(): jnp.take(plane, jnp.clip(local, 0, per_plane - 1).reshape(-1), axis=0)  7.51 us
    unnamed x67, local copies, waits for them, and re-layouts  6.63 us
    ppermute x3, starting transfers between devices, along_z(): lax.ppermute(value, 'z', perm=[(i, (i + d) % z_count) for i in range(z_co...  6.57 us
    ppermute x6, starting transfers between devices, swap(): return lax.ppermute(value, 'col', perm=[(0, 1), (1, 0)])  5.4 us
    sub x1, matrix products, on_device(): weights = jnp.exp(masked - peak)  4.81 us
    dot_general x1, matrix products, on_device(): jnp.einsum('td,kdc->ktc', gathered, query_key_value_weight, preferred_ele...  4.3 us
  transfers between devices with their start and end apart: 11, of which 5 were waited for; matrix products, arithmetic and copies ran while one was open for 42% of the time, Pallas kernels for 0%

profile of v8, /device:TPU:1, one launch (start us, length us, event | category | flops | bytes accessed | tf_op | source)
XLA Modules:
  0.0 164.0 jit_solution(10112191021650705073)
XLA Ops:
  6.6 2.2 %copy.49 = bf16[4,4,128,128]{2,3,1,0:T(8,128)(2,1)} copy(bf16[4,4,128,128]{3,2,1,0:T(8,128)(2,1)} %param.23) | data formatting | bytes 1048576 | tf_op args[10]
  8.8 2.5 %collective-permute-start.2 = (s32[6]{0:T(128)}, s32[6]{0:T(128)}, u32[]{:S(2)}, u32[]{:S(2)}) collective-permute-start(s32[6]{0:T(128)} %bitcast.167), channel_id=1, source_target_pairs={{0,32},{32,64},{64,96},{96,0},{1,33},{33,65},{65,97},{97,1},{2,34}... | collective-permute-start | bytes 80 | tf_op jit(solution)/shard_map/ppermute | solution.py:140
  11.4 3.3 %collective-permute-start.3 = (s32[6]{0:T(128)}, s32[6]{0:T(128)}, u32[]{:S(2)}, u32[]{:S(2)}) collective-permute-start(s32[6]{0:T(128)} %bitcast.168), channel_id=1, source_target_pairs={{0,64},{32,96},{64,0},{96,32},{1,65},{33,97},{65,1},{97,33},{2,66}... | collective-permute-start | bytes 80 | tf_op jit(solution)/shard_map/ppermute | solution.py:140
  14.7 0.7 collective-permute-start.4
  15.4 2.8 %copy.50 = bf16[32,1024,16]{1,0,2:T(8,128)(2,1)} copy(bf16[32,1024,16]{1,2,0:T(8,128)(2,1)} %param.18) | data formatting | bytes 2097152 | tf_op args[5]
  18.2 1.5 collective-permute-start.1
  19.7 1.2 fusion.44
  20.9 0.6 fusion.112
  21.5 2.1 %fusion.46 = bf16[256,1024]{1,0:T(8,128)(2,1)} fusion(bf16[256,1024]{1,0:T(8,128)(2,1)} %param.13, f32[1024]{0:T(1024)S(1)} %bitcast.157, f32[256]{0:T(256)S(1)} %add_rsqrt_fusion.2), kind=kLoop, calls=%fused_computation.59 | loop fusion | flops 1048576 | bytes 1053696 | tf_op jit(solution)/shard_map/convert_element_type | solution.py:19
  23.7 0.2 reduce-window.14
  23.9 0.6 compare_and_fusion.1
  24.5 0.5 iota_add_fusion
  25.1 0.6 pad_clamp_fusion.1
  25.7 0.7 fusion.71
  26.4 0.7 fusion.70
  27.1 0.2 fusion.53
  27.3 2.4 %convolution_convert_fusion = bf16[6,16,512]{2,0,1:T(8,128)(2,1)S(1)} fusion(bf16[64,16,512]{2,1,0:T(8,128)(2,1)} %param.19, s32[6]{0:T(128)S(1)} %bitcast.162), kind=kOutput, calls=%fused_computation.55 | convolution fusion | flops 6340992 | bytes 1146904 | tf_op jit(solution)/shard_map/gq,qjl->gjl/dot_general | solution.py:127
  29.8 3.3 %fusion.84 = f32[6,1024,16]{1,0,2:T(8,128)} fusion(s32[32]{0:T(128)S(1)} %iota_add_fusion.1, s32[6]{0:T(128)S(1)} %bitcast.163, bf16[32,1024,16]{1,2,0:T(8,128)(2,1)} %param.18), kind=kOutput, calls=%fused_computation.120 | convolution fusion | flops 6291648 | bytes 1441944 | tf_op jit(solution)/shard_map/sa,adr->sdr/dot_general | solution.py:117
  33.0 0.5 collective-permute-start.6
  33.5 0.7 pad_add_fusion
  34.2 0.7 gather_fusion
  34.9 1.3 compare_and_fusion
  36.3 0.6 pad_clamp_fusion
  36.9 1.5 broadcast_select_fusion.1
  38.5 0.8 copy-done.6
  39.2 1.1 convolution_bitcast_fusion.3
  40.3 0.6 copy-done.16
  40.9 0.7 fusion.108
  41.7 1.2 reduce-window.18
  42.9 0.2 slice_reduce_fusion
  43.1 0.8 reduce-window.19
  43.9 4.3 %fusion.113 = (bf16[3,512,512]{1,2,0:T(8,128)(2,1)}, f32[3,512,512]{1,2,0:T(8,128)S(1)}) fusion(bf16[3,1024,512]{2,1,0:T(8,128)(2,1)S(1)} %copy-done, bf16[256,1024]{1,0:T(8,128)(2,1)} %copy-done.8, bf16[256,1024]{1,0:T(8,128)(2,1)} %copy-done.6), kind=kOutput, calls=%fused_computation.168 | convolution fusion | flops 1613496320 | bytes 8912896 | tf_op jit(solution)/shard_map/td,kdc->ktc/dot_general | solution.py:107
  48.2 1.5 fusion.43
  49.8 0.1 copy.52
  49.9 0.5 fusion.62
  50.4 1.1 fusion.38
  51.6 31.8 %all-gather.2.cloned.1.call-done = bf16[64,4,128,128]{3,2,1,0:T(8,128)(2,1)} async-done(((bf16[4,4,128,128]{3,2,1,0:T(8,128)(2,1)}), bf16[64,4,128,128]{3,2,1,0:T(8,128)(2,1)}) %all-gather.2.cloned.1.call-update) | async-done | bytes 8388624 | tf_op jit(solution)/shard_map/all_gather | solution.py:95
  83.4 4.7 %gather_fusion.1 = bf16[24,4,128,128]{3,2,1,0:T(8,128)(2,1)S(1)} fusion(bf16[64,4,128,128]{3,2,1,0:T(8,128)(2,1)} %all-gather.2.cloned.1.call-done, s32[1024]{0:T(1024)} %pad_clamp_fusion), kind=kCustom, calls=%fused_computation.1 | custom fusion | bytes 6291552 | tf_op jit(solution)/shard_map/jit(_take)/gather | solution.py:146
  88.1 2.9 %copy.60 = bf16[4,6,4,128,128]{3,4,2,1,0:T(8,128)(2,1)} copy(bf16[4,6,4,128,128]{4,3,2,1,0:T(8,128)(2,1)S(1)} %bitcast.144) | data formatting | bytes 6291456 | tf_op jit(solution)/shard_map/jit(_take)/gather | solution.py:146
  90.9 4.0 %select_multiply_fusion = bf16[4,6,4,128,128]{3,4,2,1,0:T(8,128)(2,1)} fusion(bf16[4,6,4,128,128]{3,4,2,1,0:T(8,128)(2,1)} %copy.60, pred[4,6]{1,0:T(4,128)(4,1)S(1)} %copy-done.24, bf16[4,6]{1,0:T(4,128)(2,1)S(1)} %copy-done.23), kind=kLoop, calls=%fused_computation.14 | loop fusion | flops 3145728 | bytes 6291528 | tf_op jit(solution)/shard_map/mul | solution.py:148
  94.9 4.3 %all-to-all-start = ((bf16[4,6,4,128,128]{3,4,2,1,0:T(8,128)(2,1)}), bf16[4,6,4,128,128]{3,4,2,1,0:T(8,128)(2,1)S(1)}, u32[]{:S(2)}, u32[]{:S(2)}) async-start(bf16[4,6,4,128,128]{3,4,2,1,0:T(8,128)(2,1)} %select_multiply_fusion), calls=%async_computation | async-start | bytes 6291456 | tf_op jit(solution)/shard_map/all_to_all | solution.py:149
  99.4 0.1 multiply_reduce_fusion.3
  99.6 2.3 %fusion.111 = (bf16[1,512,512]{1,2,0:T(8,128)(2,1)}, bf16[1,512,512]{1,2,0:T(8,128)(2,1)}) fusion(bf16[3,512,512]{1,2,0:T(8,128)(2,1)} %get-tuple-element.24), kind=kLoop, calls=%fused_computation.166 | loop fusion | bytes 2097152 | tf_op jit(solution)/shard_map/slice | solution.py:151
  101.9 2.0 %copy.58 = bf16[512,4,128]{2,0,1:T(8,128)(2,1)} copy(bf16[512,4,128]{0,2,1:T(8,128)(2,1)} %bitcast.145) | data formatting | bytes 1048576 | tf_op jit(solution)/shard_map/optimization_barrier | solution.py:133
  103.9 3.2 %broadcast_multiply_fusion = bf16[512,6,4,128]{3,0,2,1:T(8,128)(2,1)} fusion(bf16[512,6]{0,1:T(8,128)(2,1)S(1)} %copy-done.12, bf16[512,4,128]{2,0,1:T(8,128)(2,1)} %copy.58), kind=kLoop, calls=%fused_computation.31 | loop fusion | flops 1572864 | bytes 3676160 | tf_op jit(solution)/shard_map/mul | solution.py:163
  107.1 4.8 %fusion.114 = (f32[4,512]{1,0:T(4,128)S(1)}, f32[4,512,512]{1,2,0:T(8,128)}) fusion(pred[512,512]{0,1:T(8,128)(4,1)S(1)} %fusion.53, bf16[512,4,128]{0,2,1:T(8,128)(2,1)} %bitcast.146, bf16[512,4,128]{0,2,1:T(8,128)(2,1)} %bitcast.153), kind=kOutput, calls=%fused_computation.169 | convolution fusion | flops 272630272 | bytes 5513216 | tf_op jit(solution)/shard_map/sub | solution.py:174
  111.9 4.2 %fusion.27 = f32[512,4,128]{0,2,1:T(8,128)} fusion(bf16[512,4,128]{0,2,1:T(8,128)(2,1)} %bitcast.151, f32[4,512]{1,0:T(4,128)S(1)} %bitcast.161, pred[512,512]{0,1:T(8,128)(4,1)S(1)} %fusion.53, bf16[512,4,128]{0,2,1:T(8,128)(2,1)} %bitcast.147, bf16[512,4,128]{0,2,1:T(8,128)(2,1)} %bitcast.154), kind=kOutput, calls=%fused_computation.40 | convolution fusion | flops 542113792 | bytes 2891776 | tf_op jit(solution)/shard_map/hqk,khd->qhd/dot_general | solution.py:179
  116.1 19.8 %all-to-all-done = bf16[4,6,4,128,128]{3,4,2,1,0:T(8,128)(2,1)S(1)} async-done(((bf16[4,6,4,128,128]{3,4,2,1,0:T(8,128)(2,1)}), bf16[4,6,4,128,128]{3,4,2,1,0:T(8,128)(2,1)S(1)}, u32[]{:S(2)}, u32[]{:S(2)}) %all-to-all-start) | async-done | bytes 3145760 | tf_op jit(solution)/shard_map/all_to_all | solution.py:149
  135.9 1.7 %reduce_sum.88 = bf16[6,4,128,128]{2,3,1,0:T(8,128)(2,1)} reduce(bf16[4,6,4,128,128]{3,4,2,1,0:T(8,128)(2,1)S(1)} %all-to-all-done, bf16[]{:T(256)} %constant.96.clone.1), dimensions={0}, to_apply=%region_8.9 | reduce | flops 1179648 | bytes 3932162 | tf_op jit(solution)/shard_map/reduce_sum | solution.py:150
  137.6 3.7 %multiply_reduce_fusion = (f32[512,4]{0,1:T(4,128)S(1)}, f32[512,4,128]{0,2,1:T(8,128)S(1)}) fusion(f32[512,4,128]{0,2,1:T(8,128)} %fusion.27, f32[512,4]{0,1:T(4,128)S(1)} %fusion.79, bf16[6,4,128,128]{2,3,1,0:T(8,128)(2,1)} %reduce_sum.88, bf16[512,6,4,128]{3,0,2,1:T(8,128)(2,1)} %broadcast_multiply_fusion), kind=kOutput, calls=%fused_computation.68 | convolution fusion | flops 403699712 | bytes 6045696 | tf_op jit(solution)/shard_map/tshi,shji->thj/dot_general | solution.py:165
  141.4 0.6 fusion.37
  142.1 1.9 %collective-permute-start.5 = (bf16[256,512]{0,1:T(8,128)(2,1)S(1)}, bf16[256,512]{0,1:T(8,128)(2,1)S(1)}, u32[]{:S(2)}, u32[]{:S(2)}) collective-permute-start(bf16[256,512]{0,1:T(8,128)(2,1)S(1)} %constant_dynamic-slice_fusion), channel_id=1, source_target_pairs={{0,1},{1,0},{2,3},{3,2},{4,5},{5,4},{6,7},{7,6},{8,9},{9,8},{10,11... | collective-permute-start | bytes 786440 | tf_op jit(solution)/shard_map/ppermute | solution.py:23
  144.0 0.5 fusion.63
  144.5 0.7 collective-permute-done.5
  145.2 1.8 %fusion.47 = (f32[256]{0:T(256)S(1)}, bf16[256,1024]{1,0:T(8,128)(2,1)S(1)}) fusion(f32[256,1024]{1,0:T(8,128)S(1)} %fusion.63, bf16[256,512]{0,1:T(8,128)(2,1)S(1)} %collective-permute-done.5, bf16[512,1024]{1,0:T(8,128)(2,1)} %collective-permute-done.6, bf16[256,1024]{1,0:T(8,128)(2,1)S(1)} %copy-done.2), kind=kOutput, calls=%fused_computation.60 | convolution fusion | flops 270270208 | bytes 3408896 | tf_op jit(solution)/shard_map/dot_general | solution.py:187
  147.0 0.2 fusion.49
  147.2 1.0 collective-permute-start.7
  148.2 1.5 collective-permute-done.7
  149.8 1.7 %fusion.8 = f32[2,256,1408]{2,1,0:T(8,128)S(1)} fusion(bf16[3,1024,1408]{2,1,0:T(8,128)(2,1)S(1)} %bitcast.171, bf16[256,1024]{1,0:T(8,128)(2,1)S(1)} %collective-permute-done.7), kind=kOutput, calls=%fused_computation.12 | convolution fusion | flops 1476395008 | bytes 9175040 | tf_op jit(solution)/shard_map/td,kdf->ktf/dot_general | solution.py:194
  151.5 1.0 fusion.12
  152.5 0.5 collective-permute-start.8
  153.0 1.7 %fusion.5 = f32[2,256,1408]{2,1,0:T(8,128)S(1)} fusion(bf16[3,1024,1408]{2,1,0:T(8,128)(2,1)S(1)} %bitcast.171, bf16[256,1024]{1,0:T(8,128)(2,1)S(1)} %fusion.49), kind=kOutput, calls=%fused_computation.11 | convolution fusion | flops 1476395008 | bytes 9175040 | tf_op jit(solution)/shard_map/td,kdf->ktf/dot_general | solution.py:194
  154.7 0.6 collective-permute-done.8
  155.3 1.8 %fusion.40 = bf16[256,1024]{1,0:T(8,128)(2,1)} fusion(f32[256,1024]{1,0:T(8,128)S(1)} %collective-permute-done.8, bf16[3,1024,1408]{2,1,0:T(8,128)(2,1)S(1)} %bitcast.171, bf16[256,1024]{1,0:T(8,128)(2,1)S(1)} %get-tuple-element.31, f32[2,256,1408]{2,1,0:T(8,128)S(1)} %fusion.5), kind=kOutput, calls=%fused_computation.52 | convolution fusion | flops 741408768 | bytes 7864320 | tf_op jit(solution)/shard_map/tf,df->td/dot_general | solution.py:198
  (92 shorter events, 1.1 us)
Async XLA Ops:
  6.5 37.3 %copy-start = (bf16[3,1024,512]{2,1,0:T(8,128)(2,1)S(1)}, bf16[3,1024,512]{2,1,0:T(8,128)(2,1)}, u32[]{:S(2)}) copy-start(bf16[3,1024,512]{2,1,0:T(8,128)(2,1)} %param.15) | copy-start | bytes 9437188
  6.5 14.4 %copy-start.20 = (f32[2,1024]{1,0:T(2,128)S(1)}, f32[2,1024]{1,0:T(2,128)}, u32[]{:S(2)}) copy-start(f32[2,1024]{1,0:T(2,128)} %param.14) | copy-start | bytes 24580
  6.5 17.0 %copy-start.27 = (s32[1,2,3]{2,1,0:T(2,128)S(1)}, s32[1,2,3]{2,1,0:T(2,128)}, u32[]{:S(2)}) copy-start(s32[1,2,3]{2,1,0:T(2,128)} %param.20) | copy-start | bytes 76
  6.5 20.8 %copy-start.21 = (s32[1,6]{1,0:T(1,128)S(1)}, s32[1,6]{1,0:T(1,128)}, u32[]{:S(2)}) copy-start(s32[1,6]{1,0:T(1,128)} %param.21) | copy-start | bytes 76
  6.5 76.9 %all-gather.2.cloned.1.call-start = ((), (), s32[]{:S(2)}) async-start(), calls=%async_computation.1 | async-start | bytes 8912896 | tf_op jit(solution)/shard_map/all_gather | solution.py:95
  8.8 24.2 %collective-permute-start.2 = (s32[6]{0:T(128)}, s32[6]{0:T(128)}, u32[]{:S(2)}, u32[]{:S(2)}) collective-permute-start(s32[6]{0:T(128)} %bitcast.167), channel_id=1, source_target_pairs={{0,32},{32,64},{64,96},{96,0},{1,33},{33,65},{65,97},{97,1},{2,34}... | collective-permute-start | bytes 80 | tf_op jit(solution)/shard_map/ppermute | solution.py:140
  11.4 22.2 %collective-permute-start.3 = (s32[6]{0:T(128)}, s32[6]{0:T(128)}, u32[]{:S(2)}, u32[]{:S(2)}) collective-permute-start(s32[6]{0:T(128)} %bitcast.168), channel_id=1, source_target_pairs={{0,64},{32,96},{64,0},{96,32},{1,65},{33,97},{65,1},{97,33},{2,66}... | collective-permute-start | bytes 80 | tf_op jit(solution)/shard_map/ppermute | solution.py:140
  14.7 18.9 %collective-permute-start.4 = (s32[6]{0:T(128)}, s32[6]{0:T(128)}, u32[]{:S(2)}, u32[]{:S(2)}) collective-permute-start(s32[6]{0:T(128)} %bitcast.169), channel_id=1, source_target_pairs={{0,96},{32,0},{64,32},{96,64},{1,97},{33,1},{65,33},{97,65},{2,98}... | collective-permute-start | bytes 80 | tf_op jit(solution)/shard_map/ppermute | solution.py:140
  18.2 30.0 %collective-permute-start.1 = (bf16[32,1024,16]{1,0,2:T(8,128)(2,1)}, bf16[32,1024,16]{1,0,2:T(8,128)(2,1)}, u32[]{:S(2)}, u32[]{:S(2)}) collective-permute-start(bf16[32,1024,16]{1,0,2:T(8,128)(2,1)} %copy.50), channel_id=1, source_target_pairs={{0,1},{1,0},{2,3},{3,2},{4,5},{5,4},{6,7},{7,6},{8,9},{9,8},{10,11... | collective-permute-start | bytes 3145736 | tf_op jit(solution)/shard_map/ppermute | solution.py:23
  23.6 13.3 %collective-permute-start = (bf16[256,1024]{1,0:T(8,128)(2,1)}, bf16[256,1024]{1,0:T(8,128)(2,1)}, u32[]{:S(2)}, u32[]{:S(2)}) collective-permute-start(bf16[256,1024]{1,0:T(8,128)(2,1)} %fusion.46), channel_id=1, source_target_pairs={{0,1},{1,0},{2,3},{3,2},{4,5},{5,4},{6,7},{7,6},{8,9},{9,8},{10,11... | collective-permute-start | bytes 1572872 | tf_op jit(solution)/shard_map/ppermute | solution.py:23
  33.0 111.5 %collective-permute-start.6 = (bf16[512,1024]{1,0:T(8,128)(2,1)}, bf16[512,1024]{1,0:T(8,128)(2,1)}, u32[]{:S(2)}, u32[]{:S(2)}) collective-permute-start(bf16[512,1024]{1,0:T(8,128)(2,1)} %param.24), channel_id=1, source_target_pairs={{0,1},{1,0},{2,3},{3,2},{4,5},{5,4},{6,7},{7,6},{8,9},{9,8},{10,11... | collective-permute-start | bytes 3145736 | tf_op jit(solution)/shard_map/ppermute | solution.py:23
  38.4 0.8 copy-start.6
  38.5 1.9 %copy-start.8 = (bf16[256,1024]{1,0:T(8,128)(2,1)}, bf16[256,1024]{1,0:T(8,128)(2,1)S(1)}, u32[]{:S(2)}) copy-start(bf16[256,1024]{1,0:T(8,128)(2,1)S(1)} %get-tuple-element.18) | copy-start | bytes 1572868
  40.3 0.6 copy-start.16
  42.9 0.9 copy-start.13
  43.9 4.4 %copy-start.3 = (f32[6,1024,16]{1,0,2:T(8,128)S(1)}, f32[6,1024,16]{1,0,2:T(8,128)}, u32[]{:S(2)}) copy-start(f32[6,1024,16]{1,0,2:T(8,128)} %fusion.84) | copy-start | bytes 1179652
  43.9 4.4 %copy-start.22 = (s32[1,6]{1,0:T(1,128)S(1)}, s32[1,6]{1,0:T(1,128)}, u32[]{:S(2)}) copy-start(s32[1,6]{1,0:T(1,128)} %param.21) | copy-start | bytes 76
  43.9 4.4 %copy-start.26 = (s32[32]{0:T(128)S(1)}, s32[32]{0:T(128)}, u32[]{:S(2)}) copy-start(s32[32]{0:T(128)} %iota_add_fusion) | copy-start | bytes 388
  43.9 6.0 %copy-start.7 = (bf16[256,1024]{1,0:T(8,128)(2,1)S(1)}, bf16[256,1024]{1,0:T(8,128)(2,1)}, u32[]{:S(2)}) copy-start(bf16[256,1024]{1,0:T(8,128)(2,1)} %copy-done.6) | copy-start | bytes 1572868
  43.9 6.0 %copy-start.9 = (bf16[256,1024]{1,0:T(8,128)(2,1)S(1)}, bf16[256,1024]{1,0:T(8,128)(2,1)}, u32[]{:S(2)}) copy-start(bf16[256,1024]{1,0:T(8,128)(2,1)} %copy-done.8) | copy-start | bytes 1572868
  48.2 2.2 %copy-start.10 = (f32[512,6]{0,1:T(8,128)S(1)}, f32[512,6]{0,1:T(8,128)}, u32[]{:S(2)}) copy-start(f32[512,6]{0,1:T(8,128)} %get-tuple-element.22) | copy-start | bytes 36868
  48.2 2.2 %copy-start.11 = (bf16[512,6]{0,1:T(8,128)(2,1)S(1)}, bf16[512,6]{0,1:T(8,128)(2,1)}, u32[]{:S(2)}) copy-start(bf16[512,6]{0,1:T(8,128)(2,1)} %get-tuple-element.23) | copy-start | bytes 18436
  88.1 2.9 %copy-start.23 = (bf16[4,6]{1,0:T(4,128)(2,1)S(1)}, bf16[4,6]{1,0:T(4,128)(2,1)}, u32[]{:S(2)}) copy-start(bf16[4,6]{1,0:T(4,128)(2,1)} %get-tuple-element.21) | copy-start | bytes 148
  88.1 2.9 %copy-start.24 = (pred[4,6]{1,0:T(4,128)(4,1)S(1)}, pred[4,6]{1,0:T(4,128)(4,1)}, u32[]{:S(2)}) copy-start(pred[4,6]{1,0:T(4,128)(4,1)} %get-tuple-element.13) | copy-start | bytes 76
  94.9 4.3 %copy-start.14 = (f32[4,4,128]{2,1,0:T(4,128)S(1)}, f32[4,4,128]{2,1,0:T(4,128)}, u32[]{:S(2)}) copy-start(f32[4,4,128]{2,1,0:T(4,128)} %copy-done.13) | copy-start | bytes 24580
  94.9 4.3 %copy-start.19 = (f32[4,5]{1,0:T(4,128)S(1)}, f32[4,5]{1,0:T(4,128)}, u32[]{:S(2)}) copy-start(f32[4,5]{1,0:T(4,128)} %reduce-window.19) | copy-start | bytes 244
  94.9 4.4 %copy-start.17 = (f32[2,512,4]{1,2,0:T(4,128)S(1)}, f32[2,512,4]{1,2,0:T(4,128)}, u32[]{:S(2)}) copy-start(f32[2,512,4]{1,2,0:T(4,128)} %copy-done.16) | copy-start | bytes 49156
  94.9 4.4 %copy-start.25 = (f32[4]{0:T(128)S(1)}, f32[4]{0:T(128)}, u32[]{:S(2)}) copy-start(f32[4]{0:T(128)} %param.17) | copy-start | bytes 52
  94.9 4.5 %copy-start.15 = (f32[6,512]{1,0:T(8,128)S(1)}, f32[6,512]{1,0:T(8,128)}, u32[]{:S(2)}) copy-start(f32[6,512]{1,0:T(8,128)} %fusion.71) | copy-start | bytes 36868
  94.9 40.9 %all-to-all-start = ((bf16[4,6,4,128,128]{3,4,2,1,0:T(8,128)(2,1)}), bf16[4,6,4,128,128]{3,4,2,1,0:T(8,128)(2,1)S(1)}, u32[]{:S(2)}, u32[]{:S(2)}) async-start(bf16[4,6,4,128,128]{3,4,2,1,0:T(8,128)(2,1)} %select_multiply_fusion), calls=%async_computation | async-start | bytes 6291456 | tf_op jit(solution)/shard_map/all_to_all | solution.py:149
  99.2 4.7 %copy-start.12 = (bf16[512,6]{0,1:T(8,128)(2,1)S(1)}, bf16[512,6]{0,1:T(8,128)(2,1)}, u32[]{:S(2)}) copy-start(bf16[512,6]{0,1:T(8,128)(2,1)} %get-tuple-element.23) | copy-start | bytes 18436
  137.6 3.8 %copy-start.5 = (bf16[1,512,512]{1,2,0:T(8,128)(2,1)S(1)}, bf16[1,512,512]{1,2,0:T(8,128)(2,1)}, u32[]{:S(2)}) copy-start(bf16[1,512,512]{1,2,0:T(8,128)(2,1)} %get-tuple-element.16) | copy-start | bytes 1572868
  137.6 3.8 %copy-start.28 = (f32[4,512,512]{1,2,0:T(8,128)S(1)}, f32[4,512,512]{1,2,0:T(8,128)}, u32[]{:S(2)}) copy-start(f32[4,512,512]{1,2,0:T(8,128)} %get-tuple-element.27) | copy-start | bytes 12582916
  141.3 8.5 %slice-start = ((s8[8650752]{0:T(1024)(128)(4,1)}), s8[4194304]{0:T(1024)(128)(4,1)S(1)}, s32[]{:S(2)}) async-start(s8[8650752]{0:T(1024)(128)(4,1)} %bitcast.170), calls=%async_computation.2 | async-start | bytes 8388608
  141.4 2.6 %copy-start.4 = (bf16[512,1024]{1,0:T(8,128)(2,1)S(1)}, bf16[512,1024]{1,0:T(8,128)(2,1)}, u32[]{:S(2)}) copy-start(bf16[512,1024]{1,0:T(8,128)(2,1)} %param.24) | copy-start | bytes 3145732
  141.4 8.4 %slice-start.1 = ((s8[8650752]{0:T(1024)(128)(4,1)}), s8[4194304]{0:T(1024)(128)(4,1)S(1)}, s32[]{:S(2)}) async-start(s8[8650752]{0:T(1024)(128)(4,1)} %bitcast.170), calls=%async_computation.3 | async-start | bytes 8388608
  141.4 8.4 %slice-start.2 = ((s8[8650752]{0:T(1024)(128)(4,1)}), s8[262144]{0:T(1024)(128)(4,1)S(1)}, s32[]{:S(2)}) async-start(s8[8650752]{0:T(1024)(128)(4,1)} %bitcast.170), calls=%async_computation.4 | async-start | bytes 524288
  142.0 3.2 %copy-start.2 = (bf16[256,1024]{1,0:T(8,128)(2,1)S(1)}, bf16[256,1024]{1,0:T(8,128)(2,1)}, u32[]{:S(2)}) copy-start(bf16[256,1024]{1,0:T(8,128)(2,1)} %param.13) | copy-start | bytes 1572868
  142.0 5.0 %copy-start.18 = (f32[1,1024]{1,0:T(1,128)S(1)}, f32[1,1024]{1,0:T(1,128)}, u32[]{:S(2)}) copy-start(f32[1,1024]{1,0:T(1,128)} %get-tuple-element.19) | copy-start | bytes 12292
  142.1 3.1 %collective-permute-start.5 = (bf16[256,512]{0,1:T(8,128)(2,1)S(1)}, bf16[256,512]{0,1:T(8,128)(2,1)S(1)}, u32[]{:S(2)}, u32[]{:S(2)}) collective-permute-start(bf16[256,512]{0,1:T(8,128)(2,1)S(1)} %constant_dynamic-slice_fusion), channel_id=1, source_target_pairs={{0,1},{1,0},{2,3},{3,2},{4,5},{5,4},{6,7},{7,6},{8,9},{9,8},{10,11... | collective-permute-start | bytes 786440 | tf_op jit(solution)/shard_map/ppermute | solution.py:23
  147.2 2.5 %collective-permute-start.7 = (bf16[256,1024]{1,0:T(8,128)(2,1)S(1)}, bf16[256,1024]{1,0:T(8,128)(2,1)S(1)}, u32[]{:S(2)}, u32[]{:S(2)}) collective-permute-start(bf16[256,1024]{1,0:T(8,128)(2,1)S(1)} %fusion.49), channel_id=1, source_target_pairs={{0,1},{1,0},{2,3},{3,2},{4,5},{5,4},{6,7},{7,6},{8,9},{9,8},{10,11... | collective-permute-start | bytes 1572872 | tf_op jit(solution)/shard_map/ppermute | solution.py:23
  152.5 2.7 %collective-permute-start.8 = (f32[256,1024]{1,0:T(8,128)S(1)}, f32[256,1024]{1,0:T(8,128)S(1)}, u32[]{:S(2)}, u32[]{:S(2)}) collective-permute-start(f32[256,1024]{1,0:T(8,128)S(1)} %fusion.12), channel_id=1, source_target_pairs={{0,1},{1,0},{2,3},{3,2},{4,5},{5,4},{6,7},{7,6},{8,9},{9,8},{10,11... | collective-permute-start | bytes 3145736 | tf_op jit(solution)/shard_map/ppermute | solution.py:23
  155.3 1.9 %copy-start.1 = (bf16[3,1024,512]{2,1,0:T(8,128)(2,1)S(1)}, bf16[3,1024,512]{2,1,0:T(8,128)(2,1)}, u32[]{:S(2)}) copy-start(bf16[3,1024,512]{2,1,0:T(8,128)(2,1)} %param.15) | copy-start | bytes 9437188
Sparse Core Ops, SparseCore 0:
  9.5 73.8 all-gather.1

commit v9 on v7

--- a/solution.py
+++ b/solution.py
@@ -198,8 +198,11 @@
             "tf,df->td", hidden, feedforward_weight[2], preferred_element_type=jnp.float32
         )
 
-    from_partner = swap(feed_part(swap(normed_two)))
-    feed = feed_part(normed_two) + from_partner
+    half = normed_two.shape[0] // 2
+    own_first = feed_part(normed_two[:half])
+    own_first, partner_two = lax.optimization_barrier((own_first, swap(normed_two)))
+    from_partner = swap(feed_part(partner_two))
+    feed = jnp.concatenate([own_first, feed_part(normed_two[half:])], axis=0) + from_partner
     return (mixed.astype(jnp.float32) + feed).astype(jnp.bfloat16)
 
 

time: 154 us -> 153 us (level)
  waiting for transfers between devices: 70 us -> 67.5 us
    ppermute x6, waiting for transfers between devices: 2.74 us -> 0.29 us  [swap(): return lax.ppermute(value, 'col', perm=[(0, 1), (1, 0)])]
    dot_general x2 -> x3, matrix products: 2.85 us -> 3.15 us  [feed_part(): jnp.einsum('tf,df->td', hidden, feedforward_weight[2], preferred_element_...]
    dot_general x2 -> x3, matrix products: 3.4 us -> 3.53 us  [feed_part(): jnp.einsum('td,kdf->ktf', rows, feedforward_weight[:2], preferred_element...]
  transfers between devices with their start and end apart: 11 -> 11, of which waited for: 4 -> 3; matrix products, arithmetic and copies ran while one was open for 29% -> 30% of each run, Pallas kernels for 0% -> 0%
where the time goes in v9:
time: 153 us
  waiting for transfers between devices  67.5 us (44%)
  matrix products  35.6 us (23%)
  between operations  13.9 us (9%)
  local copies, waits for them, and re-layouts  12.9 us (8%)
  other arithmetic  12.3 us (8%)
  starting transfers between devices  10.4 us (7%)
    all_gather x1, waiting for transfers between devices, on_device(): lax.all_gather(jnp.swapaxes(caches, -1, -2), ('y', 'x'), axis=0, tiled=True)  45.3 us
    reduce_scatter x1, waiting for transfers between devices, on_device(): states = lax.psum_scatter(slots, 'z', scatter_dimension=0, tiled=True)[0]  22 us
    ppermute x3, starting transfers between devices, along_z(): lax.ppermute(value, 'z', perm=[(i, (i + d) % z_count) for i in range(z_co...  6.57 us
    unnamed x45, local copies, waits for them, and re-layouts  5.17 us
    sub x1, matrix products, on_device(): weights = jnp.exp(masked - peak)  4.8 us
    gather x1, local copies, waits for them, and re-layouts, on_device(): jnp.take(plane, jnp.clip(local, 0, per_plane - 1).reshape(-1), axis=0)  4.53 us
    dot_general x1, matrix products, on_device(): jnp.einsum('hqk,khd->qhd', memory_w, values, preferred_element_type=jnp.f...  4.23 us
    ppermute x6, starting transfers between devices, swap(): return lax.ppermute(value, 'col', perm=[(0, 1), (1, 0)])  3.8 us
  transfers between devices with their start and end apart: 11, of which 3 were waited for; matrix products, arithmetic and copies ran while one was open for 30% of the time, Pallas kernels for 0%

profile of v9, /device:TPU:1, one launch (start us, length us, event | category | flops | bytes accessed | tf_op | source)
XLA Modules:
  0.0 152.7 jit_solution(10091454672582207684)
XLA Ops:
  6.5 0.0 all-gather.2.cloned.1.call-start
  6.6 2.2 %copy.50 = bf16[4,4,128,128]{2,3,1,0:T(8,128)(2,1)} copy(bf16[4,4,128,128]{3,2,1,0:T(8,128)(2,1)} %param.23) | data formatting | bytes 1048576 | tf_op args[10]
  8.8 0.0 reduce-scatter.2.cloned.1.call-start
  8.9 2.5 %collective-permute-start.2 = (s32[6]{0:T(128)}, s32[6]{0:T(128)S(1)}, u32[]{:S(2)}, u32[]{:S(2)}) collective-permute-start(s32[6]{0:T(128)} %bitcast.178), channel_id=1, source_target_pairs={{0,32},{32,64},{64,96},{96,0},{1,33},{33,65},{65,97},{97,1},{2,34}... | collective-permute-start | bytes 80 | tf_op jit(solution)/shard_map/ppermute | solution.py:140
  11.4 3.3 %collective-permute-start.3 = (s32[6]{0:T(128)}, s32[6]{0:T(128)S(1)}, u32[]{:S(2)}, u32[]{:S(2)}) collective-permute-start(s32[6]{0:T(128)} %bitcast.179), channel_id=1, source_target_pairs={{0,64},{32,96},{64,0},{96,32},{1,65},{33,97},{65,1},{97,33},{2,66}... | collective-permute-start | bytes 80 | tf_op jit(solution)/shard_map/ppermute | solution.py:140
  14.7 0.7 collective-permute-start.4
  15.4 2.8 %copy.51 = bf16[32,1024,16]{1,0,2:T(8,128)(2,1)} copy(bf16[32,1024,16]{1,2,0:T(8,128)(2,1)} %param.18) | data formatting | bytes 2097152 | tf_op args[5]
  18.2 1.5 collective-permute-start.1
  19.7 1.2 fusion.44
  21.0 2.0 %fusion.46 = bf16[256,1024]{1,0:T(8,128)(2,1)} fusion(bf16[256,1024]{1,0:T(8,128)(2,1)} %param.13, f32[1024]{0:T(1024)S(1)} %bitcast.168, f32[256]{0:T(256)S(1)} %add_rsqrt_fusion.2), kind=kLoop, calls=%fused_computation.62 | loop fusion | flops 1048576 | bytes 1053696 | tf_op jit(solution)/shard_map/convert_element_type | solution.py:19
  23.0 0.1 reshape.433
  23.1 0.1 reshape_squeeze.3
  23.2 0.2 reduce-window.14
  23.5 0.1 fusion.75
  23.5 2.6 %convolution_convert_fusion = bf16[6,16,512]{2,0,1:T(8,128)(2,1)S(1)} fusion(bf16[64,16,512]{2,1,0:T(8,128)(2,1)} %param.19, s32[6]{0:T(128)S(1)} %bitcast.173), kind=kOutput, calls=%fused_computation.58 | convolution fusion | flops 6340992 | bytes 1146904 | tf_op jit(solution)/shard_map/gq,qjl->gjl/dot_general | solution.py:127
  26.1 3.2 %fusion.89 = f32[6,1024,16]{1,0,2:T(8,128)} fusion(s32[32]{0:T(128)S(1)} %iota_add_fusion.1, s32[6]{0:T(128)S(1)} %bitcast.174, bf16[32,1024,16]{1,2,0:T(8,128)(2,1)} %param.18), kind=kOutput, calls=%fused_computation.132 | convolution fusion | flops 6291648 | bytes 1441944 | tf_op jit(solution)/shard_map/sa,adr->sdr/dot_general | solution.py:117
  29.4 0.6 gather_fusion
  30.0 0.1 compare_and_fusion
  30.0 0.1 min.12
  30.1 1.5 %broadcast_select_fusion.1 = (bf16[256,1024]{1,0:T(8,128)(2,1)S(1)}, bf16[256,1024]{1,0:T(8,128)(2,1)S(1)}) fusion(bf16[256,1024]{1,0:T(8,128)(2,1)} %collective-permute-done, pred[]{:T(512)S(6)} %eq.79, f32[1024]{0:T(1024)S(1)} %bitcast.169, f32[256]{0:T(256)S(1)} %add_rsqrt_fusion.2, bf16[256,1024]{1,0:T(8,128)(2,1)} %param.13), kind=kLoop, calls=%fused_computation.84 | loop fusion | flops 1572864 | bytes 2102273 | tf_op jit(solution)/shard_map/jit(_where)/select_n | solution.py:27
  31.7 3.1 %fusion.119 = (bf16[3,512,512]{1,2,0:T(8,128)(2,1)}, f32[3,512,512]{1,2,0:T(8,128)S(1)}) fusion(bf16[3,1024,512]{2,1,0:T(8,128)(2,1)S(1)} %copy-done, bf16[256,1024]{1,0:T(8,128)(2,1)S(1)} %get-tuple-element.22, bf16[256,1024]{1,0:T(8,128)(2,1)S(1)} %get-tuple-element.21), kind=kOutput, calls=%fused_computation.181 | convolution fusion | flops 1613496320 | bytes 8912896 | tf_op jit(solution)/shard_map/td,kdc->ktc/dot_general | solution.py:107
  34.8 1.5 %fusion.43 = bf16[6,1024,16]{1,0,2:T(8,128)(2,1)S(1)} fusion(f32[6,1024,16]{1,0,2:T(8,128)S(1)} %copy-done.4, bf16[32,1024,16]{1,0,2:T(8,128)(2,1)} %collective-permute-done.1, s32[32]{0:T(128)S(1)} %iota_add_fusion, s32[6]{0:T(128)S(1)} %bitcast.175), kind=kOutput, calls=%fused_computation.57 | convolution fusion | flops 6488256 | bytes 1638552 | tf_op jit(solution)/shard_map/sa,adr->sdr/dot_general | solution.py:118
  36.3 0.1 copy.53
  36.5 0.5 fusion.67
  37.0 1.1 fusion.41
  38.1 45.3 %all-gather.2.cloned.1.call-done = bf16[64,4,128,128]{3,2,1,0:T(8,128)(2,1)} async-done(((bf16[4,4,128,128]{3,2,1,0:T(8,128)(2,1)}), bf16[64,4,128,128]{3,2,1,0:T(8,128)(2,1)}) %all-gather.2.cloned.1.call-update) | async-done | bytes 8388624 | tf_op jit(solution)/shard_map/all_gather | solution.py:95
  83.4 4.5 %gather_fusion.1 = bf16[24,4,128,128]{3,2,1,0:T(8,128)(2,1)S(1)} fusion(bf16[64,4,128,128]{3,2,1,0:T(8,128)(2,1)} %all-gather.2.cloned.1.call-done, s32[1024]{0:T(1024)S(1)} %pad_clamp_fusion), kind=kCustom, calls=%fused_computation.1 | custom fusion | bytes 6291552 | tf_op jit(solution)/shard_map/jit(_take)/gather | solution.py:146
  87.9 2.0 %fusion.11 = bf16[4,6,4,128,128]{4,3,1,2,0:T(8,128)(2,1)} fusion(bf16[4,6,4,128,128]{4,3,2,1,0:T(8,128)(2,1)S(1)} %bitcast.155, pred[4,6]{1,0:T(4,128)(4,1)S(1)} %get-tuple-element.17, bf16[4,6]{1,0:T(4,128)(2,1)S(1)} %get-tuple-element.25), kind=kLoop, calls=%fused_computation.16 | loop fusion | flops 3145728 | bytes 6291528 | tf_op jit(solution)/shard_map/mul | solution.py:148
  90.0 0.9 collective-permute-start.6
  91.0 0.1 convert_reduce_fusion
  91.0 0.1 fusion.76
  91.1 0.2 fusion.54
  91.4 0.4 convolution_bitcast_fusion.3
  91.7 0.1 fusion.114
  91.9 1.2 reduce-window.18
  93.1 0.2 slice_reduce_fusion
  93.2 0.2 reduce-window.19
  93.4 0.1 add_bitcast_fusion
  93.5 0.1 bitcast_subtract_fusion.1
  93.6 0.1 multiply_reduce_fusion.3
  93.7 0.1 multiply_reduce_fusion.2
  93.8 1.0 fusion.117
  94.9 1.0 copy.59
  95.9 1.5 broadcast_multiply_fusion
  97.4 4.8 %fusion.120 = (f32[4,512]{1,0:T(4,128)S(1)}, f32[4,512,512]{1,2,0:T(8,128)}) fusion(pred[512,512]{0,1:T(8,128)(4,1)S(1)} %fusion.54, bf16[512,4,128]{0,2,1:T(8,128)(2,1)} %bitcast.156, bf16[512,4,128]{0,2,1:T(8,128)(2,1)} %bitcast.164), kind=kOutput, calls=%fused_computation.182 | convolution fusion | flops 272630272 | bytes 5513216 | tf_op jit(solution)/shard_map/sub | solution.py:173
  102.2 4.2 %fusion.35 = f32[512,4,128]{0,2,1:T(8,128)} fusion(bf16[512,4,128]{0,2,1:T(8,128)(2,1)} %bitcast.162, f32[4,512]{1,0:T(4,128)S(1)} %bitcast.172, pred[512,512]{0,1:T(8,128)(4,1)S(1)} %fusion.54, bf16[512,4,128]{0,2,1:T(8,128)(2,1)} %bitcast.157, bf16[512,4,128]{0,2,1:T(8,128)(2,1)} %bitcast.165), kind=kOutput, calls=%fused_computation.45 | convolution fusion | flops 542113792 | bytes 2891776 | tf_op jit(solution)/shard_map/hqk,khd->qhd/dot_general | solution.py:178
  106.5 22.0 %reduce-scatter.2.cloned.1.call-done = bf16[1,6,4,128,128]{4,3,1,2,0:T(8,128)(2,1)} async-done(((bf16[4,6,4,128,128]{4,3,1,2,0:T(8,128)(2,1)}), bf16[1,6,4,128,128]{4,3,1,2,0:T(8,128)(2,1)}) %reduce-scatter.2.cloned.1.call-update) | async-done | bytes 786448 | tf_op jit(solution)/shard_map/reduce_scatter | solution.py:149
  128.4 2.8 %multiply_reduce_fusion = (f32[512,4]{0,1:T(4,128)S(1)}, f32[512,4,128]{0,2,1:T(8,128)S(1)}) fusion(f32[512,4,128]{0,2,1:T(8,128)} %fusion.35, f32[512,4]{0,1:T(4,128)S(1)} %fusion.84, bf16[512,6,4,128]{3,0,1,2:T(8,128)(2,1)S(1)} %broadcast_multiply_fusion, bf16[1,6,4,128,128]{4,3,1,2,0:T(8,128)(2,1)} %reduce-scatter.2.cloned.1.call-done), kind=kOutput, calls=%fused_computation.73 | convolution fusion | flops 403699712 | bytes 6045696 | tf_op jit(solution)/shard_map/tshi,shji->thj/dot_general | solution.py:164
  131.2 0.1 copy-done.17
  131.3 0.6 fusion.40
  132.0 0.7 collective-permute-start.5
  132.7 2.3 %fusion.68 = f32[256,1024]{1,0:T(8,128)S(1)} fusion(bf16[512,1024]{1,0:T(8,128)(2,1)} %param.24, bf16[512,512]{0,1:T(8,128)(2,1)S(1)} %bitcast.161, s32[]{:T(128)S(6)} %select_n.121), kind=kOutput, calls=%fused_computation.91 | convolution fusion | flops 268435456 | bytes 2359300 | tf_op jit(solution)/shard_map/dot_general | solution.py:186
  135.0 1.8 %fusion.47 = (f32[256]{0:T(256)S(1)}, bf16[256,1024]{1,0:T(8,128)(2,1)S(1)}) fusion(f32[256,1024]{1,0:T(8,128)S(1)} %fusion.68, bf16[256,512]{0,1:T(8,128)(2,1)S(1)} %collective-permute-done.5, bf16[512,1024]{1,0:T(8,128)(2,1)} %collective-permute-done.6, bf16[256,1024]{1,0:T(8,128)(2,1)S(1)} %copy-done.2), kind=kOutput, calls=%fused_computation.63 | convolution fusion | flops 270270208 | bytes 3408896 | tf_op jit(solution)/shard_map/dot_general | solution.py:186
  136.8 0.2 fusion.49
  137.0 0.1 collective-permute-start.7
  137.2 0.9 fusion.18
  138.1 1.1 fusion.16
  139.2 1.7 %fusion.7 = f32[2,256,1408]{2,1,0:T(8,128)S(1)} fusion(bf16[3,1024,1408]{2,1,0:T(8,128)(2,1)S(1)} %bitcast.154, bf16[256,1024]{1,0:T(8,128)(2,1)S(1)} %collective-permute-done.7), kind=kOutput, calls=%fused_computation.13 | convolution fusion | flops 1476395008 | bytes 9175040 | tf_op jit(solution)/shard_map/td,kdf->ktf/dot_general | solution.py:193
  140.9 1.0 fusion.12
  141.9 0.6 collective-permute-start.8
  142.5 0.9 fusion.21
  143.4 1.1 fusion.14
  144.5 0.3 collective-permute-done.8
  144.7 1.1 fusion.50
  (72 shorter events, 0.4 us)
Async XLA Ops:
  6.5 25.2 %copy-start = (bf16[3,1024,512]{2,1,0:T(8,128)(2,1)S(1)}, bf16[3,1024,512]{2,1,0:T(8,128)(2,1)}, u32[]{:S(2)}) copy-start(bf16[3,1024,512]{2,1,0:T(8,128)(2,1)} %param.15) | copy-start | bytes 9437188
  6.5 14.4 %copy-start.11 = (f32[2,1024]{1,0:T(2,128)S(1)}, f32[2,1024]{1,0:T(2,128)}, u32[]{:S(2)}) copy-start(f32[2,1024]{1,0:T(2,128)} %param.14) | copy-start | bytes 24580
  6.5 16.5 %copy-start.16 = (s32[1,2,3]{2,1,0:T(2,128)S(1)}, s32[1,2,3]{2,1,0:T(2,128)}, u32[]{:S(2)}) copy-start(s32[1,2,3]{2,1,0:T(2,128)} %param.20) | copy-start | bytes 76
  6.5 17.0 %copy-start.12 = (s32[1,6]{1,0:T(1,128)S(1)}, s32[1,6]{1,0:T(1,128)}, u32[]{:S(2)}) copy-start(s32[1,6]{1,0:T(1,128)} %param.21) | copy-start | bytes 76
  6.5 76.8 %all-gather.2.cloned.1.call-start = ((), (), s32[]{:S(2)}) async-start(), calls=%async_computation.1 | async-start | bytes 8912896 | tf_op jit(solution)/shard_map/all_gather | solution.py:95
  8.8 119.6 %reduce-scatter.2.cloned.1.call-start = ((), (), s32[]{:S(2)}) async-start(), calls=%async_computation.2 | async-start | bytes 3932160 | tf_op jit(solution)/shard_map/reduce_scatter | solution.py:149
  8.9 20.5 %copy-start.14 = (s32[1,6]{1,0:T(1,128)S(1)}, s32[1,6]{1,0:T(1,128)}, u32[]{:S(2)}) copy-start(s32[1,6]{1,0:T(1,128)} %param.22) | copy-start | bytes 76
  8.9 20.5 %collective-permute-start.2 = (s32[6]{0:T(128)}, s32[6]{0:T(128)S(1)}, u32[]{:S(2)}, u32[]{:S(2)}) collective-permute-start(s32[6]{0:T(128)} %bitcast.178), channel_id=1, source_target_pairs={{0,32},{32,64},{64,96},{96,0},{1,33},{33,65},{65,97},{97,1},{2,34}... | collective-permute-start | bytes 80 | tf_op jit(solution)/shard_map/ppermute | solution.py:140
  11.4 17.9 %collective-permute-start.3 = (s32[6]{0:T(128)}, s32[6]{0:T(128)S(1)}, u32[]{:S(2)}, u32[]{:S(2)}) collective-permute-start(s32[6]{0:T(128)} %bitcast.179), channel_id=1, source_target_pairs={{0,64},{32,96},{64,0},{96,32},{1,65},{33,97},{65,1},{97,33},{2,66}... | collective-permute-start | bytes 80 | tf_op jit(solution)/shard_map/ppermute | solution.py:140
  14.7 14.6 %collective-permute-start.4 = (s32[6]{0:T(128)}, s32[6]{0:T(128)S(1)}, u32[]{:S(2)}, u32[]{:S(2)}) collective-permute-start(s32[6]{0:T(128)} %bitcast.180), channel_id=1, source_target_pairs={{0,96},{32,0},{64,32},{96,64},{1,97},{33,1},{65,33},{97,65},{2,98}... | collective-permute-start | bytes 80 | tf_op jit(solution)/shard_map/ppermute | solution.py:140
  18.2 16.6 %collective-permute-start.1 = (bf16[32,1024,16]{1,0,2:T(8,128)(2,1)}, bf16[32,1024,16]{1,0,2:T(8,128)(2,1)}, u32[]{:S(2)}, u32[]{:S(2)}) collective-permute-start(bf16[32,1024,16]{1,0,2:T(8,128)(2,1)} %copy.51), channel_id=1, source_target_pairs={{0,1},{1,0},{2,3},{3,2},{4,5},{5,4},{6,7},{7,6},{8,9},{9,8},{10,11... | collective-permute-start | bytes 3145736 | tf_op jit(solution)/shard_map/ppermute | solution.py:23
  23.0 7.1 %collective-permute-start = (bf16[256,1024]{1,0:T(8,128)(2,1)}, bf16[256,1024]{1,0:T(8,128)(2,1)}, u32[]{:S(2)}, u32[]{:S(2)}) collective-permute-start(bf16[256,1024]{1,0:T(8,128)(2,1)} %fusion.46), channel_id=1, source_target_pairs={{0,1},{1,0},{2,3},{3,2},{4,5},{5,4},{6,7},{7,6},{8,9},{9,8},{10,11... | collective-permute-start | bytes 1572872 | tf_op jit(solution)/shard_map/ppermute | solution.py:23
  31.7 4.8 %copy-start.6 = (bf16[256,1024]{1,0:T(8,128)(2,1)}, bf16[256,1024]{1,0:T(8,128)(2,1)S(1)}, u32[]{:S(2)}) copy-start(bf16[256,1024]{1,0:T(8,128)(2,1)S(1)} %get-tuple-element.21) | copy-start | bytes 1572868
  31.7 4.8 %copy-start.8 = (bf16[256,1024]{1,0:T(8,128)(2,1)}, bf16[256,1024]{1,0:T(8,128)(2,1)S(1)}, u32[]{:S(2)}) copy-start(bf16[256,1024]{1,0:T(8,128)(2,1)S(1)} %get-tuple-element.22) | copy-start | bytes 1572868
  31.7 3.1 %copy-start.4 = (f32[6,1024,16]{1,0,2:T(8,128)S(1)}, f32[6,1024,16]{1,0,2:T(8,128)}, u32[]{:S(2)}) copy-start(f32[6,1024,16]{1,0,2:T(8,128)} %fusion.89) | copy-start | bytes 1179652
  90.0 1.4 copy-start.7
  90.0 1.4 copy-start.9
  90.0 1.4 copy-start.15
  90.0 1.8 %copy-start.13 = (f32[4]{0:T(128)S(1)}, f32[4]{0:T(128)}, u32[]{:S(2)}) copy-start(f32[4]{0:T(128)} %param.17) | copy-start | bytes 52
  90.0 3.8 %copy-start.5 = (bf16[3,512,512]{1,2,0:T(8,128)(2,1)S(1)}, bf16[3,512,512]{1,2,0:T(8,128)(2,1)}, u32[]{:S(2)}) copy-start(bf16[3,512,512]{1,2,0:T(8,128)(2,1)} %get-tuple-element.28) | copy-start | bytes 4718596
  90.0 4.9 %copy-start.3 = (bf16[512,512]{0,1:T(8,128)(2,1)S(1)}, bf16[512,512]{0,1:T(8,128)(2,1)}, u32[]{:S(2)}) copy-start(bf16[512,512]{0,1:T(8,128)(2,1)} %fusion.41) | copy-start | bytes 1572868
  90.0 45.0 %collective-permute-start.6 = (bf16[512,1024]{1,0:T(8,128)(2,1)}, bf16[512,1024]{1,0:T(8,128)(2,1)}, u32[]{:S(2)}, u32[]{:S(2)}) collective-permute-start(bf16[512,1024]{1,0:T(8,128)(2,1)} %param.24), channel_id=1, source_target_pairs={{0,1},{1,0},{2,3},{3,2},{4,5},{5,4},{6,7},{7,6},{8,9},{9,8},{10,11... | collective-permute-start | bytes 3145736 | tf_op jit(solution)/shard_map/ppermute | solution.py:23
  128.4 2.8 %copy-start.10 = (bf16[1,512,512]{1,2,0:T(8,128)(2,1)S(1)}, bf16[1,512,512]{1,2,0:T(8,128)(2,1)}, u32[]{:S(2)}) copy-start(bf16[1,512,512]{1,2,0:T(8,128)(2,1)} %get-tuple-element.20) | copy-start | bytes 1572868
  128.4 2.9 %copy-start.17 = (f32[4,512,512]{1,2,0:T(8,128)S(1)}, f32[4,512,512]{1,2,0:T(8,128)}, u32[]{:S(2)}) copy-start(f32[4,512,512]{1,2,0:T(8,128)} %get-tuple-element.31) | copy-start | bytes 12582916
  131.2 5.9 %slice-start = ((s8[8650752]{0:T(1024)(128)(4,1)}), s8[4194304]{0:T(1024)(128)(4,1)S(1)}, s32[]{:S(2)}) async-start(s8[8650752]{0:T(1024)(128)(4,1)} %bitcast.153), calls=%async_computation.3 | async-start | bytes 8388608
  131.3 5.8 %slice-start.1 = ((s8[8650752]{0:T(1024)(128)(4,1)}), s8[4194304]{0:T(1024)(128)(4,1)S(1)}, s32[]{:S(2)}) async-start(s8[8650752]{0:T(1024)(128)(4,1)} %bitcast.153), calls=%async_computation.4 | async-start | bytes 8388608
  131.3 5.8 %slice-start.2 = ((s8[8650752]{0:T(1024)(128)(4,1)}), s8[262144]{0:T(1024)(128)(4,1)S(1)}, s32[]{:S(2)}) async-start(s8[8650752]{0:T(1024)(128)(4,1)} %bitcast.153), calls=%async_computation.5 | async-start | bytes 524288
  131.9 3.1 %copy-start.2 = (bf16[256,1024]{1,0:T(8,128)(2,1)S(1)}, bf16[256,1024]{1,0:T(8,128)(2,1)}, u32[]{:S(2)}) copy-start(bf16[256,1024]{1,0:T(8,128)(2,1)} %param.13) | copy-start | bytes 1572868
  132.0 3.0 %collective-permute-start.5 = (bf16[256,512]{0,1:T(8,128)(2,1)S(1)}, bf16[256,512]{0,1:T(8,128)(2,1)S(1)}, u32[]{:S(2)}, u32[]{:S(2)}) collective-permute-start(bf16[256,512]{0,1:T(8,128)(2,1)S(1)} %constant_dynamic-slice_fusion), channel_id=1, source_target_pairs={{0,1},{1,0},{2,3},{3,2},{4,5},{5,4},{6,7},{7,6},{8,9},{9,8},{10,11... | collective-permute-start | bytes 786440 | tf_op jit(solution)/shard_map/ppermute | solution.py:23
  137.0 2.1 %collective-permute-start.7 = (bf16[256,1024]{1,0:T(8,128)(2,1)S(1)}, bf16[256,1024]{1,0:T(8,128)(2,1)S(1)}, u32[]{:S(2)}, u32[]{:S(2)}) collective-permute-start(bf16[256,1024]{1,0:T(8,128)(2,1)S(1)} %fusion.49), channel_id=1, source_target_pairs={{0,1},{1,0},{2,3},{3,2},{4,5},{5,4},{6,7},{7,6},{8,9},{9,8},{10,11... | collective-permute-start | bytes 1572872 | tf_op jit(solution)/shard_map/ppermute | solution.py:23
  141.9 2.8 %collective-permute-start.8 = (f32[256,1024]{1,0:T(8,128)S(1)}, f32[256,1024]{1,0:T(8,128)S(1)}, u32[]{:S(2)}, u32[]{:S(2)}) collective-permute-start(f32[256,1024]{1,0:T(8,128)S(1)} %fusion.12), channel_id=1, source_target_pairs={{0,1},{1,0},{2,3},{3,2},{4,5},{5,4},{6,7},{7,6},{8,9},{9,8},{10,11... | collective-permute-start | bytes 3145736 | tf_op jit(solution)/shard_map/ppermute | solution.py:23
  143.4 2.4 %copy-start.1 = (bf16[3,1024,512]{2,1,0:T(8,128)(2,1)S(1)}, bf16[3,1024,512]{2,1,0:T(8,128)(2,1)}, u32[]{:S(2)}) copy-start(bf16[3,1024,512]{2,1,0:T(8,128)(2,1)} %param.15) | copy-start | bytes 9437188
Sparse Core Ops, SparseCore 0:
  9.5 73.8 all-gather.1
  90.1 38.2 reduce-scatter.1

commit v10 on v9

--- a/solution.py
+++ b/solution.py
@@ -146,7 +146,14 @@
     picked = jnp.take(plane, jnp.clip(local, 0, per_plane - 1).reshape(-1), axis=0)
     keep = valid.reshape(-1).astype(plane.dtype)[:, None, None, None]
     slots = (picked * keep).reshape((z_count, -1) + plane.shape[1:])
-    states = lax.psum_scatter(slots, "z", scatter_dimension=0, tiled=True)[0]
+    lead = slots.shape[2] - 1
+    states_lead = lax.psum_scatter(slots[:, :, :lead], "z", scatter_dimension=0, tiled=True)[0]
+    tail_slots = slots[:, :, lead:]
+    states_tail = jnp.take(tail_slots, z_here, axis=0).astype(jnp.float32)
+    for d in shifts:
+        outgoing = jnp.take(tail_slots, (z_here + d) % z_count, axis=0)
+        states_tail = states_tail + along_z(outgoing, d).astype(jnp.float32)
+    states = jnp.concatenate([states_lead, states_tail.astype(jnp.bfloat16)], axis=1)
     keys = projected[1].astype(jnp.bfloat16).reshape(group, local_heads, head_size)
     values = projected[2].astype(jnp.bfloat16).reshape(group, local_heads, head_size)
     gate_terms = jnp.einsum(

time: 153 us -> 158 us (1.033)
  waiting for transfers between devices: 67.5 us -> 59.1 us
  local copies, waits for them, and re-layouts: 12.9 us -> 19.5 us
  starting transfers between devices: 10.4 us -> 15.4 us
  other arithmetic: 12.3 us -> 14.7 us
    reduce_scatter x1, waiting for transfers between devices: 22 us -> 8.06 us  [on_device(): lax.psum_scatter(slots[:, :, :lead], 'z', scatter_dimension=0, tiled=True)]
    ppermute x3 -> x6, starting transfers between devices: 6.57 us -> 11.5 us  [along_z(): lax.ppermute(value, 'z', perm=[(i, (i + d) % z_count) for i in range(z_co...]
    ppermute x3 -> x6, waiting for transfers between devices: 0.01 us -> 4.47 us  [along_z(): lax.ppermute(value, 'z', perm=[(i, (i + d) % z_count) for i in range(z_co...]
    dot_general x1, matrix products: 2.29 us -> 0.47 us  [on_device(): jnp.dot(head_own, head_output_weight, preferred_element_type=jnp.float32)]
    slice x1 -> x3, local copies, waits for them, and re-layouts: 0.16 us -> 1.93 us  [the longest x1 1.7 us: on_device(): slots[:, :, :lead]]
    gather x1, local copies, waits for them, and re-layouts: 4.53 us -> 6.16 us  [on_device(): jnp.take(plane, jnp.clip(local, 0, per_plane - 1).reshape(-1), axis=0)]
    unnamed x45 -> x41, local copies, waits for them, and re-layouts: 5.17 us -> 6.16 us
  transfers between devices with their start and end apart: 11 -> 14, of which waited for: 3 -> 5; matrix products, arithmetic and copies ran while one was open for 30% -> 32% of each run, Pallas kernels for 0% -> 0%
where the time goes in v10:
time: 158 us
  waiting for transfers between devices  59.1 us (37%)
  matrix products  35.2 us (22%)
  local copies, waits for them, and re-layouts  19.5 us (12%)
  starting transfers between devices  15.4 us (10%)
  other arithmetic  14.7 us (9%)
  between operations  13.8 us (9%)
    all_gather x1, waiting for transfers between devices, on_device(): lax.all_gather(jnp.swapaxes(caches, -1, -2), ('y', 'x'), axis=0, tiled=True)  45.3 us
    ppermute x6, starting transfers between devices, along_z(): lax.ppermute(value, 'z', perm=[(i, (i + d) % z_count) for i in range(z_co...  11.5 us
    reduce_scatter x1, waiting for transfers between devices, on_device(): lax.psum_scatter(slots[:, :, :lead], 'z', scatter_dimension=0, tiled=True)  8.06 us
    gather x1, local copies, waits for them, and re-layouts, on_device(): jnp.take(plane, jnp.clip(local, 0, per_plane - 1).reshape(-1), axis=0)  6.16 us
    unnamed x41, local copies, waits for them, and re-layouts  6.16 us
    sub x1, matrix products, on_device(): weights = jnp.exp(masked - peak)  4.78 us
    ppermute x6, waiting for transfers between devices, along_z(): lax.ppermute(value, 'z', perm=[(i, (i + d) % z_count) for i in range(z_co...  4.47 us
    dot_general x1, matrix products, on_device(): jnp.einsum('hqk,khd->qhd', memory_w, values, preferred_element_type=jnp.f...  4.27 us
  transfers between devices with their start and end apart: 14, of which 5 were waited for; matrix products, arithmetic and copies ran while one was open for 32% of the time, Pallas kernels for 0%

profile of v10, /device:TPU:1, one launch (start us, length us, event | category | flops | bytes accessed | tf_op | source)
XLA Modules:
  0.0 157.7 jit_solution(18137929303268893074)
XLA Ops:
  6.6 2.2 %copy.64 = bf16[4,4,128,128]{2,3,1,0:T(8,128)(2,1)} copy(bf16[4,4,128,128]{3,2,1,0:T(8,128)(2,1)} %param.25) | data formatting | bytes 1048576 | tf_op args[10]
  8.9 2.5 %collective-permute-start.2 = (s32[6]{0:T(128)}, s32[6]{0:T(128)S(1)}, u32[]{:S(2)}, u32[]{:S(2)}) collective-permute-start(s32[6]{0:T(128)} %bitcast.183), channel_id=1, source_target_pairs={{0,32},{32,64},{64,96},{96,0},{1,33},{33,65},{65,97},{97,1},{2,34}... | collective-permute-start | bytes 80 | tf_op jit(solution)/shard_map/ppermute | solution.py:140
  11.4 3.3 %collective-permute-start.3 = (s32[6]{0:T(128)}, s32[6]{0:T(128)S(1)}, u32[]{:S(2)}, u32[]{:S(2)}) collective-permute-start(s32[6]{0:T(128)} %bitcast.184), channel_id=1, source_target_pairs={{0,64},{32,96},{64,0},{96,32},{1,65},{33,97},{65,1},{97,33},{2,66}... | collective-permute-start | bytes 80 | tf_op jit(solution)/shard_map/ppermute | solution.py:140
  14.7 0.7 collective-permute-start.4
  15.5 2.8 %copy.65 = bf16[32,1024,16]{1,0,2:T(8,128)(2,1)} copy(bf16[32,1024,16]{1,2,0:T(8,128)(2,1)} %param.20) | data formatting | bytes 2097152 | tf_op args[5]
  18.2 1.5 collective-permute-start.1
  19.7 1.2 fusion.44
  21.0 2.0 %fusion.46 = bf16[256,1024]{1,0:T(8,128)(2,1)} fusion(bf16[256,1024]{1,0:T(8,128)(2,1)} %param.15, f32[1024]{0:T(1024)S(1)} %bitcast.173, f32[256]{0:T(256)S(1)} %add_rsqrt_fusion.2), kind=kLoop, calls=%fused_computation.62 | loop fusion | flops 1048576 | bytes 1053696 | tf_op jit(solution)/shard_map/convert_element_type | solution.py:19
  23.2 0.2 reduce-window.14
  23.5 2.6 %convolution_convert_fusion = bf16[6,16,512]{2,0,1:T(8,128)(2,1)S(1)} fusion(bf16[64,16,512]{2,1,0:T(8,128)(2,1)} %param.21, s32[6]{0:T(128)S(1)} %bitcast.178), kind=kOutput, calls=%fused_computation.58 | convolution fusion | flops 6340992 | bytes 1146904 | tf_op jit(solution)/shard_map/gq,qjl->gjl/dot_general | solution.py:127
  26.1 3.2 %fusion.91 = f32[6,1024,16]{1,0,2:T(8,128)} fusion(s32[32]{0:T(128)S(1)} %iota_add_fusion.1, s32[6]{0:T(128)S(1)} %bitcast.179, bf16[32,1024,16]{1,2,0:T(8,128)(2,1)} %param.20), kind=kOutput, calls=%fused_computation.138 | convolution fusion | flops 6291648 | bytes 1441944 | tf_op jit(solution)/shard_map/sa,adr->sdr/dot_general | solution.py:117
  29.4 0.6 gather_fusion
  30.1 1.5 broadcast_select_fusion.1
  31.7 3.1 %fusion.122 = (bf16[3,512,512]{1,2,0:T(8,128)(2,1)}, f32[3,512,512]{1,2,0:T(8,128)S(1)}) fusion(bf16[3,1024,512]{2,1,0:T(8,128)(2,1)S(1)} %copy-done, bf16[256,1024]{1,0:T(8,128)(2,1)S(1)} %get-tuple-element.34, bf16[256,1024]{1,0:T(8,128)(2,1)S(1)} %get-tuple-element.33), kind=kOutput, calls=%fused_computation.188 | convolution fusion | flops 1613496320 | bytes 8912896 | tf_op jit(solution)/shard_map/td,kdc->ktc/dot_general | solution.py:107
  34.8 1.6 fusion.43
  36.3 0.1 copy.67
  36.4 0.5 fusion.69
  36.9 1.2 fusion.41
  38.1 45.3 %all-gather.2.cloned.1.call-done = bf16[64,4,128,128]{3,2,1,0:T(8,128)(2,1)} async-done(((bf16[4,4,128,128]{3,2,1,0:T(8,128)(2,1)}), bf16[64,4,128,128]{3,2,1,0:T(8,128)(2,1)}) %all-gather.2.cloned.1.call-update) | async-done | bytes 8388624 | tf_op jit(solution)/shard_map/all_gather | solution.py:95
  83.4 6.2 %gather_fusion.1 = bf16[24,4,128,128]{3,2,1,0:T(8,128)(2,1)} fusion(bf16[64,4,128,128]{3,2,1,0:T(8,128)(2,1)} %all-gather.2.cloned.1.call-done, s32[1024]{0:T(1024)S(1)} %pad_clamp_fusion), kind=kCustom, calls=%fused_computation.1 | custom fusion | bytes 6291552 | tf_op jit(solution)/shard_map/jit(_take)/gather | solution.py:146
  89.5 2.2 %fusion.11 = bf16[4,6,4,128,128]{4,3,1,2,0:T(8,128)(2,1)S(1)} fusion(bf16[4,6,4,128,128]{4,3,2,1,0:T(8,128)(2,1)} %bitcast.159, pred[4,6]{1,0:T(4,128)(4,1)S(1)} %get-tuple-element.29, bf16[4,6]{1,0:T(4,128)(2,1)S(1)} %get-tuple-element.40), kind=kLoop, calls=%fused_computation.16 | loop fusion | flops 3145728 | bytes 6291528 | tf_op jit(solution)/shard_map/mul | solution.py:148
  91.8 1.7 %slice.113 = bf16[4,6,3,128,128]{4,3,1,2,0:T(8,128)(2,1)} slice(bf16[4,6,4,128,128]{4,3,1,2,0:T(8,128)(2,1)S(1)} %fusion.11), slice={[0:4], [0:6], [0:3], [0:128], [0:128]} | slice | bytes 4718592 | tf_op jit(solution)/shard_map/slice | solution.py:150
  93.5 0.8 collective-permute-start.9
  94.3 0.1 convert_reduce_fusion
  94.4 0.2 fusion.54
  94.7 1.6 convolution_bitcast_fusion.3
  96.2 0.1 fusion.117
  96.4 1.2 reduce-window.18
  97.6 0.2 slice_reduce_fusion
  97.7 0.2 reduce-window.19
  98.0 0.1 bitcast_subtract_fusion.1
  98.1 0.1 multiply_reduce_fusion.3
  98.2 0.1 multiply_reduce_fusion.2
  98.3 2.2 %fusion.120 = (bf16[1,512,512]{1,2,0:T(8,128)(2,1)}, bf16[1,512,512]{1,2,0:T(8,128)(2,1)}) fusion(bf16[3,512,512]{1,2,0:T(8,128)(2,1)} %get-tuple-element.43), kind=kLoop, calls=%fused_computation.186 | loop fusion | bytes 2097152 | tf_op jit(solution)/shard_map/slice | solution.py:157
  100.7 1.0 copy-done.3
  101.6 0.8 select_bitcast_fusion.2
  102.5 1.3 collective-permute-start.5
  103.8 2.6 %collective-permute-start.6 = (bf16[6,1,128,128]{3,2,0,1:T(8,128)(2,1)}, bf16[6,1,128,128]{3,2,0,1:T(8,128)(2,1)}, u32[]{:S(2)}, u32[]{:S(2)}) collective-permute-start(bf16[6,1,128,128]{3,2,0,1:T(8,128)(2,1)} %get-tuple-element.37), channel_id=1, source_target_pairs={{0,64},{32,96},{64,0},{96,32},{1,65},{33,97},{65,1},{97,33},{2,66}... | collective-permute-start | bytes 589832 | tf_op jit(solution)/shard_map/ppermute | solution.py:140
  106.3 1.1 collective-permute-start.7
  107.4 2.0 %copy.73 = bf16[512,4,128]{2,0,1:T(8,128)(2,1)} copy(bf16[512,4,128]{0,2,1:T(8,128)(2,1)} %bitcast.160) | data formatting | bytes 1048576 | tf_op jit(solution)/shard_map/optimization_barrier | solution.py:133
  109.5 1.5 broadcast_multiply_fusion
  111.0 4.3 %fusion.35 = f32[512,4,128]{0,2,1:T(8,128)} fusion(bf16[512,4,128]{0,2,1:T(8,128)(2,1)} %bitcast.167, f32[4,512]{1,0:T(4,128)S(1)} %bitcast.177, pred[512,512]{0,1:T(8,128)(4,1)S(1)} %fusion.54, bf16[512,4,128]{0,2,1:T(8,128)(2,1)} %bitcast.161, bf16[512,4,128]{0,2,1:T(8,128)(2,1)} %bitcast.169), kind=kOutput, calls=%fused_computation.45 | convolution fusion | flops 542113792 | bytes 2891776 | tf_op jit(solution)/shard_map/hqk,khd->qhd/dot_general | solution.py:185
  115.3 4.8 %fusion.123 = (f32[4,512]{1,0:T(4,128)S(1)}, f32[4,512,512]{1,2,0:T(8,128)}) fusion(pred[512,512]{0,1:T(8,128)(4,1)S(1)} %fusion.54, bf16[512,4,128]{0,2,1:T(8,128)(2,1)} %bitcast.162, bf16[512,4,128]{0,2,1:T(8,128)(2,1)} %bitcast.170), kind=kOutput, calls=%fused_computation.189 | convolution fusion | flops 272630272 | bytes 5513216 | tf_op jit(solution)/shard_map/sub | solution.py:180
  120.1 4.5 %collective-permute-done.6 = bf16[6,1,128,128]{3,2,0,1:T(8,128)(2,1)} collective-permute-done((bf16[6,1,128,128]{3,2,0,1:T(8,128)(2,1)}, bf16[6,1,128,128]{3,2,0,1:T(8,128)(2,1)}, u32[]{:S(2)}, u32[]{:S(2)}) %collective-permute-start.6) | collective-permute-done | bytes 196640 | tf_op jit(solution)/shard_map/ppermute | solution.py:140
  124.5 1.3 add_convert_fusion
  125.9 8.1 %reduce-scatter.2.cloned.1.call-done = bf16[1,6,3,128,128]{4,3,1,2,0:T(8,128)(2,1)} async-done(((bf16[4,6,3,128,128]{4,3,1,2,0:T(8,128)(2,1)}), bf16[1,6,3,128,128]{4,3,1,2,0:T(8,128)(2,1)}) %reduce-scatter.2.cloned.1.call-update) | async-done | bytes 589840 | tf_op jit(solution)/shard_map/reduce_scatter | solution.py:150
  133.9 2.7 %multiply_reduce_fusion = (f32[512,4]{0,1:T(4,128)S(1)}, f32[512,4,128]{0,2,1:T(8,128)S(1)}) fusion(f32[512,4,128]{0,2,1:T(8,128)} %fusion.35, f32[512,4]{0,1:T(4,128)S(1)} %fusion.86, bf16[512,6,4,128]{3,0,1,2:T(8,128)(2,1)S(1)} %broadcast_multiply_fusion, bf16[6,1,128,128]{3,2,0,1:T(8,128)(2,1)S(1)} %add_convert_fusion, bf16[6,3,128,128]{3,2,0,1:T(8,128)(2,1)} %bitcast.164), kind=kOutput, calls=%fused_computation.73 | convolution fusion | flops 404092928 | bytes 6045696 | tf_op jit(solution)/shard_map/tshi,shji->thj/dot_general | solution.py:171
  136.7 0.1 copy-done.15
  136.8 0.6 fusion.40
  137.4 0.7 collective-permute-start.8
  138.1 0.5 fusion.70
  138.6 0.6 collective-permute-done.8
  139.3 2.1 %fusion.47 = (f32[256]{0:T(256)S(1)}, bf16[256,1024]{1,0:T(8,128)(2,1)S(1)}) fusion(f32[256,1024]{1,0:T(8,128)S(1)} %fusion.70, bf16[256,512]{0,1:T(8,128)(2,1)S(1)} %collective-permute-done.8, bf16[512,1024]{1,0:T(8,128)(2,1)} %collective-permute-done.9, bf16[256,1024]{1,0:T(8,128)(2,1)S(1)} %copy-done.2), kind=kOutput, calls=%fused_computation.63 | convolution fusion | flops 270270208 | bytes 3408896 | tf_op jit(solution)/shard_map/dot_general | solution.py:193
  141.4 0.2 fusion.49
  141.6 0.7 collective-permute-start.10
  142.3 0.9 fusion.18
  143.3 1.1 fusion.16
  144.3 1.7 %fusion.7 = f32[2,256,1408]{2,1,0:T(8,128)S(1)} fusion(bf16[3,1024,1408]{2,1,0:T(8,128)(2,1)S(1)} %bitcast.158, bf16[256,1024]{1,0:T(8,128)(2,1)S(1)} %collective-permute-done.10), kind=kOutput, calls=%fused_computation.13 | convolution fusion | flops 1476395008 | bytes 9175040 | tf_op jit(solution)/shard_map/td,kdf->ktf/dot_general | solution.py:200
  146.0 1.0 fusion.12
  147.1 0.1 collective-permute-start.11
  147.2 0.9 fusion.21
  148.1 1.1 fusion.14
  149.2 0.6 collective-permute-done.11
  149.8 1.1 fusion.50
  (78 shorter events, 1.1 us)
Async XLA Ops:
  6.5 25.1 %copy-start = (bf16[3,1024,512]{2,1,0:T(8,128)(2,1)S(1)}, bf16[3,1024,512]{2,1,0:T(8,128)(2,1)}, u32[]{:S(2)}) copy-start(bf16[3,1024,512]{2,1,0:T(8,128)(2,1)} %param.17) | copy-start | bytes 9437188
  6.5 14.4 %copy-start.9 = (f32[2,1024]{1,0:T(2,128)S(1)}, f32[2,1024]{1,0:T(2,128)}, u32[]{:S(2)}) copy-start(f32[2,1024]{1,0:T(2,128)} %param.16) | copy-start | bytes 24580
  6.5 16.5 %copy-start.14 = (s32[1,2,3]{2,1,0:T(2,128)S(1)}, s32[1,2,3]{2,1,0:T(2,128)}, u32[]{:S(2)}) copy-start(s32[1,2,3]{2,1,0:T(2,128)} %param.22) | copy-start | bytes 76
  6.5 17.0 %copy-start.10 = (s32[1,6]{1,0:T(1,128)S(1)}, s32[1,6]{1,0:T(1,128)}, u32[]{:S(2)}) copy-start(s32[1,6]{1,0:T(1,128)} %param.23) | copy-start | bytes 76
  6.5 76.8 %all-gather.2.cloned.1.call-start = ((), (), s32[]{:S(2)}) async-start(), calls=%async_computation.1 | async-start | bytes 8912896 | tf_op jit(solution)/shard_map/all_gather | solution.py:95
  8.8 125.1 %reduce-scatter.2.cloned.1.call-start = ((), (), s32[]{:S(2)}) async-start(), calls=%async_computation.2 | async-start | bytes 2949120 | tf_op jit(solution)/shard_map/reduce_scatter | solution.py:150
  8.9 20.4 %copy-start.12 = (s32[1,6]{1,0:T(1,128)S(1)}, s32[1,6]{1,0:T(1,128)}, u32[]{:S(2)}) copy-start(s32[1,6]{1,0:T(1,128)} %param.24) | copy-start | bytes 76
  8.9 20.4 %collective-permute-start.2 = (s32[6]{0:T(128)}, s32[6]{0:T(128)S(1)}, u32[]{:S(2)}, u32[]{:S(2)}) collective-permute-start(s32[6]{0:T(128)} %bitcast.183), channel_id=1, source_target_pairs={{0,32},{32,64},{64,96},{96,0},{1,33},{33,65},{65,97},{97,1},{2,34}... | collective-permute-start | bytes 80 | tf_op jit(solution)/shard_map/ppermute | solution.py:140
  11.4 17.9 %collective-permute-start.3 = (s32[6]{0:T(128)}, s32[6]{0:T(128)S(1)}, u32[]{:S(2)}, u32[]{:S(2)}) collective-permute-start(s32[6]{0:T(128)} %bitcast.184), channel_id=1, source_target_pairs={{0,64},{32,96},{64,0},{96,32},{1,65},{33,97},{65,1},{97,33},{2,66}... | collective-permute-start | bytes 80 | tf_op jit(solution)/shard_map/ppermute | solution.py:140
  14.7 14.6 %collective-permute-start.4 = (s32[6]{0:T(128)}, s32[6]{0:T(128)S(1)}, u32[]{:S(2)}, u32[]{:S(2)}) collective-permute-start(s32[6]{0:T(128)} %bitcast.185), channel_id=1, source_target_pairs={{0,96},{32,0},{64,32},{96,64},{1,97},{33,1},{65,33},{97,65},{2,98}... | collective-permute-start | bytes 80 | tf_op jit(solution)/shard_map/ppermute | solution.py:140
  18.2 16.5 %collective-permute-start.1 = (bf16[32,1024,16]{1,0,2:T(8,128)(2,1)}, bf16[32,1024,16]{1,0,2:T(8,128)(2,1)}, u32[]{:S(2)}, u32[]{:S(2)}) collective-permute-start(bf16[32,1024,16]{1,0,2:T(8,128)(2,1)} %copy.65), channel_id=1, source_target_pairs={{0,1},{1,0},{2,3},{3,2},{4,5},{5,4},{6,7},{7,6},{8,9},{9,8},{10,11... | collective-permute-start | bytes 3145736 | tf_op jit(solution)/shard_map/ppermute | solution.py:23
  23.0 7.1 %collective-permute-start = (bf16[256,1024]{1,0:T(8,128)(2,1)}, bf16[256,1024]{1,0:T(8,128)(2,1)}, u32[]{:S(2)}, u32[]{:S(2)}) collective-permute-start(bf16[256,1024]{1,0:T(8,128)(2,1)} %fusion.46), channel_id=1, source_target_pairs={{0,1},{1,0},{2,3},{3,2},{4,5},{5,4},{6,7},{7,6},{8,9},{9,8},{10,11... | collective-permute-start | bytes 1572872 | tf_op jit(solution)/shard_map/ppermute | solution.py:23
  31.6 4.8 %copy-start.6 = (bf16[256,1024]{1,0:T(8,128)(2,1)}, bf16[256,1024]{1,0:T(8,128)(2,1)S(1)}, u32[]{:S(2)}) copy-start(bf16[256,1024]{1,0:T(8,128)(2,1)S(1)} %get-tuple-element.33) | copy-start | bytes 1572868
  31.7 4.8 %copy-start.7 = (bf16[256,1024]{1,0:T(8,128)(2,1)}, bf16[256,1024]{1,0:T(8,128)(2,1)S(1)}, u32[]{:S(2)}) copy-start(bf16[256,1024]{1,0:T(8,128)(2,1)S(1)} %get-tuple-element.34) | copy-start | bytes 1572868
  31.7 3.1 %copy-start.4 = (f32[6,1024,16]{1,0,2:T(8,128)S(1)}, f32[6,1024,16]{1,0,2:T(8,128)}, u32[]{:S(2)}) copy-start(f32[6,1024,16]{1,0,2:T(8,128)} %fusion.91) | copy-start | bytes 1179652
  91.8 2.9 %copy-start.13 = (bf16[2,1024,4]{1,2,0:T(4,128)(2,1)S(1)}, bf16[2,1024,4]{1,2,0:T(4,128)(2,1)}, u32[]{:S(2)}) copy-start(bf16[2,1024,4]{1,2,0:T(4,128)(2,1)} %param.18) | copy-start | bytes 49156
  93.5 2.7 %copy-start.11 = (f32[4]{0:T(128)S(1)}, f32[4]{0:T(128)}, u32[]{:S(2)}) copy-start(f32[4]{0:T(128)} %param.19) | copy-start | bytes 52
  93.5 45.1 %collective-permute-start.9 = (bf16[512,1024]{1,0:T(8,128)(2,1)}, bf16[512,1024]{1,0:T(8,128)(2,1)}, u32[]{:S(2)}, u32[]{:S(2)}) collective-permute-start(bf16[512,1024]{1,0:T(8,128)(2,1)} %param.26), channel_id=1, source_target_pairs={{0,1},{1,0},{2,3},{3,2},{4,5},{5,4},{6,7},{7,6},{8,9},{9,8},{10,11... | collective-permute-start | bytes 3145736 | tf_op jit(solution)/shard_map/ppermute | solution.py:23
  100.7 1.0 copy-start.3
  102.5 17.6 %collective-permute-start.5 = (bf16[6,1,128,128]{3,2,0,1:T(8,128)(2,1)}, bf16[6,1,128,128]{3,2,0,1:T(8,128)(2,1)}, u32[]{:S(2)}, u32[]{:S(2)}) collective-permute-start(bf16[6,1,128,128]{3,2,0,1:T(8,128)(2,1)} %get-tuple-element.35), channel_id=1, source_target_pairs={{0,32},{32,64},{64,96},{96,0},{1,33},{33,65},{65,97},{97,1},{2,34}... | collective-permute-start | bytes 589832 | tf_op jit(solution)/shard_map/ppermute | solution.py:140
  103.8 20.7 %collective-permute-start.6 = (bf16[6,1,128,128]{3,2,0,1:T(8,128)(2,1)}, bf16[6,1,128,128]{3,2,0,1:T(8,128)(2,1)}, u32[]{:S(2)}, u32[]{:S(2)}) collective-permute-start(bf16[6,1,128,128]{3,2,0,1:T(8,128)(2,1)} %get-tuple-element.37), channel_id=1, source_target_pairs={{0,64},{32,96},{64,0},{96,32},{1,65},{33,97},{65,1},{97,33},{2,66}... | collective-permute-start | bytes 589832 | tf_op jit(solution)/shard_map/ppermute | solution.py:140
  106.3 18.2 %collective-permute-start.7 = (bf16[6,1,128,128]{3,2,0,1:T(8,128)(2,1)}, bf16[6,1,128,128]{3,2,0,1:T(8,128)(2,1)}, u32[]{:S(2)}, u32[]{:S(2)}) collective-permute-start(bf16[6,1,128,128]{3,2,0,1:T(8,128)(2,1)} %get-tuple-element.36), channel_id=1, source_target_pairs={{0,96},{32,0},{64,32},{96,64},{1,97},{33,1},{65,33},{97,65},{2,98}... | collective-permute-start | bytes 589832 | tf_op jit(solution)/shard_map/ppermute | solution.py:140
  133.9 2.8 %copy-start.8 = (bf16[1,512,512]{1,2,0:T(8,128)(2,1)S(1)}, bf16[1,512,512]{1,2,0:T(8,128)(2,1)}, u32[]{:S(2)}) copy-start(bf16[1,512,512]{1,2,0:T(8,128)(2,1)} %get-tuple-element.32) | copy-start | bytes 1572868
  133.9 2.8 %copy-start.15 = (f32[4,512,512]{1,2,0:T(8,128)S(1)}, f32[4,512,512]{1,2,0:T(8,128)}, u32[]{:S(2)}) copy-start(f32[4,512,512]{1,2,0:T(8,128)} %get-tuple-element.46) | copy-start | bytes 12582916
  136.6 5.7 %slice-start = ((s8[8650752]{0:T(1024)(128)(4,1)}), s8[4194304]{0:T(1024)(128)(4,1)S(1)}, s32[]{:S(2)}) async-start(s8[8650752]{0:T(1024)(128)(4,1)} %bitcast.157), calls=%async_computation.3 | async-start | bytes 8388608
  136.8 1.4 copy-start.5
  136.8 5.6 %slice-start.1 = ((s8[8650752]{0:T(1024)(128)(4,1)}), s8[4194304]{0:T(1024)(128)(4,1)S(1)}, s32[]{:S(2)}) async-start(s8[8650752]{0:T(1024)(128)(4,1)} %bitcast.157), calls=%async_computation.4 | async-start | bytes 8388608
  136.8 5.6 %slice-start.2 = ((s8[8650752]{0:T(1024)(128)(4,1)}), s8[262144]{0:T(1024)(128)(4,1)S(1)}, s32[]{:S(2)}) async-start(s8[8650752]{0:T(1024)(128)(4,1)} %bitcast.157), calls=%async_computation.5 | async-start | bytes 524288
  137.4 1.9 %copy-start.2 = (bf16[256,1024]{1,0:T(8,128)(2,1)S(1)}, bf16[256,1024]{1,0:T(8,128)(2,1)}, u32[]{:S(2)}) copy-start(bf16[256,1024]{1,0:T(8,128)(2,1)} %param.15) | copy-start | bytes 1572868
  137.4 1.9 %collective-permute-start.8 = (bf16[256,512]{0,1:T(8,128)(2,1)S(1)}, bf16[256,512]{0,1:T(8,128)(2,1)S(1)}, u32[]{:S(2)}, u32[]{:S(2)}) collective-permute-start(bf16[256,512]{0,1:T(8,128)(2,1)S(1)} %constant_dynamic-slice_fusion), channel_id=1, source_target_pairs={{0,1},{1,0},{2,3},{3,2},{4,5},{5,4},{6,7},{7,6},{8,9},{9,8},{10,11... | collective-permute-start | bytes 786440 | tf_op jit(solution)/shard_map/ppermute | solution.py:23
  141.6 2.7 %collective-permute-start.10 = (bf16[256,1024]{1,0:T(8,128)(2,1)S(1)}, bf16[256,1024]{1,0:T(8,128)(2,1)S(1)}, u32[]{:S(2)}, u32[]{:S(2)}) collective-permute-start(bf16[256,1024]{1,0:T(8,128)(2,1)S(1)} %fusion.49), channel_id=1, source_target_pairs={{0,1},{1,0},{2,3},{3,2},{4,5},{5,4},{6,7},{7,6},{8,9},{9,8},{10,11... | collective-permute-start | bytes 1572872 | tf_op jit(solution)/shard_map/ppermute | solution.py:23
  147.1 2.7 %collective-permute-start.11 = (f32[256,1024]{1,0:T(8,128)S(1)}, f32[256,1024]{1,0:T(8,128)S(1)}, u32[]{:S(2)}, u32[]{:S(2)}) collective-permute-start(f32[256,1024]{1,0:T(8,128)S(1)} %fusion.12), channel_id=1, source_target_pairs={{0,1},{1,0},{2,3},{3,2},{4,5},{5,4},{6,7},{7,6},{8,9},{9,8},{10,11... | collective-permute-start | bytes 3145736 | tf_op jit(solution)/shard_map/ppermute | solution.py:23
  148.1 2.8 %copy-start.1 = (bf16[3,1024,512]{2,1,0:T(8,128)(2,1)S(1)}, bf16[3,1024,512]{2,1,0:T(8,128)(2,1)}, u32[]{:S(2)}) copy-start(bf16[3,1024,512]{2,1,0:T(8,128)(2,1)} %param.17) | copy-start | bytes 9437188
Sparse Core Ops, SparseCore 0:
  9.5 73.8 all-gather.1
  93.7 40.2 reduce-scatter.1

commit v11 on v9

--- a/solution.py
+++ b/solution.py
@@ -159,11 +159,20 @@
     start_hot = (positions[None, :] == starts[:, None]).astype(jnp.float32)
     start_level = jnp.sum(start_hot[:, :, None] * before[None, :, :], axis=1)
     level = running - jnp.sum(member[:, :, None] * start_level[None, :, :], axis=1)
-    masked_queries = queries[:, None, :, :] * member.astype(jnp.bfloat16)[:, :, None, None]
+    per_core = group_lengths.shape[0] // col_count
+    halves = member.reshape(col_count, tok_rows, col_count, per_core)
+    half_member = jnp.stack([halves[c, :, c] for c in range(col_count)])
+    masked_queries = (
+        queries.reshape(col_count, tok_rows, 1, local_heads, head_size)
+        * half_member.astype(jnp.bfloat16)[:, :, :, None, None]
+    )
     masked_queries, mix_gate = lax.optimization_barrier((masked_queries, mix_gate))
     from_state = jnp.einsum(
-        "tshi,shji->thj", masked_queries, states, preferred_element_type=jnp.float32
-    )
+        "ctshi,cshji->cthj",
+        masked_queries,
+        states.reshape((col_count, per_core) + states.shape[1:]),
+        preferred_element_type=jnp.float32,
+    ).reshape(group, local_heads, head_size)
     carried = from_state * jnp.exp(level)[:, :, None]
 
     scores = jnp.einsum("qhd,khd->hqk", queries, keys, preferred_element_type=jnp.float32) * scale

time: 153 us -> 159 us (1.039)
  waiting for transfers between devices: 67.5 us -> 73.7 us
    reduce_scatter x1, waiting for transfers between devices: 22 us -> 27.7 us  [on_device(): states = lax.psum_scatter(slots, 'z', scatter_dimension=0, tiled=True)[0]]
    dot_general x1, matrix products: 0.58 us -> 3.17 us  [on_device(): jnp.einsum('hqk,khd->qhd', probs, values, preferred_element_type=jnp.floa...]
  transfers between devices with their start and end apart: 11 -> 11, of which waited for: 3 -> 3; matrix products, arithmetic and copies ran while one was open for 30% -> 29% of each run, Pallas kernels for 0% -> 0%
where the time goes in v11:
time: 159 us; the launch traced here: 158 us
  waiting for transfers between devices  73.7 us (46%)
  matrix products  35.4 us (22%)
  between operations  13.9 us (9%)
  local copies, waits for them, and re-layouts  13 us (8%)
  other arithmetic  11.9 us (7%)
  starting transfers between devices  10.5 us (7%)
    all_gather x1, waiting for transfers between devices, on_device(): lax.all_gather(jnp.swapaxes(caches, -1, -2), ('y', 'x'), axis=0, tiled=True)  45.3 us
    reduce_scatter x1, waiting for transfers between devices, on_device(): states = lax.psum_scatter(slots, 'z', scatter_dimension=0, tiled=True)[0]  27.7 us
    ppermute x3, starting transfers between devices, along_z(): lax.ppermute(value, 'z', perm=[(i, (i + d) % z_count) for i in range(z_co...  6.57 us
    unnamed x45, local copies, waits for them, and re-layouts  5.08 us
    gather x1, local copies, waits for them, and re-layouts, on_device(): jnp.take(plane, jnp.clip(local, 0, per_plane - 1).reshape(-1), axis=0)  4.53 us
    dot_general x1, matrix products, on_device(): jnp.einsum('hqk,khd->qhd', memory_w, values, preferred_element_type=jnp.f...  4.1 us
    ppermute x6, starting transfers between devices, swap(): return lax.ppermute(value, 'col', perm=[(0, 1), (1, 0)])  3.83 us
    sub x1, matrix products, on_device(): weights = jnp.exp(masked - peak)  3.6 us
  transfers between devices with their start and end apart: 11, of which 3 were waited for; matrix products, arithmetic and copies ran while one was open for 29% of the time, Pallas kernels for 0%

profile of v11, /device:TPU:1, one launch (start us, length us, event | category | flops | bytes accessed | tf_op | source)
XLA Modules:
  0.0 158.3 jit_solution(8068206905843155992)
XLA Ops:
  6.6 2.2 %copy.53 = bf16[4,4,128,128]{2,3,1,0:T(8,128)(2,1)} copy(bf16[4,4,128,128]{3,2,1,0:T(8,128)(2,1)} %param.23) | data formatting | bytes 1048576 | tf_op args[10]
  8.9 2.5 %collective-permute-start.2 = (s32[6]{0:T(128)}, s32[6]{0:T(128)S(1)}, u32[]{:S(2)}, u32[]{:S(2)}) collective-permute-start(s32[6]{0:T(128)} %bitcast.185), channel_id=1, source_target_pairs={{0,32},{32,64},{64,96},{96,0},{1,33},{33,65},{65,97},{97,1},{2,34}... | collective-permute-start | bytes 80 | tf_op jit(solution)/shard_map/ppermute | solution.py:140
  11.4 3.3 %collective-permute-start.3 = (s32[6]{0:T(128)}, s32[6]{0:T(128)S(1)}, u32[]{:S(2)}, u32[]{:S(2)}) collective-permute-start(s32[6]{0:T(128)} %bitcast.186), channel_id=1, source_target_pairs={{0,64},{32,96},{64,0},{96,32},{1,65},{33,97},{65,1},{97,33},{2,66}... | collective-permute-start | bytes 80 | tf_op jit(solution)/shard_map/ppermute | solution.py:140
  14.7 0.7 collective-permute-start.4
  15.4 2.8 %copy.54 = bf16[32,1024,16]{1,0,2:T(8,128)(2,1)} copy(bf16[32,1024,16]{1,2,0:T(8,128)(2,1)} %param.18) | data formatting | bytes 2097152 | tf_op args[5]
  18.2 1.5 collective-permute-start.1
  19.7 1.2 fusion.42
  21.0 2.0 %fusion.44 = bf16[256,1024]{1,0:T(8,128)(2,1)} fusion(bf16[256,1024]{1,0:T(8,128)(2,1)} %param.13, f32[1024]{0:T(1024)S(1)} %bitcast.175, f32[256]{0:T(256)S(1)} %add_rsqrt_fusion.2), kind=kLoop, calls=%fused_computation.59 | loop fusion | flops 1048576 | bytes 1053696 | tf_op jit(solution)/shard_map/convert_element_type | solution.py:19
  23.0 0.1 reshape.430
  23.1 0.1 reshape_squeeze.8
  23.2 0.2 reduce-window.10
  23.5 2.6 %convolution_convert_fusion = bf16[6,16,512]{2,0,1:T(8,128)(2,1)S(1)} fusion(bf16[64,16,512]{2,1,0:T(8,128)(2,1)} %param.19, s32[6]{0:T(128)S(1)} %bitcast.180), kind=kOutput, calls=%fused_computation.55 | convolution fusion | flops 6340992 | bytes 1146904 | tf_op jit(solution)/shard_map/gq,qjl->gjl/dot_general | solution.py:127
  26.1 3.3 %fusion.87 = f32[6,1024,16]{1,0,2:T(8,128)} fusion(s32[32]{0:T(128)S(1)} %iota_add_fusion.1, s32[6]{0:T(128)S(1)} %bitcast.181, bf16[32,1024,16]{1,2,0:T(8,128)(2,1)} %param.18), kind=kOutput, calls=%fused_computation.132 | convolution fusion | flops 6291648 | bytes 1441944 | tf_op jit(solution)/shard_map/sa,adr->sdr/dot_general | solution.py:117
  29.4 0.6 gather_fusion
  30.0 0.1 compare_and_fusion
  30.0 0.1 min.12
  30.1 1.5 broadcast_select_fusion.1
  31.7 3.1 %fusion.117 = (bf16[3,512,512]{1,2,0:T(8,128)(2,1)}, f32[3,512,512]{1,2,0:T(8,128)S(1)}) fusion(bf16[3,1024,512]{2,1,0:T(8,128)(2,1)S(1)} %copy-done, bf16[256,1024]{1,0:T(8,128)(2,1)S(1)} %get-tuple-element.22, bf16[256,1024]{1,0:T(8,128)(2,1)S(1)} %get-tuple-element.21), kind=kOutput, calls=%fused_computation.185 | convolution fusion | flops 1613496320 | bytes 8912896 | tf_op jit(solution)/shard_map/td,kdc->ktc/dot_general | solution.py:107
  34.8 1.5 fusion.41
  36.4 0.1 copy.56
  36.5 0.5 fusion.65
  37.0 1.1 fusion.39
  38.1 45.3 %all-gather.2.cloned.1.call-done = bf16[64,4,128,128]{3,2,1,0:T(8,128)(2,1)} async-done(((bf16[4,4,128,128]{3,2,1,0:T(8,128)(2,1)}), bf16[64,4,128,128]{3,2,1,0:T(8,128)(2,1)}) %all-gather.2.cloned.1.call-update) | async-done | bytes 8388624 | tf_op jit(solution)/shard_map/all_gather | solution.py:95
  83.4 4.5 %gather_fusion.1 = bf16[24,4,128,128]{3,2,1,0:T(8,128)(2,1)S(1)} fusion(bf16[64,4,128,128]{3,2,1,0:T(8,128)(2,1)} %all-gather.2.cloned.1.call-done, s32[1024]{0:T(1024)S(1)} %pad_clamp_fusion), kind=kCustom, calls=%fused_computation.1 | custom fusion | bytes 6291552 | tf_op jit(solution)/shard_map/jit(_take)/gather | solution.py:146
  88.0 2.0 %select_multiply_fusion = bf16[4,6,4,128,128]{4,3,2,1,0:T(8,128)(2,1)} fusion(bf16[4,6,4,128,128]{4,3,2,1,0:T(8,128)(2,1)S(1)} %bitcast.160, pred[4,6]{1,0:T(4,128)(4,1)S(1)} %get-tuple-element.17, bf16[4,6]{1,0:T(4,128)(2,1)S(1)} %get-tuple-element.27), kind=kLoop, calls=%fused_computation.15 | loop fusion | flops 3145728 | bytes 6291528 | tf_op jit(solution)/shard_map/mul | solution.py:148
  90.1 0.9 collective-permute-start.6
  91.0 0.6 broadcast.411
  91.6 0.7 reduce.5
  92.3 0.1 reshape.432
  92.4 0.1 convert_convert_fusion
  92.5 0.1 convert_reduce_fusion
  92.7 0.2 fusion.52
  92.9 0.4 convolution_bitcast_fusion.3
  93.3 0.1 fusion.112
  93.4 1.2 reduce-window.11
  94.6 0.2 slice_reduce_fusion
  94.8 0.2 reduce-window.14
  95.0 0.1 bitcast_subtract_fusion.1
  95.1 0.1 multiply_reduce_fusion.3
  95.2 0.1 multiply_reduce_fusion.2
  95.4 0.9 fusion.115
  96.2 0.1 mul.205
  96.4 0.5 copy.62
  96.8 0.3 broadcast_multiply_fusion
  97.1 3.6 %fusion.118 = (f32[4,512]{1,0:T(4,128)S(1)}, f32[4,512,512]{1,2,0:T(8,128)}) fusion(pred[512,512]{0,1:T(8,128)(4,1)S(1)} %fusion.52, bf16[512,4,128]{0,2,1:T(8,128)(2,1)S(1)} %bitcast.162, bf16[512,4,128]{0,2,1:T(8,128)(2,1)S(1)} %bitcast.171), kind=kOutput, calls=%fused_computation.186 | convolution fusion | flops 272630272 | bytes 5513216 | tf_op jit(solution)/shard_map/sub | solution.py:182
  100.7 27.7 %reduce-scatter.2.cloned.1.call-done = bf16[1,6,4,128,128]{4,3,2,1,0:T(8,128)(2,1)} async-done(((bf16[4,6,4,128,128]{4,3,2,1,0:T(8,128)(2,1)}), bf16[1,6,4,128,128]{4,3,2,1,0:T(8,128)(2,1)}) %reduce-scatter.2.cloned.1.call-update) | async-done | bytes 786448 | tf_op jit(solution)/shard_map/reduce_scatter | solution.py:149
  128.5 1.8 %convolution_bitcast_fusion.1 = f32[2,4,16,8,256]{4,3,2,1,0:T(8,128)S(1)} fusion(bf16[2,256,3,4,128]{4,1,2,3,0:T(8,128)(2,1)S(1)} %broadcast_multiply_fusion, bf16[2,3,4,128,128]{4,3,2,1,0:T(8,128)(2,1)} %bitcast.166), kind=kOutput, calls=%fused_computation.43 | convolution fusion | flops 201326592 | bytes 3407872 | tf_op jit(solution)/shard_map/ctshi,cshji->cthj/dot_general | solution.py:170
  130.2 0.1 copy.72
  130.4 4.1 %multiply_reduce_fusion = (f32[512,4]{0,1:T(4,128)S(1)}, f32[512,4,128]{0,2,1:T(8,128)}) fusion(f32[512,4,128]{0,2,1:T(8,128)S(1)} %bitcast.165, f32[512,4]{0,1:T(4,128)S(1)} %fusion.82, bf16[512,4,128]{0,2,1:T(8,128)(2,1)} %bitcast.169, f32[4,512]{1,0:T(4,128)S(1)} %bitcast.179, pred[512,512]{0,1:T(8,128)(4,1)S(1)} %fusion.52, ...), kind=kOutput, calls=%fused_computation.70 | convolution fusion | flops 543160320 | bytes 3956736 | tf_op jit(solution)/shard_map/hqk,khd->qhd/dot_general | solution.py:187
  134.5 3.2 %fusion.38 = bf16[512,4,128]{0,2,1:T(8,128)(2,1)S(1)} fusion(bf16[512,4,128]{0,2,1:T(8,128)(2,1)S(1)} %bitcast.170, f32[4,512,512]{1,2,0:T(8,128)} %get-tuple-element.33, f32[4,512]{1,0:T(4,128)S(1)} %get-tuple-element.32, f32[512,4,128]{0,2,1:T(8,128)} %get-tuple-element.35, f32[512,4]{0,1:T(4,128)S(1)} %add_rsqrt_fusion, f32[512,4]{0,1:T(4,128)S(1)} %fusion.81), kind=kOutput, calls=%fused_computation.50 | convolution fusion | flops 271581184 | bytes 6316032 | tf_op jit(solution)/shard_map/hqk,khd->qhd/dot_general | solution.py:184
  137.8 0.7 collective-permute-start.5
  138.4 1.9 %fusion.66 = f32[256,1024]{1,0:T(8,128)S(1)} fusion(bf16[512,1024]{1,0:T(8,128)(2,1)} %param.24, bf16[512,512]{0,1:T(8,128)(2,1)S(1)} %bitcast.168, s32[]{:T(128)S(6)} %select_n.121), kind=kOutput, calls=%fused_computation.89 | convolution fusion | flops 268435456 | bytes 2359300 | tf_op jit(solution)/shard_map/dot_general | solution.py:195
  140.4 1.8 %fusion.45 = (f32[256]{0:T(256)S(1)}, bf16[256,1024]{1,0:T(8,128)(2,1)S(1)}) fusion(f32[256,1024]{1,0:T(8,128)S(1)} %fusion.66, bf16[256,512]{0,1:T(8,128)(2,1)S(1)} %collective-permute-done.5, bf16[512,1024]{1,0:T(8,128)(2,1)} %collective-permute-done.6, bf16[256,1024]{1,0:T(8,128)(2,1)S(1)} %copy-done.2), kind=kOutput, calls=%fused_computation.60 | convolution fusion | flops 270270208 | bytes 3408896 | tf_op jit(solution)/shard_map/dot_general | solution.py:195
  142.2 0.2 fusion.47
  142.4 0.6 collective-permute-start.7
  143.0 0.9 fusion.17
  143.9 1.1 fusion.15
  145.0 1.7 %fusion.7 = f32[2,256,1408]{2,1,0:T(8,128)S(1)} fusion(bf16[3,1024,1408]{2,1,0:T(8,128)(2,1)S(1)} %bitcast.159, bf16[256,1024]{1,0:T(8,128)(2,1)S(1)} %collective-permute-done.7), kind=kOutput, calls=%fused_computation.13 | convolution fusion | flops 1476395008 | bytes 9175040 | tf_op jit(solution)/shard_map/td,kdf->ktf/dot_general | solution.py:202
  146.7 1.0 fusion.11
  147.7 0.1 collective-permute-start.8
  147.8 0.9 fusion.20
  148.8 1.1 fusion.13
  149.8 0.6 collective-permute-done.8
  150.5 1.1 fusion.48
  (82 shorter events, 0.7 us)
Async XLA Ops:
  6.5 25.2 %copy-start = (bf16[3,1024,512]{2,1,0:T(8,128)(2,1)S(1)}, bf16[3,1024,512]{2,1,0:T(8,128)(2,1)}, u32[]{:S(2)}) copy-start(bf16[3,1024,512]{2,1,0:T(8,128)(2,1)} %param.15) | copy-start | bytes 9437188
  6.5 14.4 %copy-start.12 = (f32[2,1024]{1,0:T(2,128)S(1)}, f32[2,1024]{1,0:T(2,128)}, u32[]{:S(2)}) copy-start(f32[2,1024]{1,0:T(2,128)} %param.14) | copy-start | bytes 24580
  6.5 16.5 %copy-start.15 = (s32[1,2,3]{2,1,0:T(2,128)S(1)}, s32[1,2,3]{2,1,0:T(2,128)}, u32[]{:S(2)}) copy-start(s32[1,2,3]{2,1,0:T(2,128)} %param.20) | copy-start | bytes 76
  6.5 17.0 %copy-start.13 = (s32[1,6]{1,0:T(1,128)S(1)}, s32[1,6]{1,0:T(1,128)}, u32[]{:S(2)}) copy-start(s32[1,6]{1,0:T(1,128)} %param.21) | copy-start | bytes 76
  6.5 76.9 %all-gather.2.cloned.1.call-start = ((), (), s32[]{:S(2)}) async-start(), calls=%async_computation.1 | async-start | bytes 8912896 | tf_op jit(solution)/shard_map/all_gather | solution.py:95
  8.8 119.7 %reduce-scatter.2.cloned.1.call-start = ((), (), s32[]{:S(2)}) async-start(), calls=%async_computation.2 | async-start | bytes 3932160 | tf_op jit(solution)/shard_map/reduce_scatter | solution.py:149
  8.8 20.5 %copy-start.16 = (s32[1,6]{1,0:T(1,128)S(1)}, s32[1,6]{1,0:T(1,128)}, u32[]{:S(2)}) copy-start(s32[1,6]{1,0:T(1,128)} %param.22) | copy-start | bytes 76
  8.9 20.5 %collective-permute-start.2 = (s32[6]{0:T(128)}, s32[6]{0:T(128)S(1)}, u32[]{:S(2)}, u32[]{:S(2)}) collective-permute-start(s32[6]{0:T(128)} %bitcast.185), channel_id=1, source_target_pairs={{0,32},{32,64},{64,96},{96,0},{1,33},{33,65},{65,97},{97,1},{2,34}... | collective-permute-start | bytes 80 | tf_op jit(solution)/shard_map/ppermute | solution.py:140
  11.4 18.0 %collective-permute-start.3 = (s32[6]{0:T(128)}, s32[6]{0:T(128)S(1)}, u32[]{:S(2)}, u32[]{:S(2)}) collective-permute-start(s32[6]{0:T(128)} %bitcast.186), channel_id=1, source_target_pairs={{0,64},{32,96},{64,0},{96,32},{1,65},{33,97},{65,1},{97,33},{2,66}... | collective-permute-start | bytes 80 | tf_op jit(solution)/shard_map/ppermute | solution.py:140
  14.7 14.7 %collective-permute-start.4 = (s32[6]{0:T(128)}, s32[6]{0:T(128)S(1)}, u32[]{:S(2)}, u32[]{:S(2)}) collective-permute-start(s32[6]{0:T(128)} %bitcast.187), channel_id=1, source_target_pairs={{0,96},{32,0},{64,32},{96,64},{1,97},{33,1},{65,33},{97,65},{2,98}... | collective-permute-start | bytes 80 | tf_op jit(solution)/shard_map/ppermute | solution.py:140
  18.2 16.6 %collective-permute-start.1 = (bf16[32,1024,16]{1,0,2:T(8,128)(2,1)}, bf16[32,1024,16]{1,0,2:T(8,128)(2,1)}, u32[]{:S(2)}, u32[]{:S(2)}) collective-permute-start(bf16[32,1024,16]{1,0,2:T(8,128)(2,1)} %copy.54), channel_id=1, source_target_pairs={{0,1},{1,0},{2,3},{3,2},{4,5},{5,4},{6,7},{7,6},{8,9},{9,8},{10,11... | collective-permute-start | bytes 3145736 | tf_op jit(solution)/shard_map/ppermute | solution.py:23
  23.0 7.1 %collective-permute-start = (bf16[256,1024]{1,0:T(8,128)(2,1)}, bf16[256,1024]{1,0:T(8,128)(2,1)}, u32[]{:S(2)}, u32[]{:S(2)}) collective-permute-start(bf16[256,1024]{1,0:T(8,128)(2,1)} %fusion.44), channel_id=1, source_target_pairs={{0,1},{1,0},{2,3},{3,2},{4,5},{5,4},{6,7},{7,6},{8,9},{9,8},{10,11... | collective-permute-start | bytes 1572872 | tf_op jit(solution)/shard_map/ppermute | solution.py:23
  31.7 4.8 %copy-start.6 = (bf16[256,1024]{1,0:T(8,128)(2,1)}, bf16[256,1024]{1,0:T(8,128)(2,1)S(1)}, u32[]{:S(2)}) copy-start(bf16[256,1024]{1,0:T(8,128)(2,1)S(1)} %get-tuple-element.21) | copy-start | bytes 1572868
  31.7 4.8 %copy-start.8 = (bf16[256,1024]{1,0:T(8,128)(2,1)}, bf16[256,1024]{1,0:T(8,128)(2,1)S(1)}, u32[]{:S(2)}) copy-start(bf16[256,1024]{1,0:T(8,128)(2,1)S(1)} %get-tuple-element.22) | copy-start | bytes 1572868
  31.7 3.1 %copy-start.4 = (f32[6,1024,16]{1,0,2:T(8,128)S(1)}, f32[6,1024,16]{1,0,2:T(8,128)}, u32[]{:S(2)}) copy-start(f32[6,1024,16]{1,0,2:T(8,128)} %fusion.87) | copy-start | bytes 1179652
  90.0 2.9 %copy-start.7 = (bf16[256,1024]{1,0:T(8,128)(2,1)S(1)}, bf16[256,1024]{1,0:T(8,128)(2,1)}, u32[]{:S(2)}) copy-start(bf16[256,1024]{1,0:T(8,128)(2,1)} %copy-done.6) | copy-start | bytes 1572868
  90.0 2.9 %copy-start.9 = (bf16[256,1024]{1,0:T(8,128)(2,1)S(1)}, bf16[256,1024]{1,0:T(8,128)(2,1)}, u32[]{:S(2)}) copy-start(bf16[256,1024]{1,0:T(8,128)(2,1)} %copy-done.8) | copy-start | bytes 1572868
  90.0 2.9 %copy-start.17 = (bf16[2,1024,4]{1,2,0:T(4,128)(2,1)S(1)}, bf16[2,1024,4]{1,2,0:T(4,128)(2,1)}, u32[]{:S(2)}) copy-start(bf16[2,1024,4]{1,2,0:T(4,128)(2,1)} %param.16) | copy-start | bytes 49156
  90.0 3.3 %copy-start.14 = (f32[4]{0:T(128)S(1)}, f32[4]{0:T(128)}, u32[]{:S(2)}) copy-start(f32[4]{0:T(128)} %param.17) | copy-start | bytes 52
  90.0 5.3 %copy-start.5 = (bf16[3,512,512]{1,2,0:T(8,128)(2,1)S(1)}, bf16[3,512,512]{1,2,0:T(8,128)(2,1)}, u32[]{:S(2)}) copy-start(bf16[3,512,512]{1,2,0:T(8,128)(2,1)} %get-tuple-element.30) | copy-start | bytes 4718596
  90.0 6.2 %copy-start.3 = (bf16[512,512]{0,1:T(8,128)(2,1)S(1)}, bf16[512,512]{0,1:T(8,128)(2,1)}, u32[]{:S(2)}) copy-start(bf16[512,512]{0,1:T(8,128)(2,1)} %fusion.39) | copy-start | bytes 1572868
  90.1 50.3 %collective-permute-start.6 = (bf16[512,1024]{1,0:T(8,128)(2,1)}, bf16[512,1024]{1,0:T(8,128)(2,1)}, u32[]{:S(2)}, u32[]{:S(2)}) collective-permute-start(bf16[512,1024]{1,0:T(8,128)(2,1)} %param.24), channel_id=1, source_target_pairs={{0,1},{1,0},{2,3},{3,2},{4,5},{5,4},{6,7},{7,6},{8,9},{9,8},{10,11... | collective-permute-start | bytes 3145736 | tf_op jit(solution)/shard_map/ppermute | solution.py:23
  96.2 4.5 %copy-start.11 = (bf16[1,512,512]{1,2,0:T(8,128)(2,1)}, bf16[1,512,512]{1,2,0:T(8,128)(2,1)S(1)}, u32[]{:S(2)}) copy-start(bf16[1,512,512]{1,2,0:T(8,128)(2,1)S(1)} %get-tuple-element.19) | copy-start | bytes 1572868
  130.4 4.1 %copy-start.10 = (bf16[1,512,512]{1,2,0:T(8,128)(2,1)S(1)}, bf16[1,512,512]{1,2,0:T(8,128)(2,1)}, u32[]{:S(2)}) copy-start(bf16[1,512,512]{1,2,0:T(8,128)(2,1)} %get-tuple-element.20) | copy-start | bytes 1572868
  134.5 8.5 %slice-start = ((s8[8650752]{0:T(1024)(128)(4,1)}), s8[4194304]{0:T(1024)(128)(4,1)S(1)}, s32[]{:S(2)}) async-start(s8[8650752]{0:T(1024)(128)(4,1)} %bitcast.158), calls=%async_computation.3 | async-start | bytes 8388608
  134.5 8.5 %slice-start.1 = ((s8[8650752]{0:T(1024)(128)(4,1)}), s8[4194304]{0:T(1024)(128)(4,1)S(1)}, s32[]{:S(2)}) async-start(s8[8650752]{0:T(1024)(128)(4,1)} %bitcast.158), calls=%async_computation.4 | async-start | bytes 8388608
  134.5 8.5 %slice-start.2 = ((s8[8650752]{0:T(1024)(128)(4,1)}), s8[262144]{0:T(1024)(128)(4,1)S(1)}, s32[]{:S(2)}) async-start(s8[8650752]{0:T(1024)(128)(4,1)} %bitcast.158), calls=%async_computation.5 | async-start | bytes 524288
  137.7 2.7 %copy-start.2 = (bf16[256,1024]{1,0:T(8,128)(2,1)S(1)}, bf16[256,1024]{1,0:T(8,128)(2,1)}, u32[]{:S(2)}) copy-start(bf16[256,1024]{1,0:T(8,128)(2,1)} %param.13) | copy-start | bytes 1572868
  137.8 2.6 %collective-permute-start.5 = (bf16[256,512]{0,1:T(8,128)(2,1)S(1)}, bf16[256,512]{0,1:T(8,128)(2,1)S(1)}, u32[]{:S(2)}, u32[]{:S(2)}) collective-permute-start(bf16[256,512]{0,1:T(8,128)(2,1)S(1)} %constant_dynamic-slice_fusion), channel_id=1, source_target_pairs={{0,1},{1,0},{2,3},{3,2},{4,5},{5,4},{6,7},{7,6},{8,9},{9,8},{10,11... | collective-permute-start | bytes 786440 | tf_op jit(solution)/shard_map/ppermute | solution.py:23
  142.4 2.6 %collective-permute-start.7 = (bf16[256,1024]{1,0:T(8,128)(2,1)S(1)}, bf16[256,1024]{1,0:T(8,128)(2,1)S(1)}, u32[]{:S(2)}, u32[]{:S(2)}) collective-permute-start(bf16[256,1024]{1,0:T(8,128)(2,1)S(1)} %fusion.47), channel_id=1, source_target_pairs={{0,1},{1,0},{2,3},{3,2},{4,5},{5,4},{6,7},{7,6},{8,9},{9,8},{10,11... | collective-permute-start | bytes 1572872 | tf_op jit(solution)/shard_map/ppermute | solution.py:23
  147.7 2.7 %collective-permute-start.8 = (f32[256,1024]{1,0:T(8,128)S(1)}, f32[256,1024]{1,0:T(8,128)S(1)}, u32[]{:S(2)}, u32[]{:S(2)}) collective-permute-start(f32[256,1024]{1,0:T(8,128)S(1)} %fusion.11), channel_id=1, source_target_pairs={{0,1},{1,0},{2,3},{3,2},{4,5},{5,4},{6,7},{7,6},{8,9},{9,8},{10,11... | collective-permute-start | bytes 3145736 | tf_op jit(solution)/shard_map/ppermute | solution.py:23
  148.8 2.7 %copy-start.1 = (bf16[3,1024,512]{2,1,0:T(8,128)(2,1)S(1)}, bf16[3,1024,512]{2,1,0:T(8,128)(2,1)}, u32[]{:S(2)}) copy-start(bf16[3,1024,512]{2,1,0:T(8,128)(2,1)} %param.15) | copy-start | bytes 9437188
Sparse Core Ops, SparseCore 0:
  9.5 73.8 all-gather.1
  90.2 38.2 reduce-scatter.1
